TPU v7x, 768 devices: a whole 4x8x12 slice. The times are simulated.
768 devices in a mesh: chan: 32 (over z_lo, y), row: 8 (over x, core), col: 3 (over z_hi).
Axes of the slice: x: 4, y: 8, z: 12 (z_hi: 3, z_lo: 4; z = z_hi * 4 + z_lo), core: 2. Of those that a mesh axis runs over, the one named last changes fastest.
Arguments:
- voltages: bfloat16 [24, 64, 2, 16, 128], P(('row', 'col'), 'chan'), may hold values from -270 to 270
- source_flux: float32 [128, 64], P('chan'), may hold values from 0.1 to 10
- initial_gains: float32 [128, 2, 24, 64], P('chan', None, ('row', 'col')), may hold values from -4 to 4
- antenna_positions: float32 [2, 24, 64], replicated, may hold values from -1 to 1
- flagged: int32 [24, 64], replicated, may hold values 0 or 1
- source_pixels: int32 [64, 2], replicated, may hold values from 0 to 255
Outputs:
- gains: float32 [128, 2, 24, 64], P('chan', None, ('row', 'col'))
Inputs may be any that keep to these rules, and one draw needn't show every extreme that they name: flagged holds 0 or 1 for each antenna, the same for all channels.
All inputs are finite; a program needn't handle non-finite values.
Results may differ from a plain program's by a relative error of at most 0.012.
Values may be sent and summed in bfloat16 or wider, within the bound.
No kernel may reach another device: no remote copies, remote signals or barrier semaphores. Data moves between devices by JAX's collectives and lax.ppermute only.
A program may use at most 32 MiB of HBM per device.

v0:
```python
import math

import jax
import jax.numpy as jnp
from jax import lax
from jax.sharding import PartitionSpec as P

PIX = 256
ITERS = 3


phase_scale = 2.0 * math.pi * 8.0
small_eps = 1e-06


def steering(positions, ell_coord, emm_coord, frequencies):
    angle = (
        phase_scale
        * frequencies[:, None, None]
        * (
            positions[0][None, :, None] * ell_coord[None, None, :]
            + positions[1][None, :, None] * emm_coord[None, None, :]
        )
    )
    return (jnp.cos(angle).astype(jnp.bfloat16), (-jnp.sin(angle)).astype(jnp.bfloat16))


def antenna_major(block):
    count, subant, halves, samples, chans = block.shape
    return jnp.transpose(block, (4, 0, 1, 2, 3)).reshape(chans, count * subant, halves, samples)


def share(own_gains):
    gathered = lax.all_gather(own_gains[:, :, None, :], "col", axis=2, tiled=True)
    return gathered.reshape(gathered.shape[0], 2, gathered.shape[2] * gathered.shape[3])


def on_device(voltages, source_flux, initial_gains, antenna_positions, flagged, source_pixels):
    n_rows = lax.axis_size("row")
    n_cols = lax.axis_size("col")
    n_chans = lax.axis_size("chan")
    row_index = lax.axis_index("row")
    col_index = lax.axis_index("col")
    chan_index = lax.axis_index("chan")
    subant = antenna_positions.shape[2]
    per_chan = source_flux.shape[0]
    samples = voltages.shape[3]
    row_pieces = lax.all_gather(voltages, "col", axis=0, tiled=True)
    col_pieces = lax.all_gather(voltages, "row", axis=0, tiled=True)
    row_volt, col_volt = (
        lax.all_to_all(row_pieces, "chan", split_axis=4, concat_axis=1, tiled=True),
        lax.all_to_all(col_pieces, "chan", split_axis=4, concat_axis=1, tiled=True),
    )
    row_antenna = antenna_major(row_volt)
    col_antenna = antenna_major(col_volt)
    row_count = row_antenna.shape[1]
    col_count = col_antenna.shape[1]
    row_left = row_antenna.reshape(per_chan, row_count, 2 * samples)
    row_swap = jnp.concatenate([row_antenna[:, :, 1], -row_antenna[:, :, 0]], axis=2)
    col_left = col_antenna.reshape(per_chan, col_count, 2 * samples)
    vis_re = (
        jnp.einsum("cqk,cpk->cqp", row_left, col_left, preferred_element_type=jnp.float32) / samples
    )
    vis_im = (
        jnp.einsum("cqk,cpk->cqp", row_swap, col_left, preferred_element_type=jnp.float32) / samples
    )
    row_pos = lax.dynamic_slice_in_dim(antenna_positions, row_index * n_cols, n_cols, 1).reshape(
        2, row_count
    )
    col_pos = lax.dynamic_index_in_dim(
        antenna_positions.reshape(2, n_rows, n_cols, subant), col_index, 2, keepdims=False
    ).reshape(2, col_count)
    row_flag = lax.dynamic_slice_in_dim(flagged, row_index * n_cols, n_cols, 0).reshape(row_count)
    own_flag = lax.dynamic_index_in_dim(flagged, row_index * n_cols + col_index, 0, keepdims=False)
    row_ids = row_index * n_cols * subant + jnp.arange(row_count, dtype=jnp.int32)
    col_ids = (
        (jnp.arange(n_rows, dtype=jnp.int32) * n_cols + col_index)[:, None] * subant
        + jnp.arange(subant, dtype=jnp.int32)[None, :]
    ).reshape(col_count)
    pixel_float = source_pixels.astype(jnp.float32)
    ell_coord = (pixel_float[:, 0] - 0.5 * PIX) / PIX
    emm_coord = (pixel_float[:, 1] - 0.5 * PIX) / PIX
    channel_ids = chan_index * per_chan + jnp.arange(per_chan, dtype=jnp.int32)
    frequencies = 1.0 + channel_ids.astype(jnp.float32) / (per_chan * n_chans)
    steer_re, steer_im = steering(row_pos, ell_coord, emm_coord, frequencies)
    far_re, far_im = steering(col_pos, ell_coord, emm_coord, frequencies)
    weight_re = (source_flux[:, None, :] * far_re).astype(jnp.bfloat16)
    weight_im = (source_flux[:, None, :] * far_im).astype(jnp.bfloat16)
    steer_both = jnp.concatenate([steer_re, steer_im], axis=2)
    steer_swap = jnp.concatenate([steer_im, -steer_re], axis=2)
    weight_both = jnp.concatenate([weight_re, weight_im], axis=2)
    model_re = jnp.einsum(
        "cqk,cpk->cqp", steer_both, weight_both, preferred_element_type=jnp.float32
    )
    model_im = jnp.einsum(
        "cqk,cpk->cqp", steer_swap, weight_both, preferred_element_type=jnp.float32
    )
    live = (1 - row_flag).astype(jnp.float32)
    apart = (row_ids[:, None] != col_ids[None, :]).astype(jnp.float32)
    keep = (live[:, None] * apart)[None, :, :]
    data_re = keep * (model_re * vis_re + model_im * vis_im)
    data_im = keep * (model_re * vis_im - model_im * vis_re)
    power = keep * (model_re * model_re + model_im * model_im)
    highest = lax.Precision.HIGHEST
    current = initial_gains[:, :, 0, :]
    own_count = current.shape[2]
    for iteration in range(ITERS):
        row_gains = share(current)
        gain_re = row_gains[:, 0]
        gain_im = row_gains[:, 1]
        num_re = jnp.einsum("cq,cqp->cp", gain_re, data_re, precision=highest) + jnp.einsum(
            "cq,cqp->cp", gain_im, data_im, precision=highest
        )
        num_im = jnp.einsum("cq,cqp->cp", gain_re, data_im, precision=highest) - jnp.einsum(
            "cq,cqp->cp", gain_im, data_re, precision=highest
        )
        denominator = jnp.einsum(
            "cq,cqp->cp", gain_re * gain_re + gain_im * gain_im, power, precision=highest
        )
        total_re, total_im, total_den = lax.psum((num_re, num_im, denominator), "row")
        total_re = lax.dynamic_slice_in_dim(total_re, row_index * own_count, own_count, 1)
        total_im = lax.dynamic_slice_in_dim(total_im, row_index * own_count, own_count, 1)
        total_den = lax.dynamic_slice_in_dim(total_den, row_index * own_count, own_count, 1)
        fresh = jnp.stack(
            [total_re / (total_den + small_eps), -total_im / (total_den + small_eps)], axis=1
        )
        current = jnp.where(own_flag[None, None, :] == 1, current, 0.5 * (current + fresh))
    return current[:, :, None, :]


def solution(mesh):
    in_specs = (
        P(("row", "col"), "chan", None, None, None),
        P("chan", None),
        P("chan", None, ("row", "col"), None),
        P(),
        P(),
        P(),
    )
    out_specs = P("chan", None, ("row", "col"), None)
    return jax.shard_map(
        on_device, mesh=mesh, in_specs=in_specs, out_specs=out_specs, check_vma=False
    )
```

profile of v0, /device:TPU:1, one launch (start us, length us, event | category | flops | bytes accessed | tf_op | source)
XLA Modules:
  0.0 211.6 jit_solution(17591464646651303989)
XLA Ops:
  0.0 21.7 %all_gather.15 = bf16[3,2,2,16,128]{4,3,2,1,0:T(8,128)(2,1)S(1)} all-gather(bf16[1,2,2,16,128]{4,3,2,1,0:T(8,128)(2,1)} %param.6), channel_id=1, replica_groups=mesh['chan'=32,'row'=8,'col'=3] {'col'}, dimensions={0}, use_global_device_ids=true | all-gather | bytes 65536 | tf_op jit(solution)/shard_map/all_gather | solution.py:48
  21.7 0.4 copy.133
  22.1 1.1 reshape.352
  23.2 10.1 %all-to-all-start = ((bf16[32,2,384]{2,1,0:T(2,128)(2,1)}), bf16[32,2,384]{2,1,0:T(2,128)(2,1)S(1)}, u32[]{:S(2)}, u32[]{:S(2)}) async-start(bf16[32,2,384]{2,1,0:T(2,128)(2,1)} %reshape.352), calls=%async_computation | async-start | bytes 98304 | tf_op jit(solution)/shard_map/all_to_all | solution.py:51
  33.4 15.9 %all_gather.16 = bf16[8,2,2,16,128]{4,3,2,1,0:T(8,128)(2,1)S(1)} all-gather(bf16[1,2,2,16,128]{4,3,2,1,0:T(8,128)(2,1)} %param.6), channel_id=1, replica_groups=mesh['chan'=32,'row'=8,'col'=3] {'row'}, dimensions={0}, use_global_device_ids=true | all-gather | bytes 147456 | tf_op jit(solution)/shard_map/all_gather | solution.py:49
  49.3 0.7 convert_element_type.48
  50.0 0.8 copy.131
  50.8 0.7 constant_dynamic-slice_fusion
  51.8 1.6 fusion.3
  53.4 2.0 fusion.89
  55.5 1.4 copy.137
  56.9 1.8 reshape.350
  58.9 0.7 fusion.61
  59.8 10.8 %all_gather.17 = f32[4,2,3,64]{3,0,1,2:T(4,128)S(1)} all-gather(f32[4,2,1,64]{3,0,1,2:T(4,128)S(1)} %copy.145), channel_id=1, replica_groups=mesh['chan'=32,'row'=8,'col'=3] {'col'}, dimensions={2}, use_global_device_ids=true | all-gather | bytes 8192 | tf_op jit(solution)/shard_map/all_gather | solution.py:34
  70.8 0.7 compare_bitcast_fusion
  71.6 2.2 %multiply_convert_fusion.1 = (bf16[4,512,64]{1,2,0:T(8,128)(2,1)S(1)}, bf16[4,512,64]{1,2,0:T(8,128)(2,1)S(1)}) fusion(f32[512,64]{0,1:T(8,128)S(1)} %multiply_add_fusion, f32[4]{0:T(128)S(1)} %add_multiply_fusion.2, f32[4,64]{1,0:T(4,128)S(1)} %copy-done.11), kind=kLoop, calls=%fused_computation.14 | loop fusion | flops 1310720 | bytes 656400 | tf_op jit(solution)/shard_map/convert_element_type | solution.py:87
  73.8 0.9 compare_select_fusion
  74.7 1.6 fusion.7
  76.3 10.0 %all-to-all-start.1 = ((bf16[32,2,1024]{2,1,0:T(2,128)(2,1)}), bf16[32,2,1024]{2,1,0:T(2,128)(2,1)S(1)}, u32[]{:S(2)}, u32[]{:S(2)}) async-start(bf16[32,2,1024]{2,1,0:T(2,128)(2,1)} %reshape.350), calls=%async_computation.1 | async-start | bytes 262144 | tf_op jit(solution)/shard_map/all_to_all | solution.py:52
  86.4 0.5 reshape.353
  87.9 7.8 %all-to-all-done.1 = bf16[32,2,1024]{2,1,0:T(2,128)(2,1)S(1)} async-done(((bf16[32,2,1024]{2,1,0:T(2,128)(2,1)}), bf16[32,2,1024]{2,1,0:T(2,128)(2,1)S(1)}, u32[]{:S(2)}, u32[]{:S(2)}) %all-to-all-start.1) | async-done | bytes 131104 | tf_op jit(solution)/shard_map/all_to_all | solution.py:52
  95.7 0.7 reshape.351
  96.6 1.3 copy.140
  98.2 0.4 convolution_multiply_fusion.1
  98.6 0.4 convolution_multiply_fusion
  99.0 0.5 copy-done.3
  99.8 0.9 subtract_multiply_fusion
  100.7 0.9 fusion.38
  101.6 0.9 fusion.40
  102.5 0.9 fusion.56
  103.4 0.9 fusion.58
  104.4 0.9 fusion.46
  105.2 23.6 %all-reduce.2 = (f32[4,512]{1,0:T(4,128)S(1)}, f32[4,512]{1,0:T(4,128)S(1)}, f32[4,512]{1,0:T(4,128)S(1)}) all-reduce(f32[4,512]{1,0:T(4,128)S(1)} %get-tuple-element.39, f32[4,512]{1,0:T(4,128)S(1)} %bitcast.207, f32[4,512]{1,0:T(4,128)S(1)} %get-tuple-element.40), channel_id=1, replica_groups=mesh['chan'=32,'row'=8,'col'=3] {'row'}, use_global_device_ids=true, to_apply=%region_2.3 | all-reduce | flops 6144 | bytes 49152 | tf_op jit(solution)/shard_map/psum | solution.py:120
  128.9 11.0 %all_gather.18 = f32[4,2,3,64]{3,0,2,1:T(4,128)S(1)} all-gather(f32[4,2,1,64]{3,0,2,1:T(4,128)S(1)} %fusion.20), channel_id=1, replica_groups=mesh['chan'=32,'row'=8,'col'=3] {'col'}, dimensions={2}, use_global_device_ids=true | all-gather | bytes 8192 | tf_op jit(solution)/shard_map/all_gather | solution.py:34
  140.0 0.8 fusion.34
  140.8 0.9 fusion.36
  141.7 0.9 fusion.52
  142.5 0.9 fusion.54
  143.4 0.9 fusion.44
  144.3 25.7 %all-reduce.1 = (f32[4,512]{1,0:T(4,128)S(1)}, f32[4,512]{1,0:T(4,128)S(1)}, f32[4,512]{1,0:T(4,128)S(1)}) all-reduce(f32[4,512]{1,0:T(4,128)S(1)} %bitcast_subtract_fusion.1, f32[4,512]{1,0:T(4,128)S(1)} %bitcast.208, f32[4,512]{1,0:T(4,128)S(1)} %bitcast_add_fusion.1), channel_id=1, replica_groups=mesh['chan'=32,'row'=8,'col'=3] {'row'}, use_global_device_ids=true, to_apply=%region_5.6 | all-reduce | flops 6144 | bytes 49152 | tf_op jit(solution)/shard_map/psum | solution.py:120
  170.0 10.8 %all_gather.19 = f32[4,2,3,64]{3,0,1,2:T(4,128)S(1)} all-gather(f32[4,2,1,64]{3,0,1,2:T(4,128)S(1)} %bitcast_select_fusion), channel_id=1, replica_groups=mesh['chan'=32,'row'=8,'col'=3] {'col'}, dimensions={2}, use_global_device_ids=true | all-gather | bytes 8192 | tf_op jit(solution)/shard_map/all_gather | solution.py:34
  180.9 0.8 fusion.30
  181.8 0.9 fusion.32
  182.7 0.9 fusion.48
  183.5 0.9 fusion.50
  184.4 0.9 fusion.42
  185.3 25.7 %all-reduce = (f32[4,512]{1,0:T(4,128)S(1)}, f32[4,512]{1,0:T(4,128)S(1)}, f32[4,512]{1,0:T(4,128)S(1)}) all-reduce(f32[4,512]{1,0:T(4,128)S(1)} %bitcast_subtract_fusion, f32[4,512]{1,0:T(4,128)S(1)} %bitcast.209, f32[4,512]{1,0:T(4,128)S(1)} %bitcast_add_fusion), channel_id=1, replica_groups=mesh['chan'=32,'row'=8,'col'=3] {'row'}, use_global_device_ids=true, to_apply=%region_8.9 | all-reduce | flops 6144 | bytes 49152 | tf_op jit(solution)/shard_map/psum | solution.py:120
  211.0 0.6 copy.162
  (77 shorter events, 3.2 us)
Async XLA Ops:
  23.2 53.1 %all-to-all-start = ((bf16[32,2,384]{2,1,0:T(2,128)(2,1)}), bf16[32,2,384]{2,1,0:T(2,128)(2,1)S(1)}, u32[]{:S(2)}, u32[]{:S(2)}) async-start(bf16[32,2,384]{2,1,0:T(2,128)(2,1)} %reshape.352), calls=%async_computation | async-start | bytes 98304 | tf_op jit(solution)/shard_map/all_to_all | solution.py:51
  51.8 8.0 %copy-start.10 = (f32[4,2,1,64]{3,2,1,0:T(1,128)S(1)}, f32[4,2,1,64]{3,2,1,0:T(1,128)}, u32[]{:S(2)}) copy-start(f32[4,2,1,64]{3,2,1,0:T(1,128)} %param.8) | copy-start | bytes 6148
  53.4 21.3 %copy-start.6 = (bf16[4,192,64]{2,1,0:T(8,128)(2,1)}, bf16[4,192,64]{2,1,0:T(8,128)(2,1)S(1)}, u32[]{:S(2)}) copy-start(bf16[4,192,64]{2,1,0:T(8,128)(2,1)S(1)} %get-tuple-element.22) | copy-start | bytes 294916
  53.4 18.1 %copy-start.11 = (f32[4,64]{1,0:T(4,128)S(1)}, f32[4,64]{1,0:T(4,128)}, u32[]{:S(2)}) copy-start(f32[4,64]{1,0:T(4,128)} %param.7) | copy-start | bytes 3076
  73.8 2.5 %copy-start.4 = (bf16[4,512,64]{1,2,0:T(8,128)(2,1)}, bf16[4,512,64]{1,2,0:T(8,128)(2,1)S(1)}, u32[]{:S(2)}) copy-start(bf16[4,512,64]{1,2,0:T(8,128)(2,1)S(1)} %get-tuple-element.20) | copy-start | bytes 786436
  76.3 19.4 %all-to-all-start.1 = ((bf16[32,2,1024]{2,1,0:T(2,128)(2,1)}), bf16[32,2,1024]{2,1,0:T(2,128)(2,1)S(1)}, u32[]{:S(2)}, u32[]{:S(2)}) async-start(bf16[32,2,1024]{2,1,0:T(2,128)(2,1)} %reshape.350), calls=%async_computation.1 | async-start | bytes 262144 | tf_op jit(solution)/shard_map/all_to_all | solution.py:52
  98.1 1.4 copy-start.3
  98.1 1.4 copy-start.5
  98.1 1.5 copy-start.7
  98.1 1.6 copy-start.8
  98.1 1.6 copy-start.9
  100.6 3.7 %copy-start = (f32[4,192,512]{2,1,0:T(8,128)}, f32[4,192,512]{2,1,0:T(8,128)S(1)}, u32[]{:S(2)}) copy-start(f32[4,192,512]{2,1,0:T(8,128)S(1)} %get-tuple-element.18) | copy-start | bytes 4718596
  141.7 1.7 copy-start.1
  182.7 1.7 copy-start.2
where the time goes:
time: 214 us; the launch traced here: 212 us
  blocking collectives  145 us (68%)
  starting transfers between devices  20.2 us (9%)
  matrix products  16.4 us (8%)
  local copies, waits for them, and re-layouts  12.4 us (6%)
  other arithmetic  9.44 us (4%)
  waiting for transfers between devices  7.76 us (4%)
    psum x3, blocking collectives, on_device(): lax.psum((num_re, num_im, denominator), 'row')  74.9 us
    all_gather x3, blocking collectives, share(): lax.all_gather(own_gains[:, :, None, :], 'col', axis=2, tiled=True)  32.6 us
    all_gather x1, blocking collectives, on_device(): row_pieces = lax.all_gather(voltages, 'col', axis=0, tiled=True)  21.7 us
    all_gather x1, blocking collectives, on_device(): col_pieces = lax.all_gather(voltages, 'row', axis=0, tiled=True)  15.9 us
    all_to_all x1, starting transfers between devices, on_device(): lax.all_to_all(row_pieces, 'chan', split_axis=4, concat_axis=1, tiled=True)  10.1 us
    all_to_all x1, starting transfers between devices, on_device(): lax.all_to_all(col_pieces, 'chan', split_axis=4, concat_axis=1, tiled=True)  10 us
    all_to_all x1, waiting for transfers between devices, on_device(): lax.all_to_all(col_pieces, 'chan', split_axis=4, concat_axis=1, tiled=True)  7.76 us
    unnamed x33, local copies, waits for them, and re-layouts  5.63 us
  transfers between devices with their start and end apart: 2, of which 1 were waited for; matrix products, arithmetic and copies ran while one was open for 8% of the time, Pallas kernels for 0%

commit v1 on v0

v1 whole, which is shorter than its diff:
```python
import math

import jax
import jax.numpy as jnp
from jax import lax
from jax.sharding import PartitionSpec as P

PIX = 256
ITERS = 3


phase_scale = 2.0 * math.pi * 8.0
small_eps = 1e-06


def steering(positions, ell_coord, emm_coord, frequencies):
    angle = (
        phase_scale
        * frequencies[:, None, None]
        * (
            positions[0][None, :, None] * ell_coord[None, None, :]
            + positions[1][None, :, None] * emm_coord[None, None, :]
        )
    )
    return (jnp.cos(angle).astype(jnp.bfloat16), (-jnp.sin(angle)).astype(jnp.bfloat16))


def antenna_major(block):
    count, subant, halves, samples, chans = block.shape
    return jnp.transpose(block, (4, 0, 1, 2, 3)).reshape(chans, count * subant, halves, samples)


def on_device(voltages, source_flux, initial_gains, antenna_positions, flagged, source_pixels):
    n_rows = lax.axis_size("row")
    n_cols = lax.axis_size("col")
    n_chans = lax.axis_size("chan")
    row_index = lax.axis_index("row")
    col_index = lax.axis_index("col")
    chan_index = lax.axis_index("chan")
    groups, subant = antenna_positions.shape[1], antenna_positions.shape[2]
    antennas = groups * subant
    per_chan = source_flux.shape[0]
    samples = voltages.shape[3]
    own_group = row_index * n_cols + col_index

    own_volt = lax.all_to_all(voltages, "chan", split_axis=4, concat_axis=1, tiled=True)
    all_volt = lax.all_gather(own_volt, ("row", "col"), axis=0, tiled=True)
    all_gains = lax.all_gather(initial_gains, ("row", "col"), axis=2, tiled=True)

    q_antenna = antenna_major(all_volt)
    p_antenna = antenna_major(own_volt)
    q_left = q_antenna.reshape(per_chan, antennas, 2 * samples)
    q_swap = jnp.concatenate([q_antenna[:, :, 1], -q_antenna[:, :, 0]], axis=2)
    p_left = p_antenna.reshape(per_chan, subant, 2 * samples)
    vis_re = (
        jnp.einsum("cpk,cqk->cpq", p_left, q_left, preferred_element_type=jnp.float32) / samples
    )
    vis_im = (
        jnp.einsum("cpk,cqk->cpq", p_left, q_swap, preferred_element_type=jnp.float32) / samples
    )
    positions = antenna_positions.reshape(2, antennas)
    p_pos = lax.dynamic_index_in_dim(antenna_positions, own_group, 1, keepdims=False)
    flag_vec = flagged.reshape(antennas)
    own_flag = lax.dynamic_index_in_dim(flagged, own_group, 0, keepdims=False)
    q_ids = jnp.arange(antennas, dtype=jnp.int32)
    p_ids = own_group * subant + jnp.arange(subant, dtype=jnp.int32)
    pixel_float = source_pixels.astype(jnp.float32)
    ell_coord = (pixel_float[:, 0] - 0.5 * PIX) / PIX
    emm_coord = (pixel_float[:, 1] - 0.5 * PIX) / PIX
    channel_ids = chan_index * per_chan + jnp.arange(per_chan, dtype=jnp.int32)
    frequencies = 1.0 + channel_ids.astype(jnp.float32) / (per_chan * n_chans)
    steer_re, steer_im = steering(positions, ell_coord, emm_coord, frequencies)
    far_re, far_im = steering(p_pos, ell_coord, emm_coord, frequencies)
    weight_re = (source_flux[:, None, :] * far_re).astype(jnp.bfloat16)
    weight_im = (source_flux[:, None, :] * far_im).astype(jnp.bfloat16)
    steer_both = jnp.concatenate([steer_re, steer_im], axis=2)
    steer_swap = jnp.concatenate([steer_im, -steer_re], axis=2)
    weight_both = jnp.concatenate([weight_re, weight_im], axis=2)
    model_re = jnp.einsum(
        "cpk,cqk->cpq", weight_both, steer_both, preferred_element_type=jnp.float32
    )
    model_im = jnp.einsum(
        "cpk,cqk->cpq", weight_both, steer_swap, preferred_element_type=jnp.float32
    )
    live = (1 - flag_vec).astype(jnp.float32)
    apart = (p_ids[:, None] != q_ids[None, :]).astype(jnp.float32)
    keep = (live[None, :] * apart)[None, :, :]
    data_re = keep * (model_re * vis_re + model_im * vis_im)
    data_im = keep * (model_re * vis_im - model_im * vis_re)
    power = keep * (model_re * model_re + model_im * model_im)
    highest = lax.Precision.HIGHEST
    current = initial_gains[:, :, 0, :]
    gains_q = all_gains.reshape(per_chan, 2, antennas)
    for iteration in range(ITERS):
        if iteration > 0:
            gains_q = lax.all_gather(current, ("row", "col"), axis=2, tiled=True)
        gain_re = gains_q[:, 0]
        gain_im = gains_q[:, 1]
        num_re = jnp.einsum("cq,cpq->cp", gain_re, data_re, precision=highest) + jnp.einsum(
            "cq,cpq->cp", gain_im, data_im, precision=highest
        )
        num_im = jnp.einsum("cq,cpq->cp", gain_re, data_im, precision=highest) - jnp.einsum(
            "cq,cpq->cp", gain_im, data_re, precision=highest
        )
        denominator = jnp.einsum(
            "cq,cpq->cp", gain_re * gain_re + gain_im * gain_im, power, precision=highest
        )
        fresh = jnp.stack(
            [num_re / (denominator + small_eps), -num_im / (denominator + small_eps)], axis=1
        )
        current = jnp.where(own_flag[None, None, :] == 1, current, 0.5 * (current + fresh))
    return current[:, :, None, :]


def solution(mesh):
    in_specs = (
        P(("row", "col"), "chan", None, None, None),
        P("chan", None),
        P("chan", None, ("row", "col"), None),
        P(),
        P(),
        P(),
    )
    out_specs = P("chan", None, ("row", "col"), None)
    return jax.shard_map(
        on_device, mesh=mesh, in_specs=in_specs, out_specs=out_specs, check_vma=False
    )
```

time: 214 us -> 486 us (2.27)
  the two profiles are of different devices: /device:TPU:1 before, /device:TPU:94 now
where the time goes in v1:
time: 486 us; the launch traced here: 485 us
  blocking collectives  390 us (80%)
  other arithmetic  30.4 us (6%)
  matrix products  28.6 us (6%)
  local copies, waits for them, and re-layouts  23.6 us (5%)
  starting transfers between devices  12 us (2%)
    all_gather x2, blocking collectives, on_device(): gains_q = lax.all_gather(current, ('row', 'col'), axis=2, tiled=True)  254 us
    all_gather x1, blocking collectives, on_device(): all_volt = lax.all_gather(own_volt, ('row', 'col'), axis=0, tiled=True)  70.3 us
    all_gather x1, blocking collectives, on_device(): lax.all_gather(initial_gains, ('row', 'col'), axis=2, tiled=True)  66.2 us
    all_to_all x1, starting transfers between devices, on_device(): lax.all_to_all(voltages, 'chan', split_axis=4, concat_axis=1, tiled=True)  12 us
    convert_element_type x1, other arithmetic, steering(): jnp.cos(angle).astype(jnp.bfloat16)  11.7 us
    neg x1, other arithmetic, on_device(): steer_swap = jnp.concatenate([steer_im, -steer_re], axis=2)  11.6 us
  transfers between devices with their start and end apart: 1, of which 0 were waited for; matrix products, arithmetic and copies ran while one was open for 7% of the time, Pallas kernels for 0%

profile of v1, /device:TPU:94, one launch (start us, length us, event | category | flops | bytes accessed | tf_op | source)
XLA Modules:
  0.0 485.4 jit_solution(10886795503305492934)
XLA Ops:
  0.0 0.8 copy.71
  0.8 0.7 reshape.283
  1.6 12.0 %all-to-all-start = ((bf16[32,2,128]{2,1,0:T(2,128)(2,1)}), bf16[32,2,128]{2,1,0:T(2,128)(2,1)S(1)}, u32[]{:S(2)}, u32[]{:S(2)}) async-start(bf16[32,2,128]{2,1,0:T(2,128)(2,1)} %reshape.283), calls=%async_computation | async-start | bytes 32768 | tf_op jit(solution)/shard_map/all_to_all | solution.py:46
  13.6 0.7 convert_element_type.48
  14.3 0.7 fusion.52
  15.6 11.7 %fusion = (bf16[4,1536,64]{2,1,0:T(8,128)(2,1)S(1)}, bf16[4,1536,64]{2,1,0:T(8,128)(2,1)S(1)}) fusion(f32[1536,64]{1,0:T(8,128)S(1)} %multiply_add_fusion, f32[4]{0:T(128)S(1)} %add_multiply_fusion.2), kind=kLoop, calls=%fused_computation.2 | loop fusion | flops 1572864 | bytes 1966096 | tf_op jit(solution)/shard_map/convert_element_type | solution.py:25
  27.4 11.6 %fusion.48 = bf16[4,1536,64]{2,1,0:T(8,128)(2,1)} fusion(f32[1536,64]{1,0:T(8,128)S(1)} %multiply_add_fusion, f32[4]{0:T(128)S(1)} %add_multiply_fusion.2), kind=kLoop, calls=%fused_computation.93 | loop fusion | flops 1966080 | bytes 1179664 | tf_op jit(solution)/shard_map/neg | solution.py:77
  39.5 0.7 convert_element_type.46
  40.1 66.2 %all_gather.13 = f32[4,2,24,64]{3,0,1,2:T(4,128)S(1)} all-gather(f32[4,2,1,64]{3,0,1,2:T(4,128)S(1)} %copy.78), channel_id=1, replica_groups=mesh['chan'=32,'row'=8,'col'=3] {'row','col'}, dimensions={2}, use_global_device_ids=true | all-gather | bytes 51200 | tf_op jit(solution)/shard_map/all_gather | solution.py:48
  106.5 0.7 fusion.51
  107.1 0.7 fusion.42
  107.9 0.6 multiply_convert_fusion.1
  108.5 0.8 fusion.15
  109.3 1.4 fusion.22
  110.7 2.2 fusion.4
  112.9 1.2 compare_bitcast_fusion
  114.1 0.6 copy.127
  114.7 1.4 copy.83
  116.6 70.3 %all_gather.12 = bf16[24,64,2,16,4]{1,3,4,2,0:T(8,128)(2,1)S(1)} all-gather(bf16[1,64,2,16,4]{1,3,4,2,0:T(8,128)(2,1)S(1)} %copy.75), channel_id=1, replica_groups=mesh['chan'=32,'row'=8,'col'=3] {'row','col'}, dimensions={0}, use_global_device_ids=true | all-gather | bytes 409600 | tf_op jit(solution)/shard_map/all_gather | solution.py:47
  189.9 0.5 copy-done.3
  190.9 3.0 add_multiply_fusion.1
  193.9 1.4 fusion.25
  195.4 1.4 fusion.29
  196.8 1.4 fusion.31
  198.3 1.5 fusion.23
  199.7 1.4 fusion.27
  201.5 113.6 %all_gather.14 = f32[4,2,1536]{0,1,2:T(2,128)S(1)} all-gather(f32[4,2,64]{0,1,2:T(2,128)S(1)} %bitcast_select_fusion), channel_id=1, replica_groups=mesh['chan'=32,'row'=8,'col'=3] {'row','col'}, dimensions={2}, use_global_device_ids=true | all-gather | bytes 51200 | tf_op jit(solution)/shard_map/all_gather | solution.py:96
  315.1 2.1 fusion.50
  317.2 1.4 copy.99
  318.6 1.4 fusion.57
  320.0 1.4 fusion.54
  321.4 1.4 copy.97
  322.8 1.4 fusion.56
  324.2 1.4 fusion.53
  325.6 1.0 add_bitcast_fusion.1
  326.6 1.4 copy.101
  328.0 2.8 fusion.55
  331.1 140.3 %all_gather.15 = f32[4,2,1536]{0,1,2:T(2,128)S(1)} all-gather(f32[4,2,64]{0,1,2:T(2,128)S(1)} %multiply_select_fusion), channel_id=1, replica_groups=mesh['chan'=32,'row'=8,'col'=3] {'row','col'}, dimensions={2}, use_global_device_ids=true | all-gather | bytes 51200 | tf_op jit(solution)/shard_map/all_gather | solution.py:96
  471.4 2.1 fusion.49
  473.5 1.4 copy.107
  474.9 1.4 fusion.62
  476.3 1.4 fusion.59
  477.7 1.4 copy.105
  479.2 1.4 fusion.61
  480.6 1.4 fusion.58
  482.4 1.0 copy-done.1
  483.4 1.4 fusion.60
  484.8 0.6 copy.88
  (82 shorter events, 6.2 us)
Async XLA Ops:
  1.6 114.6 %all-to-all-start = ((bf16[32,2,128]{2,1,0:T(2,128)(2,1)}), bf16[32,2,128]{2,1,0:T(2,128)(2,1)S(1)}, u32[]{:S(2)}, u32[]{:S(2)}) async-start(bf16[32,2,128]{2,1,0:T(2,128)(2,1)} %reshape.283), calls=%async_computation | async-start | bytes 32768 | tf_op jit(solution)/shard_map/all_to_all | solution.py:46
  27.3 83.4 %copy-start.2 = (bf16[4,1536,64]{2,1,0:T(8,128)(2,1)}, bf16[4,1536,64]{2,1,0:T(8,128)(2,1)S(1)}, u32[]{:S(2)}) copy-start(bf16[4,1536,64]{2,1,0:T(8,128)(2,1)S(1)} %get-tuple-element.13) | copy-start | bytes 2359300
  27.3 12.1 %copy-start.21 = (s32[24,64]{1,0:T(8,128)S(1)}, s32[24,64]{1,0:T(8,128)}, u32[]{:S(2)}) copy-start(s32[24,64]{1,0:T(8,128)} %param.10) | copy-start | bytes 18436
  27.3 12.8 %copy-start.19 = (f32[4,2,1,64]{3,2,1,0:T(1,128)S(1)}, f32[4,2,1,64]{3,2,1,0:T(1,128)}, u32[]{:S(2)}) copy-start(f32[4,2,1,64]{3,2,1,0:T(1,128)} %param.8) | copy-start | bytes 6148
  27.3 80.6 %copy-start.23 = (f32[4,64]{1,0:T(4,128)S(1)}, f32[4,64]{1,0:T(4,128)}, u32[]{:S(2)}) copy-start(f32[4,64]{1,0:T(4,128)} %param.7) | copy-start | bytes 3076
  106.4 1.5 copy-start.9
  108.5 4.4 copy-start.11
  108.5 4.4 copy-start.13
  110.7 3.4 copy-start.16
  189.0 1.4 copy-start.3
  189.0 1.9 copy-start.8
  189.0 1.9 copy-start.12
  189.1 1.9 copy-start.14
  190.9 3.0 copy-start.10
  193.9 5.8 %copy-start = (f32[4,64,1536]{2,1,0:T(8,128)}, f32[4,64,1536]{2,1,0:T(8,128)S(1)}, u32[]{:S(2)}) copy-start(f32[4,64,1536]{2,1,0:T(8,128)S(1)} %get-tuple-element.7) | copy-start | bytes 4718596
  193.9 1.5 copy-start.17
  196.8 2.9 copy-start.18
  198.3 3.0 copy-start.15
  198.3 3.0 copy-start.22
  322.8 2.8 copy-start.6
  322.8 2.8 copy-start.7
  479.1 2.8 copy-start.4
  479.2 2.8 copy-start.5
  482.0 1.4 copy-start.1
  482.1 2.7 copy-start.20

commit v2 on v0

--- a/solution.py
+++ b/solution.py
@@ -31,8 +31,10 @@
 
 
 def share(own_gains):
-    gathered = lax.all_gather(own_gains[:, :, None, :], "col", axis=2, tiled=True)
-    return gathered.reshape(gathered.shape[0], 2, gathered.shape[2] * gathered.shape[3])
+    n_cols = lax.axis_size("col")
+    outgoing = jnp.broadcast_to(own_gains[None], (n_cols,) + own_gains.shape)
+    gathered = lax.all_to_all(outgoing, "col", 0, 0, tiled=True)
+    return jnp.transpose(gathered, (1, 2, 0, 3))
 
 
 def on_device(voltages, source_flux, initial_gains, antenna_positions, flagged, source_pixels):
@@ -103,11 +105,11 @@
     power = keep * (model_re * model_re + model_im * model_im)
     highest = lax.Precision.HIGHEST
     current = initial_gains[:, :, 0, :]
-    own_count = current.shape[2]
+    row_flags = row_flag.reshape(1, 1, n_cols, subant)
+    row_gains = share(current)
     for iteration in range(ITERS):
-        row_gains = share(current)
-        gain_re = row_gains[:, 0]
-        gain_im = row_gains[:, 1]
+        gain_re = row_gains[:, 0].reshape(per_chan, row_count)
+        gain_im = row_gains[:, 1].reshape(per_chan, row_count)
         num_re = jnp.einsum("cq,cqp->cp", gain_re, data_re, precision=highest) + jnp.einsum(
             "cq,cqp->cp", gain_im, data_im, precision=highest
         )
@@ -117,14 +119,20 @@
         denominator = jnp.einsum(
             "cq,cqp->cp", gain_re * gain_re + gain_im * gain_im, power, precision=highest
         )
-        total_re, total_im, total_den = lax.psum((num_re, num_im, denominator), "row")
-        total_re = lax.dynamic_slice_in_dim(total_re, row_index * own_count, own_count, 1)
-        total_im = lax.dynamic_slice_in_dim(total_im, row_index * own_count, own_count, 1)
-        total_den = lax.dynamic_slice_in_dim(total_den, row_index * own_count, own_count, 1)
+        partial = jnp.stack([num_re, num_im, denominator], axis=0).reshape(3, per_chan, n_rows, subant)
+        outgoing = jnp.broadcast_to(
+            jnp.transpose(partial, (2, 0, 1, 3))[:, None], (n_rows, n_cols, 3, per_chan, subant)
+        ).reshape(n_rows * n_cols, 3, per_chan, subant)
+        incoming = lax.all_to_all(outgoing, ("row", "col"), 0, 0, tiled=True)
+        totals = incoming.reshape(n_rows, n_cols, 3, per_chan, subant).sum(axis=0)
+        total_re = jnp.transpose(totals[:, 0], (1, 0, 2))
+        total_im = jnp.transpose(totals[:, 1], (1, 0, 2))
+        total_den = jnp.transpose(totals[:, 2], (1, 0, 2))
         fresh = jnp.stack(
             [total_re / (total_den + small_eps), -total_im / (total_den + small_eps)], axis=1
         )
-        current = jnp.where(own_flag[None, None, :] == 1, current, 0.5 * (current + fresh))
+        row_gains = jnp.where(row_flags == 1, row_gains, 0.5 * (row_gains + fresh))
+    current = lax.dynamic_index_in_dim(row_gains, col_index, 2, keepdims=False)
     return current[:, :, None, :]
 
 

time: 214 us -> 173 us (0.81)
  blocking collectives: 145 us -> 43.2 us
  waiting for transfers between devices: 7.76 us -> 35.4 us
  starting transfers between devices: 20.2 us -> 44.9 us
  local copies, waits for them, and re-layouts: 12.4 us -> 18 us
  other arithmetic: 9.44 us -> 13.3 us
    psum x3 -> x0, blocking collectives: 74.9 us -> none  [on_device(): lax.psum((num_re, num_im, denominator), 'row')]
    all_gather x3 -> x0, blocking collectives: 32.6 us -> none  [share(): lax.all_gather(own_gains[:, :, None, :], 'col', axis=2, tiled=True)]
    all_to_all x0 -> x3, starting transfers between devices: none -> 30.7 us  [the longest x2 16.2 us: on_device(): incoming = lax.all_to_all(outgoing, ('row', 'col'), 0, 0, tiled=True)]
    all_to_all x0 -> x3, waiting for transfers between devices: none -> 20.2 us  [the longest x2 20.2 us: on_device(): incoming = lax.all_to_all(outgoing, ('row', 'col'), 0, 0, tiled=True)]
    all_to_all x0 -> x1, blocking collectives: none -> 15.4 us  [on_device(): incoming = lax.all_to_all(outgoing, ('row', 'col'), 0, 0, tiled=True)]
    all_gather x1, blocking collectives: 21.7 us -> 13.7 us  [on_device(): row_pieces = lax.all_gather(voltages, 'col', axis=0, tiled=True)]
    all_to_all x1, waiting for transfers between devices: 0.01 us -> 7.46 us  [on_device(): lax.all_to_all(row_pieces, 'chan', split_axis=4, concat_axis=1, tiled=True)]
    all_to_all x1, starting transfers between devices: 10 us -> 4.04 us  [on_device(): lax.all_to_all(col_pieces, 'chan', split_axis=4, concat_axis=1, tiled=True)]
  transfers between devices with their start and end apart: 2 -> 5, of which waited for: 1 -> 4; matrix products, arithmetic and copies ran while one was open for 8% -> 12% of each run, Pallas kernels for 0% -> 0%
where the time goes in v2:
time: 173 us; the launch traced here: 172 us
  starting transfers between devices  44.9 us (26%)
  blocking collectives  43.2 us (25%)
  waiting for transfers between devices  35.4 us (20%)
  local copies, waits for them, and re-layouts  18 us (10%)
  matrix products  16.4 us (9%)
  other arithmetic  13.3 us (8%)
    all_to_all x2, waiting for transfers between devices, on_device(): incoming = lax.all_to_all(outgoing, ('row', 'col'), 0, 0, tiled=True)  20.2 us
    all_to_all x2, starting transfers between devices, on_device(): incoming = lax.all_to_all(outgoing, ('row', 'col'), 0, 0, tiled=True)  16.2 us
    all_to_all x1, blocking collectives, on_device(): incoming = lax.all_to_all(outgoing, ('row', 'col'), 0, 0, tiled=True)  15.4 us
    all_to_all x1, starting transfers between devices, share(): gathered = lax.all_to_all(outgoing, 'col', 0, 0, tiled=True)  14.5 us
    all_gather x1, blocking collectives, on_device(): col_pieces = lax.all_gather(voltages, 'row', axis=0, tiled=True)  14.1 us
    all_gather x1, blocking collectives, on_device(): row_pieces = lax.all_gather(voltages, 'col', axis=0, tiled=True)  13.7 us
    all_to_all x1, starting transfers between devices, on_device(): lax.all_to_all(row_pieces, 'chan', split_axis=4, concat_axis=1, tiled=True)  10.2 us
    unnamed x36, local copies, waits for them, and re-layouts  8.4 us
  transfers between devices with their start and end apart: 5, of which 4 were waited for; matrix products, arithmetic and copies ran while one was open for 12% of the time, Pallas kernels for 0%

profile of v2, /device:TPU:1, one launch (start us, length us, event | category | flops | bytes accessed | tf_op | source)
XLA Modules:
  0.0 171.7 jit_solution(5479967404297750421)
XLA Ops:
  0.0 0.7 copy.227
  1.4 14.5 %all-to-all-start = ((f32[3,1,512]{2,1,0:T(1,128)}), f32[3,1,512]{2,1,0:T(1,128)S(1)}, u32[]{:S(2)}, u32[]{:S(2)}) async-start(f32[3,1,512]{2,1,0:T(1,128)} %reshape.379), calls=%async_computation | async-start | bytes 12288 | tf_op jit(solution)/shard_map/all_to_all | solution.py:36
  16.5 0.8 copy.229
  17.3 0.7 constant_dynamic-slice_fusion
  18.3 1.6 fusion.3
  19.9 2.0 %fusion.54 = bf16[4,192,64]{2,1,0:T(8,128)(2,1)} fusion(f32[192,64]{1,0:T(8,128)S(1)} %multiply_add_fusion.1, f32[4]{0:T(128)S(1)} %add_multiply_fusion.2), kind=kLoop, calls=%fused_computation.113 | loop fusion | flops 245760 | bytes 147472 | tf_op jit(solution)/shard_map/neg | solution.py:92
  22.0 14.1 %all_gather.7 = bf16[8,2,2,16,128]{4,3,2,1,0:T(8,128)(2,1)S(1)} all-gather(bf16[1,2,2,16,128]{4,3,2,1,0:T(8,128)(2,1)} %param.6), channel_id=1, replica_groups=mesh['chan'=32,'row'=8,'col'=3] {'row'}, dimensions={0}, use_global_device_ids=true | all-gather | bytes 147456 | tf_op jit(solution)/shard_map/all_gather | solution.py:51
  36.2 0.7 subtract_convert_fusion
  37.3 3.0 %multiply_convert_fusion.1 = (bf16[4,512,64]{1,2,0:T(8,128)(2,1)S(1)}, bf16[4,512,64]{1,2,0:T(8,128)(2,1)S(1)}) fusion(f32[512,64]{0,1:T(8,128)S(1)} %multiply_add_fusion, f32[4]{0:T(128)S(1)} %add_multiply_fusion.2, f32[4,64]{1,0:T(4,128)} %param.7), kind=kLoop, calls=%fused_computation.14 | loop fusion | flops 1310720 | bytes 656400 | tf_op jit(solution)/shard_map/convert_element_type | solution.py:89
  40.3 0.9 compare_select_fusion
  41.1 1.6 fusion.7
  42.7 13.7 %all_gather.6 = bf16[3,2,2,16,128]{4,3,2,1,0:T(8,128)(2,1)S(1)} all-gather(bf16[1,2,2,16,128]{4,3,2,1,0:T(8,128)(2,1)S(1)} %copy-done.10), channel_id=1, replica_groups=mesh['chan'=32,'row'=8,'col'=3] {'col'}, dimensions={0}, use_global_device_ids=true | all-gather | bytes 65536 | tf_op jit(solution)/shard_map/all_gather | solution.py:50
  56.9 1.1 reshape.383
  58.0 1.4 copy.235
  59.4 1.8 %reshape.381 = bf16[32,2,1024]{2,1,0:T(2,128)(2,1)} reshape(bf16[128,2,2,8,16]{4,3,2,1,0:T(8,128)(2,1)S(1)} %bitcast.260) | data formatting | bytes 262144
  61.2 10.2 %all-to-all-start.1 = ((bf16[32,2,384]{2,1,0:T(2,128)(2,1)}), bf16[32,2,384]{2,1,0:T(2,128)(2,1)S(1)}, u32[]{:S(2)}, u32[]{:S(2)}) async-start(bf16[32,2,384]{2,1,0:T(2,128)(2,1)} %reshape.383), calls=%async_computation.1 | async-start | bytes 98304 | tf_op jit(solution)/shard_map/all_to_all | solution.py:53
  73.0 7.5 %all-to-all-done.1 = bf16[32,2,384]{2,1,0:T(2,128)(2,1)S(1)} async-done(((bf16[32,2,384]{2,1,0:T(2,128)(2,1)}), bf16[32,2,384]{2,1,0:T(2,128)(2,1)S(1)}, u32[]{:S(2)}, u32[]{:S(2)}) %all-to-all-start.1) | async-done | bytes 49184 | tf_op jit(solution)/shard_map/all_to_all | solution.py:53
  80.5 4.0 %all-to-all-start.2 = ((bf16[32,2,1024]{2,1,0:T(2,128)(2,1)}), bf16[32,2,1024]{2,1,0:T(2,128)(2,1)S(1)}, u32[]{:S(2)}, u32[]{:S(2)}) async-start(bf16[32,2,1024]{2,1,0:T(2,128)(2,1)} %reshape.381), calls=%async_computation.2 | async-start | bytes 262144 | tf_op jit(solution)/shard_map/all_to_all | solution.py:54
  86.1 7.7 %all-to-all-done.2 = bf16[32,2,1024]{2,1,0:T(2,128)(2,1)S(1)} async-done(((bf16[32,2,1024]{2,1,0:T(2,128)(2,1)}), bf16[32,2,1024]{2,1,0:T(2,128)(2,1)S(1)}, u32[]{:S(2)}, u32[]{:S(2)}) %all-to-all-start.2) | async-done | bytes 131104 | tf_op jit(solution)/shard_map/all_to_all | solution.py:54
  93.8 0.7 reshape.382
  94.8 1.3 copy.238
  97.9 0.9 subtract_multiply_fusion
  98.8 0.9 fusion.61
  99.7 0.9 fusion.59
  100.7 0.9 fusion.60
  101.6 0.9 fusion.58
  102.5 0.9 fusion.48
  103.7 0.8 reshape.385
  104.5 10.8 %all-to-all-start.3 = ((f32[24,1,768]{2,1,0:T(1,128)}), f32[24,1,768]{2,1,0:T(1,128)S(1)}, u32[]{:S(2)}, u32[]{:S(2)}) async-start(f32[24,1,768]{2,1,0:T(1,128)} %reshape.385), calls=%async_computation.3 | async-start | bytes 147456 | tf_op jit(solution)/shard_map/all_to_all | solution.py:126
  115.3 0.7 fusion.50
  116.0 10.3 %all-to-all-done.3 = f32[24,1,768]{2,1,0:T(1,128)S(1)} async-done(((f32[24,1,768]{2,1,0:T(1,128)}), f32[24,1,768]{2,1,0:T(1,128)S(1)}, u32[]{:S(2)}, u32[]{:S(2)}) %all-to-all-start.3) | async-done | bytes 73760 | tf_op jit(solution)/shard_map/all_to_all | solution.py:126
  126.3 0.8 reduce.9
  127.7 0.9 fusion.65
  128.6 0.9 fusion.63
  129.4 0.9 fusion.64
  130.3 0.9 fusion.62
  131.1 0.9 fusion.46
  132.5 15.4 %all_to_all.56 = f32[24,1,768]{2,1,0:T(1,128)S(1)} all-to-all(f32[24,1,768]{2,1,0:T(1,128)S(1)} %reshape.387), channel_id=1, replica_groups=mesh['chan'=32,'row'=8,'col'=3] {'row','col'}, dimensions={0} | all-to-all | bytes 147456 | tf_op jit(solution)/shard_map/all_to_all | solution.py:126
  147.9 0.8 reduce.10
  149.3 0.9 fusion.69
  150.1 0.9 fusion.67
  151.0 0.9 fusion.68
  151.9 0.9 fusion.66
  152.7 0.9 fusion.44
  153.9 0.8 reshape.389
  154.7 5.5 %all-to-all-start.5 = ((f32[24,1,768]{2,1,0:T(1,128)}), f32[24,1,768]{2,1,0:T(1,128)S(1)}, u32[]{:S(2)}, u32[]{:S(2)}) async-start(f32[24,1,768]{2,1,0:T(1,128)} %reshape.389), calls=%async_computation.5 | async-start | bytes 147456 | tf_op jit(solution)/shard_map/all_to_all | solution.py:126
  160.2 9.9 %all-to-all-done.5 = f32[24,1,768]{2,1,0:T(1,128)S(1)} async-done(((f32[24,1,768]{2,1,0:T(1,128)}), f32[24,1,768]{2,1,0:T(1,128)S(1)}, u32[]{:S(2)}, u32[]{:S(2)}) %all-to-all-start.5) | async-done | bytes 73760 | tf_op jit(solution)/shard_map/all_to_all | solution.py:126
  170.1 0.8 reduce.11
  (124 shorter events, 10.8 us)
Async XLA Ops:
  1.4 59.8 %all-to-all-start = ((f32[3,1,512]{2,1,0:T(1,128)}), f32[3,1,512]{2,1,0:T(1,128)S(1)}, u32[]{:S(2)}, u32[]{:S(2)}) async-start(f32[3,1,512]{2,1,0:T(1,128)} %reshape.379), calls=%async_computation | async-start | bytes 12288 | tf_op jit(solution)/shard_map/all_to_all | solution.py:36
  19.9 22.8 %copy-start.6 = (bf16[4,192,64]{2,1,0:T(8,128)(2,1)}, bf16[4,192,64]{2,1,0:T(8,128)(2,1)S(1)}, u32[]{:S(2)}) copy-start(bf16[4,192,64]{2,1,0:T(8,128)(2,1)S(1)} %get-tuple-element.13) | copy-start | bytes 294916
  40.3 0.9 copy-start.4
  40.3 2.5 %copy-start.10 = (bf16[1,2,2,16,128]{4,3,2,1,0:T(8,128)(2,1)S(1)}, bf16[1,2,2,16,128]{4,3,2,1,0:T(8,128)(2,1)}, u32[]{:S(2)}) copy-start(bf16[1,2,2,16,128]{4,3,2,1,0:T(8,128)(2,1)} %param.6) | copy-start | bytes 49156
  61.2 19.3 %all-to-all-start.1 = ((bf16[32,2,384]{2,1,0:T(2,128)(2,1)}), bf16[32,2,384]{2,1,0:T(2,128)(2,1)S(1)}, u32[]{:S(2)}, u32[]{:S(2)}) async-start(bf16[32,2,384]{2,1,0:T(2,128)(2,1)} %reshape.383), calls=%async_computation.1 | async-start | bytes 98304 | tf_op jit(solution)/shard_map/all_to_all | solution.py:53
  80.5 13.3 %all-to-all-start.2 = ((bf16[32,2,1024]{2,1,0:T(2,128)(2,1)}), bf16[32,2,1024]{2,1,0:T(2,128)(2,1)S(1)}, u32[]{:S(2)}, u32[]{:S(2)}) async-start(bf16[32,2,1024]{2,1,0:T(2,128)(2,1)} %reshape.381), calls=%async_computation.2 | async-start | bytes 262144 | tf_op jit(solution)/shard_map/all_to_all | solution.py:54
  96.2 1.4 copy-start.3
  96.3 1.4 copy-start.5
  96.3 1.5 copy-start.7
  96.3 1.6 copy-start.8
  96.3 1.6 copy-start.9
  98.8 3.7 %copy-start = (f32[4,192,512]{2,1,0:T(8,128)}, f32[4,192,512]{2,1,0:T(8,128)S(1)}, u32[]{:S(2)}) copy-start(f32[4,192,512]{2,1,0:T(8,128)S(1)} %get-tuple-element.9) | copy-start | bytes 4718596
  104.5 21.8 %all-to-all-start.3 = ((f32[24,1,768]{2,1,0:T(1,128)}), f32[24,1,768]{2,1,0:T(1,128)S(1)}, u32[]{:S(2)}, u32[]{:S(2)}) async-start(f32[24,1,768]{2,1,0:T(1,128)} %reshape.385), calls=%async_computation.3 | async-start | bytes 147456 | tf_op jit(solution)/shard_map/all_to_all | solution.py:126
  129.4 1.7 %copy-start.1 = (f32[4,192,512]{2,1,0:T(8,128)S(1)}, f32[4,192,512]{2,1,0:T(8,128)}, u32[]{:S(2)}) copy-start(f32[4,192,512]{2,1,0:T(8,128)} %copy-done) | copy-start | bytes 4718596
  151.0 1.7 %copy-start.2 = (f32[4,192,512]{2,1,0:T(8,128)S(1)}, f32[4,192,512]{2,1,0:T(8,128)}, u32[]{:S(2)}) copy-start(f32[4,192,512]{2,1,0:T(8,128)} %copy-done) | copy-start | bytes 4718596
  154.7 15.4 %all-to-all-start.5 = ((f32[24,1,768]{2,1,0:T(1,128)}), f32[24,1,768]{2,1,0:T(1,128)S(1)}, u32[]{:S(2)}, u32[]{:S(2)}) async-start(f32[24,1,768]{2,1,0:T(1,128)} %reshape.389), calls=%async_computation.5 | async-start | bytes 147456 | tf_op jit(solution)/shard_map/all_to_all | solution.py:126

commit v3 on v2

--- a/solution.py
+++ b/solution.py
@@ -37,6 +37,13 @@
     return jnp.transpose(gathered, (1, 2, 0, 3))
 
 
+def gather_groups(block, axis):
+    count = lax.axis_size(axis)
+    outgoing = jnp.broadcast_to(block[None], (count,) + block.shape)
+    gathered = lax.all_to_all(outgoing, axis, 0, 0, tiled=True)
+    return gathered.reshape((count * block.shape[0],) + block.shape[1:])
+
+
 def on_device(voltages, source_flux, initial_gains, antenna_positions, flagged, source_pixels):
     n_rows = lax.axis_size("row")
     n_cols = lax.axis_size("col")
@@ -47,12 +54,9 @@
     subant = antenna_positions.shape[2]
     per_chan = source_flux.shape[0]
     samples = voltages.shape[3]
-    row_pieces = lax.all_gather(voltages, "col", axis=0, tiled=True)
-    col_pieces = lax.all_gather(voltages, "row", axis=0, tiled=True)
-    row_volt, col_volt = (
-        lax.all_to_all(row_pieces, "chan", split_axis=4, concat_axis=1, tiled=True),
-        lax.all_to_all(col_pieces, "chan", split_axis=4, concat_axis=1, tiled=True),
-    )
+    own_volt = lax.all_to_all(voltages, "chan", split_axis=4, concat_axis=1, tiled=True)
+    row_volt = gather_groups(own_volt, "col")
+    col_volt = gather_groups(own_volt, "row")
     row_antenna = antenna_major(row_volt)
     col_antenna = antenna_major(col_volt)
     row_count = row_antenna.shape[1]

time: 173 us -> 149 us (0.86)
  blocking collectives: 43.2 us -> 15.3 us
  starting transfers between devices: 44.9 us -> 50.7 us
  local copies, waits for them, and re-layouts: 18 us -> 13.5 us
  waiting for transfers between devices: 35.4 us -> 38.2 us
    all_gather x2 -> x0, blocking collectives: 27.8 us -> none  [the longest x1 14.1 us: on_device(): col_pieces = lax.all_gather(voltages, 'row', axis=0, tiled=True)]
    all_to_all x2 -> x3, starting transfers between devices: 14.2 us -> 25 us  [the longest x2 15 us: gather_groups(): gathered = lax.all_to_all(outgoing, axis, 0, 0, tiled=True)]
    all_to_all x2, starting transfers between devices: 16.2 us -> 11.2 us  [on_device(): incoming = lax.all_to_all(outgoing, ('row', 'col'), 0, 0, tiled=True)]
    all_to_all x2 -> x3, waiting for transfers between devices: 15.2 us -> 18.3 us  [the longest x2 11 us: gather_groups(): gathered = lax.all_to_all(outgoing, axis, 0, 0, tiled=True)]
    all_gather x2 -> x0, local copies, waits for them, and re-layouts: 1.86 us -> none  [the longest x1 1.43 us: on_device(): col_pieces = lax.all_gather(voltages, 'row', axis=0, tiled=True)]
    unnamed x36 -> x41, local copies, waits for them, and re-layouts: 8.4 us -> 7.38 us
  transfers between devices with their start and end apart: 5 -> 6, of which waited for: 4 -> 5; matrix products, arithmetic and copies ran while one was open for 12% -> 12% of each run, Pallas kernels for 0% -> 0%
where the time goes in v3:
time: 149 us; the launch traced here: 148 us
  starting transfers between devices  50.7 us (34%)
  waiting for transfers between devices  38.2 us (26%)
  matrix products  16.4 us (11%)
  blocking collectives  15.3 us (10%)
  local copies, waits for them, and re-layouts  13.5 us (9%)
  other arithmetic  13.3 us (9%)
    all_to_all x2, waiting for transfers between devices, on_device(): incoming = lax.all_to_all(outgoing, ('row', 'col'), 0, 0, tiled=True)  19.8 us
    all_to_all x1, blocking collectives, on_device(): incoming = lax.all_to_all(outgoing, ('row', 'col'), 0, 0, tiled=True)  15.3 us
    all_to_all x2, starting transfers between devices, gather_groups(): gathered = lax.all_to_all(outgoing, axis, 0, 0, tiled=True)  15 us
    all_to_all x1, starting transfers between devices, share(): gathered = lax.all_to_all(outgoing, 'col', 0, 0, tiled=True)  14.5 us
    all_to_all x2, starting transfers between devices, on_device(): incoming = lax.all_to_all(outgoing, ('row', 'col'), 0, 0, tiled=True)  11.2 us
    all_to_all x2, waiting for transfers between devices, gather_groups(): gathered = lax.all_to_all(outgoing, axis, 0, 0, tiled=True)  11 us
    all_to_all x1, starting transfers between devices, on_device(): lax.all_to_all(voltages, 'chan', split_axis=4, concat_axis=1, tiled=True)  9.94 us
    unnamed x41, local copies, waits for them, and re-layouts  7.38 us
  transfers between devices with their start and end apart: 6, of which 5 were waited for; matrix products, arithmetic and copies ran while one was open for 12% of the time, Pallas kernels for 0%

profile of v3, /device:TPU:1, one launch (start us, length us, event | category | flops | bytes accessed | tf_op | source)
XLA Modules:
  0.0 147.9 jit_solution(14716341463003314960)
XLA Ops:
  0.0 0.7 copy.188
  0.7 0.7 reshape.393
  1.4 14.5 %all-to-all-start = ((f32[3,1,512]{2,1,0:T(1,128)}), f32[3,1,512]{2,1,0:T(1,128)S(1)}, u32[]{:S(2)}, u32[]{:S(2)}) async-start(f32[3,1,512]{2,1,0:T(1,128)} %reshape.393), calls=%async_computation | async-start | bytes 12288 | tf_op jit(solution)/shard_map/all_to_all | solution.py:36
  15.8 0.7 convert_element_type.48
  16.5 0.8 copy.190
  17.3 0.7 constant_dynamic-slice_fusion
  18.3 1.6 %fusion.3 = (bf16[4,192,64]{2,1,0:T(8,128)(2,1)S(1)}, bf16[4,192,64]{2,1,0:T(8,128)(2,1)S(1)}) fusion(f32[192,64]{1,0:T(8,128)S(1)} %multiply_add_fusion.1, f32[4]{0:T(128)S(1)} %add_multiply_fusion.2), kind=kLoop, calls=%fused_computation.15 | loop fusion | flops 196608 | bytes 245776 | tf_op jit(solution)/shard_map/convert_element_type | solution.py:25
  19.9 2.0 %fusion.54 = bf16[4,192,64]{2,1,0:T(8,128)(2,1)} fusion(f32[192,64]{1,0:T(8,128)S(1)} %multiply_add_fusion.1, f32[4]{0:T(128)S(1)} %add_multiply_fusion.2), kind=kLoop, calls=%fused_computation.113 | loop fusion | flops 245760 | bytes 147472 | tf_op jit(solution)/shard_map/neg | solution.py:96
  22.1 0.7 subtract_convert_fusion
  23.2 3.0 %multiply_convert_fusion.1 = (bf16[4,512,64]{1,2,0:T(8,128)(2,1)S(1)}, bf16[4,512,64]{1,2,0:T(8,128)(2,1)S(1)}) fusion(f32[512,64]{0,1:T(8,128)S(1)} %multiply_add_fusion, f32[4]{0:T(128)S(1)} %add_multiply_fusion.2, f32[4,64]{1,0:T(4,128)} %param.7), kind=kLoop, calls=%fused_computation.14 | loop fusion | flops 1310720 | bytes 656400 | tf_op jit(solution)/shard_map/convert_element_type | solution.py:93
  26.2 0.9 compare_select_fusion
  27.1 1.6 %fusion.7 = f32[4,192,512]{2,1,0:T(8,128)} fusion(bf16[4,512,64]{1,2,0:T(8,128)(2,1)S(1)} %get-tuple-element.11, bf16[4,512,64]{1,2,0:T(8,128)(2,1)S(1)} %get-tuple-element.10, bf16[4,192,64]{2,1,0:T(8,128)(2,1)S(1)} %get-tuple-element.13, bf16[4,192,64]{2,1,0:T(8,128)(2,1)S(1)} %get-tuple-element.12), kind=kOutput, calls=%fused_computation.20 | convolution fusion | flops 102105088 | bytes 2293760 | tf_op jit(solution)/shard_map/cqk,cpk->cqp/dot_general | solution.py:98
  28.8 0.7 reshape.395
  29.5 9.9 %all-to-all-start.1 = ((bf16[32,2,128]{2,1,0:T(2,128)(2,1)}), bf16[32,2,128]{2,1,0:T(2,128)(2,1)S(1)}, u32[]{:S(2)}, u32[]{:S(2)}) async-start(bf16[32,2,128]{2,1,0:T(2,128)(2,1)} %reshape.395), calls=%async_computation.1 | async-start | bytes 32768 | tf_op jit(solution)/shard_map/all_to_all | solution.py:57
  41.1 7.4 %all-to-all-done.1 = bf16[32,2,128]{2,1,0:T(2,128)(2,1)S(1)} async-done(((bf16[32,2,128]{2,1,0:T(2,128)(2,1)}), bf16[32,2,128]{2,1,0:T(2,128)(2,1)S(1)}, u32[]{:S(2)}, u32[]{:S(2)}) %all-to-all-start.1) | async-done | bytes 16416 | tf_op jit(solution)/shard_map/all_to_all | solution.py:57
  49.0 0.8 reshape.399
  49.8 6.6 %all-to-all-start.2 = ((bf16[3,2,4096]{2,1,0:T(2,128)(2,1)}), bf16[3,2,4096]{2,1,0:T(2,128)(2,1)S(1)}, u32[]{:S(2)}, u32[]{:S(2)}) async-start(bf16[3,2,4096]{2,1,0:T(2,128)(2,1)} %reshape.399), calls=%async_computation.2 | async-start | bytes 98304 | tf_op jit(solution)/shard_map/all_to_all | solution.py:43
  56.4 0.9 reshape.397
  57.3 6.3 %all-to-all-done.2 = bf16[3,2,4096]{2,1,0:T(2,128)(2,1)S(1)} async-done(((bf16[3,2,4096]{2,1,0:T(2,128)(2,1)}), bf16[3,2,4096]{2,1,0:T(2,128)(2,1)S(1)}, u32[]{:S(2)}, u32[]{:S(2)}) %all-to-all-start.2) | async-done | bytes 49184 | tf_op jit(solution)/shard_map/all_to_all | solution.py:43
  63.6 8.4 %all-to-all-start.3 = ((bf16[8,2,4096]{2,1,0:T(2,128)(2,1)}), bf16[8,2,4096]{2,1,0:T(2,128)(2,1)S(1)}, u32[]{:S(2)}, u32[]{:S(2)}) async-start(bf16[8,2,4096]{2,1,0:T(2,128)(2,1)} %reshape.397), calls=%async_computation.3 | async-start | bytes 262144 | tf_op jit(solution)/shard_map/all_to_all | solution.py:43
  72.6 4.7 %all-to-all-done.3 = bf16[8,2,4096]{2,1,0:T(2,128)(2,1)S(1)} async-done(((bf16[8,2,4096]{2,1,0:T(2,128)(2,1)}), bf16[8,2,4096]{2,1,0:T(2,128)(2,1)S(1)}, u32[]{:S(2)}, u32[]{:S(2)}) %all-to-all-start.3) | async-done | bytes 131104 | tf_op jit(solution)/shard_map/all_to_all | solution.py:43
  79.6 0.9 subtract_multiply_fusion
  80.5 0.9 fusion.61
  81.4 0.9 fusion.59
  82.3 0.9 fusion.60
  83.3 0.9 fusion.58
  84.2 0.9 fusion.48
  85.4 0.8 reshape.401
  86.2 5.8 %all-to-all-start.4 = ((f32[24,1,768]{2,1,0:T(1,128)}), f32[24,1,768]{2,1,0:T(1,128)S(1)}, u32[]{:S(2)}, u32[]{:S(2)}) async-start(f32[24,1,768]{2,1,0:T(1,128)} %reshape.401), calls=%async_computation.4 | async-start | bytes 147456 | tf_op jit(solution)/shard_map/all_to_all | solution.py:130
  91.9 0.7 fusion.50
  92.7 10.0 %all-to-all-done.4 = f32[24,1,768]{2,1,0:T(1,128)S(1)} async-done(((f32[24,1,768]{2,1,0:T(1,128)}), f32[24,1,768]{2,1,0:T(1,128)S(1)}, u32[]{:S(2)}, u32[]{:S(2)}) %all-to-all-start.4) | async-done | bytes 73760 | tf_op jit(solution)/shard_map/all_to_all | solution.py:130
  102.6 0.8 reduce.9
  104.0 0.9 fusion.65
  104.9 0.9 fusion.63
  105.8 0.9 fusion.64
  106.6 0.9 fusion.62
  107.5 0.9 fusion.46
  108.8 15.3 %all_to_all.45 = f32[24,1,768]{2,1,0:T(1,128)S(1)} all-to-all(f32[24,1,768]{2,1,0:T(1,128)S(1)} %reshape.403), channel_id=1, replica_groups=mesh['chan'=32,'row'=8,'col'=3] {'row','col'}, dimensions={0} | all-to-all | bytes 147456 | tf_op jit(solution)/shard_map/all_to_all | solution.py:130
  124.1 0.8 reduce.10
  125.5 0.9 fusion.69
  126.3 0.9 fusion.67
  127.2 0.9 fusion.68
  128.1 0.9 fusion.66
  128.9 0.9 fusion.44
  130.1 0.8 reshape.405
  130.9 5.5 %all-to-all-start.6 = ((f32[24,1,768]{2,1,0:T(1,128)}), f32[24,1,768]{2,1,0:T(1,128)S(1)}, u32[]{:S(2)}, u32[]{:S(2)}) async-start(f32[24,1,768]{2,1,0:T(1,128)} %reshape.405), calls=%async_computation.6 | async-start | bytes 147456 | tf_op jit(solution)/shard_map/all_to_all | solution.py:130
  136.4 9.9 %all-to-all-done.6 = f32[24,1,768]{2,1,0:T(1,128)S(1)} async-done(((f32[24,1,768]{2,1,0:T(1,128)}), f32[24,1,768]{2,1,0:T(1,128)S(1)}, u32[]{:S(2)}, u32[]{:S(2)}) %all-to-all-start.6) | async-done | bytes 73760 | tf_op jit(solution)/shard_map/all_to_all | solution.py:130
  146.2 0.8 reduce.11
  (130 shorter events, 8.8 us)
Async XLA Ops:
  1.4 28.1 %all-to-all-start = ((f32[3,1,512]{2,1,0:T(1,128)}), f32[3,1,512]{2,1,0:T(1,128)S(1)}, u32[]{:S(2)}, u32[]{:S(2)}) async-start(f32[3,1,512]{2,1,0:T(1,128)} %reshape.393), calls=%async_computation | async-start | bytes 12288 | tf_op jit(solution)/shard_map/all_to_all | solution.py:36
  19.9 8.7 %copy-start.6 = (bf16[4,192,64]{2,1,0:T(8,128)(2,1)}, bf16[4,192,64]{2,1,0:T(8,128)(2,1)S(1)}, u32[]{:S(2)}) copy-start(bf16[4,192,64]{2,1,0:T(8,128)(2,1)S(1)} %get-tuple-element.13) | copy-start | bytes 294916
  26.2 0.9 copy-start.4
  26.2 2.5 %copy-start.10 = (bf16[1,2,2,16,128]{4,3,2,1,0:T(8,128)(2,1)S(1)}, bf16[1,2,2,16,128]{4,3,2,1,0:T(8,128)(2,1)}, u32[]{:S(2)}) copy-start(bf16[1,2,2,16,128]{4,3,2,1,0:T(8,128)(2,1)} %param.6) | copy-start | bytes 49156
  29.5 18.9 %all-to-all-start.1 = ((bf16[32,2,128]{2,1,0:T(2,128)(2,1)}), bf16[32,2,128]{2,1,0:T(2,128)(2,1)S(1)}, u32[]{:S(2)}, u32[]{:S(2)}) async-start(bf16[32,2,128]{2,1,0:T(2,128)(2,1)} %reshape.395), calls=%async_computation.1 | async-start | bytes 32768 | tf_op jit(solution)/shard_map/all_to_all | solution.py:57
  49.8 13.9 %all-to-all-start.2 = ((bf16[3,2,4096]{2,1,0:T(2,128)(2,1)}), bf16[3,2,4096]{2,1,0:T(2,128)(2,1)S(1)}, u32[]{:S(2)}, u32[]{:S(2)}) async-start(bf16[3,2,4096]{2,1,0:T(2,128)(2,1)} %reshape.399), calls=%async_computation.2 | async-start | bytes 98304 | tf_op jit(solution)/shard_map/all_to_all | solution.py:43
  63.6 13.6 %all-to-all-start.3 = ((bf16[8,2,4096]{2,1,0:T(2,128)(2,1)}), bf16[8,2,4096]{2,1,0:T(2,128)(2,1)S(1)}, u32[]{:S(2)}, u32[]{:S(2)}) async-start(bf16[8,2,4096]{2,1,0:T(2,128)(2,1)} %reshape.397), calls=%async_computation.3 | async-start | bytes 262144 | tf_op jit(solution)/shard_map/all_to_all | solution.py:43
  77.9 1.4 copy-start.3
  77.9 1.4 copy-start.5
  77.9 1.5 copy-start.7
  77.9 1.6 %copy-start.8 = (f32[192,512]{1,0:T(8,128)S(1)}, f32[192,512]{1,0:T(8,128)}, u32[]{:S(2)}) copy-start(f32[192,512]{1,0:T(8,128)} %compare_select_fusion) | copy-start | bytes 1179652
  77.9 1.6 %copy-start.9 = (bf16[4,192,64]{2,1,0:T(8,128)(2,1)S(1)}, bf16[4,192,64]{2,1,0:T(8,128)(2,1)}, u32[]{:S(2)}) copy-start(bf16[4,192,64]{2,1,0:T(8,128)(2,1)} %fusion.54) | copy-start | bytes 294916
  80.5 3.7 %copy-start = (f32[4,192,512]{2,1,0:T(8,128)}, f32[4,192,512]{2,1,0:T(8,128)S(1)}, u32[]{:S(2)}) copy-start(f32[4,192,512]{2,1,0:T(8,128)S(1)} %get-tuple-element.9) | copy-start | bytes 4718596
  86.2 16.5 %all-to-all-start.4 = ((f32[24,1,768]{2,1,0:T(1,128)}), f32[24,1,768]{2,1,0:T(1,128)S(1)}, u32[]{:S(2)}, u32[]{:S(2)}) async-start(f32[24,1,768]{2,1,0:T(1,128)} %reshape.401), calls=%async_computation.4 | async-start | bytes 147456 | tf_op jit(solution)/shard_map/all_to_all | solution.py:130
  105.8 1.7 %copy-start.1 = (f32[4,192,512]{2,1,0:T(8,128)S(1)}, f32[4,192,512]{2,1,0:T(8,128)}, u32[]{:S(2)}) copy-start(f32[4,192,512]{2,1,0:T(8,128)} %copy-done) | copy-start | bytes 4718596
  127.2 1.7 %copy-start.2 = (f32[4,192,512]{2,1,0:T(8,128)S(1)}, f32[4,192,512]{2,1,0:T(8,128)}, u32[]{:S(2)}) copy-start(f32[4,192,512]{2,1,0:T(8,128)} %copy-done) | copy-start | bytes 4718596
  130.9 15.4 %all-to-all-start.6 = ((f32[24,1,768]{2,1,0:T(1,128)}), f32[24,1,768]{2,1,0:T(1,128)S(1)}, u32[]{:S(2)}, u32[]{:S(2)}) async-start(f32[24,1,768]{2,1,0:T(1,128)} %reshape.405), calls=%async_computation.6 | async-start | bytes 147456 | tf_op jit(solution)/shard_map/all_to_all | solution.py:130

commit v4 on v3

--- a/solution.py
+++ b/solution.py
@@ -30,13 +30,6 @@
     return jnp.transpose(block, (4, 0, 1, 2, 3)).reshape(chans, count * subant, halves, samples)
 
 
-def share(own_gains):
-    n_cols = lax.axis_size("col")
-    outgoing = jnp.broadcast_to(own_gains[None], (n_cols,) + own_gains.shape)
-    gathered = lax.all_to_all(outgoing, "col", 0, 0, tiled=True)
-    return jnp.transpose(gathered, (1, 2, 0, 3))
-
-
 def gather_groups(block, axis):
     count = lax.axis_size(axis)
     outgoing = jnp.broadcast_to(block[None], (count,) + block.shape)
@@ -55,7 +48,14 @@
     per_chan = source_flux.shape[0]
     samples = voltages.shape[3]
     own_volt = lax.all_to_all(voltages, "chan", split_axis=4, concat_axis=1, tiled=True)
-    row_volt = gather_groups(own_volt, "col")
+    volt_size = own_volt.size
+    row_both = gather_groups(
+        jnp.concatenate(
+            [own_volt.astype(jnp.float32).reshape(-1), initial_gains.reshape(-1)]
+        )[None],
+        "col",
+    )
+    row_volt = row_both[:, :volt_size].astype(jnp.bfloat16).reshape((n_cols,) + own_volt.shape[1:])
     col_volt = gather_groups(own_volt, "row")
     row_antenna = antenna_major(row_volt)
     col_antenna = antenna_major(col_volt)
@@ -108,9 +108,8 @@
     data_im = keep * (model_re * vis_im - model_im * vis_re)
     power = keep * (model_re * model_re + model_im * model_im)
     highest = lax.Precision.HIGHEST
-    current = initial_gains[:, :, 0, :]
     row_flags = row_flag.reshape(1, 1, n_cols, subant)
-    row_gains = share(current)
+    row_gains = jnp.transpose(row_both[:, volt_size:].reshape(n_cols, per_chan, 2, subant), (1, 2, 0, 3))
     for iteration in range(ITERS):
         gain_re = row_gains[:, 0].reshape(per_chan, row_count)
         gain_im = row_gains[:, 1].reshape(per_chan, row_count)
@@ -124,8 +123,22 @@
             "cq,cqp->cp", gain_re * gain_re + gain_im * gain_im, power, precision=highest
         )
         partial = jnp.stack([num_re, num_im, denominator], axis=0).reshape(3, per_chan, n_rows, subant)
+        partial = jnp.transpose(partial, (2, 0, 1, 3))
+        if iteration == ITERS - 1:
+            incoming = lax.all_to_all(partial, "row", 0, 0, tiled=True)
+            own_totals = incoming.sum(axis=0)
+            fresh = jnp.stack(
+                [
+                    own_totals[0] / (own_totals[2] + small_eps),
+                    -own_totals[1] / (own_totals[2] + small_eps),
+                ],
+                axis=1,
+            )
+            current = lax.dynamic_index_in_dim(row_gains, col_index, 2, keepdims=False)
+            current = jnp.where(own_flag[None, None, :] == 1, current, 0.5 * (current + fresh))
+            break
         outgoing = jnp.broadcast_to(
-            jnp.transpose(partial, (2, 0, 1, 3))[:, None], (n_rows, n_cols, 3, per_chan, subant)
+            partial[:, None], (n_rows, n_cols, 3, per_chan, subant)
         ).reshape(n_rows * n_cols, 3, per_chan, subant)
         incoming = lax.all_to_all(outgoing, ("row", "col"), 0, 0, tiled=True)
         totals = incoming.reshape(n_rows, n_cols, 3, per_chan, subant).sum(axis=0)
@@ -136,7 +149,6 @@
             [total_re / (total_den + small_eps), -total_im / (total_den + small_eps)], axis=1
         )
         row_gains = jnp.where(row_flags == 1, row_gains, 0.5 * (row_gains + fresh))
-    current = lax.dynamic_index_in_dim(row_gains, col_index, 2, keepdims=False)
     return current[:, :, None, :]
 
 

time: 149 us -> 142 us (0.953)
  blocking collectives: 15.3 us -> 0 us
  local copies, waits for them, and re-layouts: 13.5 us -> 23.7 us
  matrix products: 16.4 us -> 20.1 us
  waiting for transfers between devices: 38.2 us -> 34.5 us
  starting transfers between devices: 50.7 us -> 47.2 us
    all_to_all x1 -> x0, blocking collectives: 15.3 us -> none  [on_device(): incoming = lax.all_to_all(outgoing, ('row', 'col'), 0, 0, tiled=True)]
    all_to_all x1, starting transfers between devices: 14.5 us -> 3.66 us  [on_device(): incoming = lax.all_to_all(partial, 'row', 0, 0, tiled=True)]
    all_to_all x1, waiting for transfers between devices: 7.35 us -> 0.01 us  [on_device(): lax.all_to_all(voltages, 'chan', split_axis=4, concat_axis=1, tiled=True)]
    all_to_all x1, waiting for transfers between devices: 0.01 us -> 4.01 us  [on_device(): incoming = lax.all_to_all(partial, 'row', 0, 0, tiled=True)]
    all_to_all x1, starting transfers between devices: 9.94 us -> 13.5 us  [on_device(): lax.all_to_all(voltages, 'chan', split_axis=4, concat_axis=1, tiled=True)]
    reshape x1 -> x4, local copies, waits for them, and re-layouts: 0.14 us -> 3.59 us  [the longest x1 3.41 us: on_device(): row_both[:, :volt_size].astype(jnp.bfloat16)]
    dot_general x3, matrix products: 2.58 us -> 5.39 us  [on_device(): jnp.einsum('cq,cqp->cp', gain_re * gain_re + gain_im * gain_im, power, pr...]
    all_to_all x2, starting transfers between devices: 11.2 us -> 13.9 us  [on_device(): incoming = lax.all_to_all(outgoing, ('row', 'col'), 0, 0, tiled=True)]
  transfers between devices with their start and end apart: 6 -> 6, of which waited for: 5 -> 5; matrix products, arithmetic and copies ran while one was open for 12% -> 11% of each run, Pallas kernels for 0% -> 0%
where the time goes in v4:
time: 142 us; the launch traced here: 141 us
  starting transfers between devices  47.2 us (33%)
  waiting for transfers between devices  34.5 us (24%)
  local copies, waits for them, and re-layouts  23.7 us (17%)
  matrix products  20.1 us (14%)
  other arithmetic  14.6 us (10%)
    all_to_all x2, waiting for transfers between devices, on_device(): incoming = lax.all_to_all(outgoing, ('row', 'col'), 0, 0, tiled=True)  19 us
    all_to_all x2, starting transfers between devices, gather_groups(): gathered = lax.all_to_all(outgoing, axis, 0, 0, tiled=True)  16.2 us
    all_to_all x2, starting transfers between devices, on_device(): incoming = lax.all_to_all(outgoing, ('row', 'col'), 0, 0, tiled=True)  13.9 us
    all_to_all x1, starting transfers between devices, on_device(): lax.all_to_all(voltages, 'chan', split_axis=4, concat_axis=1, tiled=True)  13.5 us
    all_to_all x2, waiting for transfers between devices, gather_groups(): gathered = lax.all_to_all(outgoing, axis, 0, 0, tiled=True)  11.5 us
    unnamed x47, local copies, waits for them, and re-layouts  9.8 us
    dot_general x3, matrix products, on_device(): jnp.einsum('cq,cqp->cp', gain_re * gain_re + gain_im * gain_im, power, pr...  5.39 us
    all_to_all x1, waiting for transfers between devices, on_device(): incoming = lax.all_to_all(partial, 'row', 0, 0, tiled=True)  4.01 us
  transfers between devices with their start and end apart: 6, of which 5 were waited for; matrix products, arithmetic and copies ran while one was open for 11% of the time, Pallas kernels for 0%

profile of v4, /device:TPU:1, one launch (start us, length us, event | category | flops | bytes accessed | tf_op | source)
XLA Modules:
  0.0 140.7 jit_solution(15873685722402467581)
XLA Ops:
  0.0 0.8 copy.189
  0.8 0.7 reshape.464
  1.6 13.5 %all-to-all-start = ((bf16[32,2,128]{2,1,0:T(2,128)(2,1)}), bf16[32,2,128]{2,1,0:T(2,128)(2,1)S(1)}, u32[]{:S(2)}, u32[]{:S(2)}) async-start(bf16[32,2,128]{2,1,0:T(2,128)(2,1)} %reshape.464), calls=%async_computation | async-start | bytes 32768 | tf_op jit(solution)/shard_map/all_to_all | solution.py:50
  15.1 0.8 copy.195
  15.8 0.7 constant_dynamic-slice_fusion
  17.5 1.6 %fusion.3 = (bf16[4,192,64]{2,1,0:T(8,128)(2,1)S(1)}, bf16[4,192,64]{2,1,0:T(8,128)(2,1)S(1)}) fusion(f32[192,64]{1,0:T(8,128)S(1)} %multiply_add_fusion.1, f32[4]{0:T(128)S(1)} %add_multiply_fusion.2), kind=kLoop, calls=%fused_computation.15 | loop fusion | flops 196608 | bytes 245776 | tf_op jit(solution)/shard_map/convert_element_type | solution.py:25
  19.1 2.0 %fusion.47 = bf16[4,192,64]{2,1,0:T(8,128)(2,1)} fusion(f32[192,64]{1,0:T(8,128)S(1)} %multiply_add_fusion.1, f32[4]{0:T(128)S(1)} %add_multiply_fusion.2), kind=kLoop, calls=%fused_computation.109 | loop fusion | flops 245760 | bytes 147472 | tf_op jit(solution)/shard_map/neg | solution.py:96
  22.4 3.0 %multiply_convert_fusion.1 = (bf16[4,512,64]{1,2,0:T(8,128)(2,1)S(1)}, bf16[4,512,64]{1,2,0:T(8,128)(2,1)S(1)}) fusion(f32[512,64]{0,1:T(8,128)S(1)} %multiply_add_fusion, f32[4]{0:T(128)S(1)} %add_multiply_fusion.2, f32[4,64]{1,0:T(4,128)} %param.7), kind=kLoop, calls=%fused_computation.14 | loop fusion | flops 1310720 | bytes 656400 | tf_op jit(solution)/shard_map/convert_element_type | solution.py:93
  25.4 0.9 compare_select_fusion
  26.3 1.6 %fusion.7 = f32[4,192,512]{2,1,0:T(8,128)} fusion(bf16[4,512,64]{1,2,0:T(8,128)(2,1)S(1)} %get-tuple-element.13, bf16[4,512,64]{1,2,0:T(8,128)(2,1)S(1)} %get-tuple-element.12, bf16[4,192,64]{2,1,0:T(8,128)(2,1)S(1)} %get-tuple-element.15, bf16[4,192,64]{2,1,0:T(8,128)(2,1)S(1)} %get-tuple-element.14), kind=kOutput, calls=%fused_computation.20 | convolution fusion | flops 102105088 | bytes 2293760 | tf_op jit(solution)/shard_map/cqk,cpk->cqp/dot_general | solution.py:98
  29.5 1.0 copy.192
  31.4 0.9 reshape.466
  32.3 5.3 %all-to-all-start.2 = ((bf16[8,2,4096]{2,1,0:T(2,128)(2,1)}), bf16[8,2,4096]{2,1,0:T(2,128)(2,1)S(1)}, u32[]{:S(2)}, u32[]{:S(2)}) async-start(bf16[8,2,4096]{2,1,0:T(2,128)(2,1)} %reshape.466), calls=%async_computation.2 | async-start | bytes 262144 | tf_op jit(solution)/shard_map/all_to_all | solution.py:36
  37.5 5.2 %all-to-all-done.2 = bf16[8,2,4096]{2,1,0:T(2,128)(2,1)S(1)} async-done(((bf16[8,2,4096]{2,1,0:T(2,128)(2,1)}), bf16[8,2,4096]{2,1,0:T(2,128)(2,1)S(1)}, u32[]{:S(2)}, u32[]{:S(2)}) %all-to-all-start.2) | async-done | bytes 131104 | tf_op jit(solution)/shard_map/all_to_all | solution.py:36
  43.5 10.9 %all-to-all-start.1 = ((f32[3,1,8704]{2,1,0:T(1,128)}), f32[3,1,8704]{2,1,0:T(1,128)S(1)}, u32[]{:S(2)}, u32[]{:S(2)}) async-start(f32[3,1,8704]{2,1,0:T(1,128)} %broadcast_in_dim.25), calls=%async_computation.1 | async-start | bytes 208896 | tf_op jit(solution)/shard_map/all_to_all | solution.py:36
  55.1 6.3 %all-to-all-done.1 = f32[3,1,8704]{2,1,0:T(1,128)S(1)} async-done(((f32[3,1,8704]{2,1,0:T(1,128)}), f32[3,1,8704]{2,1,0:T(1,128)S(1)}, u32[]{:S(2)}, u32[]{:S(2)}) %all-to-all-start.1) | async-done | bytes 104480 | tf_op jit(solution)/shard_map/all_to_all | solution.py:36
  62.0 3.4 %reshape.401 = bf16[3,64,2,16,4]{4,3,2,1,0:T(8,128)(2,1)S(1)} reshape(bf16[3,8192]{1,0:T(4,128)(2,1)S(1)} %slice.177) | data formatting | bytes 98304 | tf_op jit(solution)/shard_map/reshape | solution.py:58
  65.7 1.3 copy.258
  67.0 0.8 negate_bitcast_fusion
  67.8 0.7 copy.257
  68.5 1.4 %copy.250 = bf16[4,192,32]{1,2,0:T(8,128)(2,1)S(1)} copy(bf16[4,192,32]{0,2,1:T(8,128)(2,1)S(1)} %bitcast.217) | data formatting | bytes 98304 | tf_op jit(solution)/shard_map/reshape;reshape | solution.py:64
  72.5 2.1 %subtract_multiply_fusion = (f32[4,192,512]{2,1,0:T(8,128)S(1)}, f32[4,192,512]{2,1,0:T(8,128)S(1)}, f32[4,192,512]{2,1,0:T(8,128)}) fusion(f32[4,192,512]{2,1,0:T(8,128)S(1)} %convolution_multiply_fusion.1, f32[4,192,512]{2,1,0:T(8,128)S(1)} %copy-done.1, f32[4,192,512]{2,1,0:T(8,128)S(1)} %convolution_multiply_fusion, f32[192,512]{1,0:T(8,128)S(1)} %copy-done.6, ...), kind=kOutput, calls=%fused_computation.1 | convolution fusion | flops 106823680 | bytes 10551296 | tf_op jit(solution)/shard_map/cqk,cpk->cqp/dot_general | solution.py:101
  74.6 0.9 fusion.52
  75.5 0.9 fusion.54
  76.3 0.9 fusion.53
  77.2 0.9 fusion.55
  78.4 2.3 %fusion.38 = f32[4,1,512]{2,1,0:T(1,128)S(1)} fusion(f32[4,192,512]{2,1,0:T(8,128)} %get-tuple-element.9, f32[4,192,1]{1,0,2:T(4,128)S(1)} %add_bitcast_fusion.2), kind=kOutput, calls=%fused_computation.81 | convolution fusion | flops 4718592 | bytes 1584128 | tf_op jit(solution)/shard_map/cq,cqp->cp/dot_general | solution.py:122
  80.8 0.8 reshape.468
  81.6 8.4 %all-to-all-start.3 = ((f32[24,1,768]{2,1,0:T(1,128)}), f32[24,1,768]{2,1,0:T(1,128)S(1)}, u32[]{:S(2)}, u32[]{:S(2)}) async-start(f32[24,1,768]{2,1,0:T(1,128)} %reshape.468), calls=%async_computation.3 | async-start | bytes 147456 | tf_op jit(solution)/shard_map/all_to_all | solution.py:143
  90.0 0.7 fusion.43
  90.7 9.2 %all-to-all-done.3 = f32[24,1,768]{2,1,0:T(1,128)S(1)} async-done(((f32[24,1,768]{2,1,0:T(1,128)}), f32[24,1,768]{2,1,0:T(1,128)S(1)}, u32[]{:S(2)}, u32[]{:S(2)}) %all-to-all-start.3) | async-done | bytes 73760 | tf_op jit(solution)/shard_map/all_to_all | solution.py:143
  100.4 0.8 reduce.12
  101.5 0.9 fusion.56
  102.4 0.9 fusion.58
  103.4 0.9 fusion.57
  104.2 0.9 fusion.59
  105.4 2.3 %fusion.36 = f32[4,1,512]{2,1,0:T(1,128)S(1)} fusion(f32[4,192,512]{2,1,0:T(8,128)} %get-tuple-element.9, f32[4,192,1]{1,0,2:T(4,128)S(1)} %add_bitcast_fusion.1), kind=kOutput, calls=%fused_computation.79 | convolution fusion | flops 4718592 | bytes 1584128 | tf_op jit(solution)/shard_map/cq,cqp->cp/dot_general | solution.py:122
  107.8 0.8 reshape.470
  108.6 5.5 %all-to-all-start.4 = ((f32[24,1,768]{2,1,0:T(1,128)}), f32[24,1,768]{2,1,0:T(1,128)S(1)}, u32[]{:S(2)}, u32[]{:S(2)}) async-start(f32[24,1,768]{2,1,0:T(1,128)} %reshape.470), calls=%async_computation.4 | async-start | bytes 147456 | tf_op jit(solution)/shard_map/all_to_all | solution.py:143
  114.1 9.9 %all-to-all-done.4 = f32[24,1,768]{2,1,0:T(1,128)S(1)} async-done(((f32[24,1,768]{2,1,0:T(1,128)}), f32[24,1,768]{2,1,0:T(1,128)S(1)}, u32[]{:S(2)}, u32[]{:S(2)}) %all-to-all-start.4) | async-done | bytes 73760 | tf_op jit(solution)/shard_map/all_to_all | solution.py:143
  124.0 0.8 reduce.13
  125.1 0.9 fusion.60
  126.0 0.9 fusion.62
  126.9 0.9 fusion.61
  127.8 0.9 fusion.63
  129.2 0.9 fusion.34
  130.8 3.7 %all-to-all-start.5 = ((f32[8,1,768]{2,1,0:T(1,128)}), f32[8,1,768]{2,1,0:T(1,128)S(1)}, u32[]{:S(2)}, u32[]{:S(2)}) async-start(f32[8,1,768]{2,1,0:T(1,128)} %reshape.472), calls=%async_computation.5 | async-start | bytes 49152 | tf_op jit(solution)/shard_map/all_to_all | solution.py:128
  135.2 4.0 %all-to-all-done.5 = f32[8,1,768]{2,1,0:T(1,128)S(1)} async-done(((f32[8,1,768]{2,1,0:T(1,128)}), f32[8,1,768]{2,1,0:T(1,128)S(1)}, u32[]{:S(2)}, u32[]{:S(2)}) %all-to-all-start.5) | async-done | bytes 24608 | tf_op jit(solution)/shard_map/all_to_all | solution.py:128
  (139 shorter events, 15.1 us)
Async XLA Ops:
  1.6 27.6 %all-to-all-start = ((bf16[32,2,128]{2,1,0:T(2,128)(2,1)}), bf16[32,2,128]{2,1,0:T(2,128)(2,1)S(1)}, u32[]{:S(2)}, u32[]{:S(2)}) async-start(bf16[32,2,128]{2,1,0:T(2,128)(2,1)} %reshape.464), calls=%async_computation | async-start | bytes 32768 | tf_op jit(solution)/shard_map/all_to_all | solution.py:50
  19.1 8.7 %copy-start.4 = (bf16[4,192,64]{2,1,0:T(8,128)(2,1)}, bf16[4,192,64]{2,1,0:T(8,128)(2,1)S(1)}, u32[]{:S(2)}) copy-start(bf16[4,192,64]{2,1,0:T(8,128)(2,1)S(1)} %get-tuple-element.15) | copy-start | bytes 294916
  25.4 0.9 copy-start.2
  25.4 3.0 %copy-start.14 = (f32[4,2,1,64]{3,2,1,0:T(1,128)S(1)}, f32[4,2,1,64]{3,2,1,0:T(1,128)}, u32[]{:S(2)}) copy-start(f32[4,2,1,64]{3,2,1,0:T(1,128)} %param.8) | copy-start | bytes 6148
  32.3 10.5 %all-to-all-start.2 = ((bf16[8,2,4096]{2,1,0:T(2,128)(2,1)}), bf16[8,2,4096]{2,1,0:T(2,128)(2,1)S(1)}, u32[]{:S(2)}, u32[]{:S(2)}) async-start(bf16[8,2,4096]{2,1,0:T(2,128)(2,1)} %reshape.466), calls=%async_computation.2 | async-start | bytes 262144 | tf_op jit(solution)/shard_map/all_to_all | solution.py:36
  43.5 17.8 %all-to-all-start.1 = ((f32[3,1,8704]{2,1,0:T(1,128)}), f32[3,1,8704]{2,1,0:T(1,128)S(1)}, u32[]{:S(2)}, u32[]{:S(2)}) async-start(f32[3,1,8704]{2,1,0:T(1,128)} %broadcast_in_dim.25), calls=%async_computation.1 | async-start | bytes 208896 | tf_op jit(solution)/shard_map/all_to_all | solution.py:36
  67.0 3.0 %copy-start.13 = (f32[3,512]{1,0:T(4,128)S(1)}, f32[3,512]{1,0:T(4,128)}, u32[]{:S(2)}) copy-start(f32[3,512]{1,0:T(4,128)} %slice.106) | copy-start | bytes 18436
  70.1 1.2 copy-start.8
  70.2 1.1 copy-start.10
  70.9 1.4 %copy-start.1 = (f32[4,192,512]{2,1,0:T(8,128)S(1)}, f32[4,192,512]{2,1,0:T(8,128)}, u32[]{:S(2)}) copy-start(f32[4,192,512]{2,1,0:T(8,128)} %fusion.7) | copy-start | bytes 4718596
  70.9 1.4 %copy-start.3 = (bf16[4,512,64]{1,2,0:T(8,128)(2,1)S(1)}, bf16[4,512,64]{1,2,0:T(8,128)(2,1)}, u32[]{:S(2)}) copy-start(bf16[4,512,64]{1,2,0:T(8,128)(2,1)} %copy-done.2) | copy-start | bytes 786436
  70.9 1.5 %copy-start.5 = (bf16[4,192,64]{2,1,0:T(8,128)(2,1)S(1)}, bf16[4,192,64]{2,1,0:T(8,128)(2,1)}, u32[]{:S(2)}) copy-start(bf16[4,192,64]{2,1,0:T(8,128)(2,1)} %copy-done.4) | copy-start | bytes 294916
  70.9 1.6 %copy-start.6 = (f32[192,512]{1,0:T(8,128)S(1)}, f32[192,512]{1,0:T(8,128)}, u32[]{:S(2)}) copy-start(f32[192,512]{1,0:T(8,128)} %compare_select_fusion) | copy-start | bytes 1179652
  70.9 1.6 %copy-start.7 = (bf16[4,192,64]{2,1,0:T(8,128)(2,1)S(1)}, bf16[4,192,64]{2,1,0:T(8,128)(2,1)}, u32[]{:S(2)}) copy-start(bf16[4,192,64]{2,1,0:T(8,128)(2,1)} %fusion.47) | copy-start | bytes 294916
  74.6 1.7 %copy-start.12 = (f32[4,192,1]{1,2,0:T(1,128)S(1)}, f32[4,192,1]{1,2,0:T(1,128)}, u32[]{:S(2)}) copy-start(f32[4,192,1]{1,2,0:T(1,128)} %reshape.436) | copy-start | bytes 9220
  76.3 1.7 %copy-start.9 = (f32[4,1,3,64]{3,2,0,1:T(4,128)S(1)}, f32[4,1,3,64]{3,2,0,1:T(4,128)}, u32[]{:S(2)}) copy-start(f32[4,1,3,64]{3,2,0,1:T(4,128)} %copy-done.8) | copy-start | bytes 9220
  76.3 1.8 %copy-start.11 = (f32[4,1,3,64]{3,2,0,1:T(4,128)S(1)}, f32[4,1,3,64]{3,2,0,1:T(4,128)}, u32[]{:S(2)}) copy-start(f32[4,1,3,64]{3,2,0,1:T(4,128)} %copy-done.10) | copy-start | bytes 9220
  81.6 18.3 %all-to-all-start.3 = ((f32[24,1,768]{2,1,0:T(1,128)}), f32[24,1,768]{2,1,0:T(1,128)S(1)}, u32[]{:S(2)}, u32[]{:S(2)}) async-start(f32[24,1,768]{2,1,0:T(1,128)} %reshape.468), calls=%async_computation.3 | async-start | bytes 147456 | tf_op jit(solution)/shard_map/all_to_all | solution.py:143
  108.6 15.4 %all-to-all-start.4 = ((f32[24,1,768]{2,1,0:T(1,128)}), f32[24,1,768]{2,1,0:T(1,128)S(1)}, u32[]{:S(2)}, u32[]{:S(2)}) async-start(f32[24,1,768]{2,1,0:T(1,128)} %reshape.470), calls=%async_computation.4 | async-start | bytes 147456 | tf_op jit(solution)/shard_map/all_to_all | solution.py:143
  127.8 1.4 %copy-start = (f32[4,192,512]{2,1,0:T(8,128)S(1)}, f32[4,192,512]{2,1,0:T(8,128)}, u32[]{:S(2)}) copy-start(f32[4,192,512]{2,1,0:T(8,128)} %get-tuple-element.9) | copy-start | bytes 4718596
  130.8 8.4 %all-to-all-start.5 = ((f32[8,1,768]{2,1,0:T(1,128)}), f32[8,1,768]{2,1,0:T(1,128)S(1)}, u32[]{:S(2)}, u32[]{:S(2)}) async-start(f32[8,1,768]{2,1,0:T(1,128)} %reshape.472), calls=%async_computation.5 | async-start | bytes 49152 | tf_op jit(solution)/shard_map/all_to_all | solution.py:128

commit v5 on v4

--- a/solution.py
+++ b/solution.py
@@ -49,13 +49,14 @@
     samples = voltages.shape[3]
     own_volt = lax.all_to_all(voltages, "chan", split_axis=4, concat_axis=1, tiled=True)
     volt_size = own_volt.size
-    row_both = gather_groups(
-        jnp.concatenate(
-            [own_volt.astype(jnp.float32).reshape(-1), initial_gains.reshape(-1)]
-        )[None],
-        "col",
-    )
-    row_volt = row_both[:, :volt_size].astype(jnp.bfloat16).reshape((n_cols,) + own_volt.shape[1:])
+    gains_flat = initial_gains.reshape(-1)
+    gains_hi = lax.reduce_precision(gains_flat, exponent_bits=8, mantissa_bits=7)
+    gains_rest = gains_flat - gains_hi
+    gains_mid = lax.reduce_precision(gains_rest, exponent_bits=8, mantissa_bits=7)
+    gains_lo = gains_rest - gains_mid
+    gains_parts = jnp.stack([gains_hi, gains_mid, gains_lo]).astype(jnp.bfloat16).reshape(-1)
+    row_both = gather_groups(jnp.concatenate([own_volt.reshape(-1), gains_parts])[None], "col")
+    row_volt = row_both[:, :volt_size].reshape((n_cols,) + own_volt.shape[1:])
     col_volt = gather_groups(own_volt, "row")
     row_antenna = antenna_major(row_volt)
     col_antenna = antenna_major(col_volt)
@@ -109,19 +110,17 @@
     power = keep * (model_re * model_re + model_im * model_im)
     highest = lax.Precision.HIGHEST
     row_flags = row_flag.reshape(1, 1, n_cols, subant)
-    row_gains = jnp.transpose(row_both[:, volt_size:].reshape(n_cols, per_chan, 2, subant), (1, 2, 0, 3))
+    parts = row_both[:, volt_size:].astype(jnp.float32).reshape(n_cols, 3, per_chan, 2, subant)
+    row_gains = jnp.transpose((parts[:, 0] + parts[:, 1]) + parts[:, 2], (1, 2, 0, 3))
+    stacked_data = jnp.concatenate([data_re, data_im, power], axis=2)
     for iteration in range(ITERS):
         gain_re = row_gains[:, 0].reshape(per_chan, row_count)
         gain_im = row_gains[:, 1].reshape(per_chan, row_count)
-        num_re = jnp.einsum("cq,cqp->cp", gain_re, data_re, precision=highest) + jnp.einsum(
-            "cq,cqp->cp", gain_im, data_im, precision=highest
-        )
-        num_im = jnp.einsum("cq,cqp->cp", gain_re, data_im, precision=highest) - jnp.einsum(
-            "cq,cqp->cp", gain_im, data_re, precision=highest
-        )
-        denominator = jnp.einsum(
-            "cq,cqp->cp", gain_re * gain_re + gain_im * gain_im, power, precision=highest
-        )
+        weights = jnp.stack([gain_re, gain_im, gain_re * gain_re + gain_im * gain_im], axis=1)
+        products = jnp.einsum("ckq,cqm->ckm", weights, stacked_data, precision=highest)
+        num_re = products[:, 0, :col_count] + products[:, 1, col_count : 2 * col_count]
+        num_im = products[:, 0, col_count : 2 * col_count] - products[:, 1, :col_count]
+        denominator = products[:, 2, 2 * col_count :]
         partial = jnp.stack([num_re, num_im, denominator], axis=0).reshape(3, per_chan, n_rows, subant)
         partial = jnp.transpose(partial, (2, 0, 1, 3))
         if iteration == ITERS - 1:

time: 142 us -> 139 us (0.979)
  matrix products: 20.1 us -> 12.9 us
  local copies, waits for them, and re-layouts: 23.7 us -> 28.6 us
  waiting for transfers between devices: 34.5 us -> 31.2 us
  other arithmetic: 14.6 us -> 17.8 us
    dot_general x15 -> x3, matrix products: 15.7 us -> 9.78 us  [on_device(): jnp.einsum('ckq,cqm->ckm', weights, stacked_data, precision=highest)]
    all_to_all x2, waiting for transfers between devices: 11.5 us -> 8.22 us  [gather_groups(): gathered = lax.all_to_all(outgoing, axis, 0, 0, tiled=True)]
    unnamed x47 -> x41, local copies, waits for them, and re-layouts: 9.8 us -> 12.6 us
    reshape x4, local copies, waits for them, and re-layouts: 3.59 us -> 6.01 us  [the longest x1 4.28 us: on_device(): row_volt = row_both[:, :volt_size].reshape((n_cols,) + own_volt.shape[1:])]
    convert_element_type x2 -> x1, local copies, waits for them, and re-layouts: 1.65 us -> 0.02 us  [on_device(): jnp.stack([gains_hi, gains_mid, gains_lo]).astype(jnp.bfloat16).reshape(-1)]
  transfers between devices with their start and end apart: 6 -> 6, of which waited for: 5 -> 5; matrix products, arithmetic and copies ran while one was open for 11% -> 14% of each run, Pallas kernels for 0% -> 0%
where the time goes in v5:
time: 139 us; the launch traced here: 138 us
  starting transfers between devices  46.9 us (34%)
  waiting for transfers between devices  31.2 us (22%)
  local copies, waits for them, and re-layouts  28.6 us (21%)
  other arithmetic  17.8 us (13%)
  matrix products  12.9 us (9%)
    all_to_all x2, waiting for transfers between devices, on_device(): incoming = lax.all_to_all(outgoing, ('row', 'col'), 0, 0, tiled=True)  19 us
    all_to_all x2, starting transfers between devices, gather_groups(): gathered = lax.all_to_all(outgoing, axis, 0, 0, tiled=True)  16.2 us
    all_to_all x2, starting transfers between devices, on_device(): incoming = lax.all_to_all(outgoing, ('row', 'col'), 0, 0, tiled=True)  13.6 us
    all_to_all x1, starting transfers between devices, on_device(): lax.all_to_all(voltages, 'chan', split_axis=4, concat_axis=1, tiled=True)  13.5 us
    unnamed x41, local copies, waits for them, and re-layouts  12.6 us
    dot_general x3, matrix products, on_device(): jnp.einsum('ckq,cqm->ckm', weights, stacked_data, precision=highest)  9.78 us
    all_to_all x2, waiting for transfers between devices, gather_groups(): gathered = lax.all_to_all(outgoing, axis, 0, 0, tiled=True)  8.22 us
    reshape x1, local copies, waits for them, and re-layouts, on_device(): row_volt = row_both[:, :volt_size].reshape((n_cols,) + own_volt.shape[1:])  4.28 us
  transfers between devices with their start and end apart: 6, of which 5 were waited for; matrix products, arithmetic and copies ran while one was open for 14% of the time, Pallas kernels for 0%

profile of v5, /device:TPU:1, one launch (start us, length us, event | category | flops | bytes accessed | tf_op | source)
XLA Modules:
  0.0 138.0 jit_solution(8733331212629188086)
XLA Ops:
  0.0 0.8 copy.229
  0.8 0.7 reshape.665
  1.6 13.5 %all-to-all-start = ((bf16[32,2,128]{2,1,0:T(2,128)(2,1)}), bf16[32,2,128]{2,1,0:T(2,128)(2,1)S(1)}, u32[]{:S(2)}, u32[]{:S(2)}) async-start(bf16[32,2,128]{2,1,0:T(2,128)(2,1)} %reshape.665), calls=%async_computation | async-start | bytes 32768 | tf_op jit(solution)/shard_map/all_to_all | solution.py:50
  15.0 0.7 convert_element_type.55
  15.7 0.8 copy.237
  16.5 0.7 constant_dynamic-slice_fusion
  17.6 1.6 %fusion.6 = (bf16[4,192,64]{2,1,0:T(8,128)(2,1)S(1)}, bf16[4,192,64]{2,1,0:T(8,128)(2,1)S(1)}) fusion(f32[192,64]{1,0:T(8,128)S(1)} %multiply_add_fusion.1, f32[4]{0:T(128)S(1)} %add_multiply_fusion.2), kind=kLoop, calls=%fused_computation.19 | loop fusion | flops 196608 | bytes 245776 | tf_op jit(solution)/shard_map/convert_element_type | solution.py:25
  19.2 2.0 %fusion.58 = bf16[4,192,64]{2,1,0:T(8,128)(2,1)} fusion(f32[192,64]{1,0:T(8,128)S(1)} %multiply_add_fusion.1, f32[4]{0:T(128)S(1)} %add_multiply_fusion.2), kind=kLoop, calls=%fused_computation.129 | loop fusion | flops 245760 | bytes 147472 | tf_op jit(solution)/shard_map/neg | solution.py:97
  21.7 1.4 reduce.29
  23.4 0.7 subtract_convert_fusion
  24.4 3.0 %multiply_convert_fusion.1 = (bf16[4,512,64]{1,2,0:T(8,128)(2,1)S(1)}, bf16[4,512,64]{1,2,0:T(8,128)(2,1)S(1)}) fusion(f32[512,64]{0,1:T(8,128)S(1)} %multiply_add_fusion, f32[4]{0:T(128)S(1)} %add_multiply_fusion.2, f32[4,64]{1,0:T(4,128)} %param.7), kind=kLoop, calls=%fused_computation.18 | loop fusion | flops 1310720 | bytes 656400 | tf_op jit(solution)/shard_map/convert_element_type | solution.py:94
  27.4 0.9 compare_select_fusion
  29.0 0.8 copy.231
  30.1 0.9 reshape.669
  30.9 5.3 %all-to-all-start.2 = ((bf16[8,2,4096]{2,1,0:T(2,128)(2,1)}), bf16[8,2,4096]{2,1,0:T(2,128)(2,1)S(1)}, u32[]{:S(2)}, u32[]{:S(2)}) async-start(bf16[8,2,4096]{2,1,0:T(2,128)(2,1)} %reshape.669), calls=%async_computation.2 | async-start | bytes 262144 | tf_op jit(solution)/shard_map/all_to_all | solution.py:36
  36.2 0.8 reshape.621
  37.6 1.0 reduce.30
  38.6 0.7 reshape.667
  39.3 2.1 %all-to-all-done.2 = bf16[8,2,4096]{2,1,0:T(2,128)(2,1)S(1)} async-done(((bf16[8,2,4096]{2,1,0:T(2,128)(2,1)}), bf16[8,2,4096]{2,1,0:T(2,128)(2,1)S(1)}, u32[]{:S(2)}, u32[]{:S(2)}) %all-to-all-start.2) | async-done | bytes 131104 | tf_op jit(solution)/shard_map/all_to_all | solution.py:36
  41.4 10.9 %all-to-all-start.1 = ((bf16[3,2,4864]{2,1,0:T(2,128)(2,1)}), bf16[3,2,4864]{2,1,0:T(2,128)(2,1)S(1)}, u32[]{:S(2)}, u32[]{:S(2)}) async-start(bf16[3,2,4864]{2,1,0:T(2,128)(2,1)} %reshape.667), calls=%async_computation.1 | async-start | bytes 116736 | tf_op jit(solution)/shard_map/all_to_all | solution.py:36
  53.0 6.1 %all-to-all-done.1 = bf16[3,2,4864]{2,1,0:T(2,128)(2,1)S(1)} async-done(((bf16[3,2,4864]{2,1,0:T(2,128)(2,1)}), bf16[3,2,4864]{2,1,0:T(2,128)(2,1)S(1)}, u32[]{:S(2)}, u32[]{:S(2)}) %all-to-all-start.1) | async-done | bytes 58400 | tf_op jit(solution)/shard_map/all_to_all | solution.py:36
  59.3 0.6 slice.183
  60.5 4.3 %reshape.627 = bf16[3,64,2,16,4]{4,3,2,1,0:T(8,128)(2,1)S(1)} reshape(bf16[3,8192]{1,0:T(4,128)(2,1)} %slice.183) | data formatting | bytes 98304 | tf_op jit(solution)/shard_map/reshape | solution.py:59
  64.8 1.4 %fusion.59 = (bf16[4,192,1,16]{0,3,2,1:T(8,128)(2,1)}, bf16[4,192,1,16]{0,3,2,1:T(8,128)(2,1)}) fusion(bf16[4,192,2,16]{0,3,2,1:T(8,128)(2,1)S(1)} %bitcast.135), kind=kLoop, calls=%fused_computation.130 | loop fusion | bytes 98304 | tf_op jit(solution)/shard_map/slice | solution.py:66
  66.2 2.5 %copy.281 = bf16[4,192,1,16]{1,3,0,2:T(8,128)(2,1)} copy(bf16[4,192,1,16]{0,3,2,1:T(8,128)(2,1)} %get-tuple-element.20) | data formatting | bytes 49152
  68.8 1.4 negate_bitcast_fusion
  70.1 2.5 %copy.280 = bf16[4,192,1,16]{1,3,0,2:T(8,128)(2,1)} copy(bf16[4,192,1,16]{0,3,2,1:T(8,128)(2,1)} %get-tuple-element.19) | data formatting | bytes 49152
  72.7 2.1 %copy.270 = bf16[4,192,32]{1,2,0:T(8,128)(2,1)} copy(bf16[4,192,32]{0,2,1:T(8,128)(2,1)S(1)} %bitcast.136) | data formatting | bytes 98304 | tf_op jit(solution)/shard_map/reshape;reshape | solution.py:65
  74.7 0.8 reshape.635
  75.9 1.3 convolution_multiply_fusion.1
  77.7 0.9 add_multiply_fusion.1
  78.6 2.3 %fusion.2 = f32[4,3,1536]{2,1,0:T(4,128)S(1)} fusion(f32[4,192,512]{2,1,0:T(8,128)S(1)} %get-tuple-element.18, f32[4,192,512]{2,1,0:T(8,128)S(1)} %get-tuple-element.17, f32[4,192,512]{2,1,0:T(8,128)S(1)} %get-tuple-element.16, f32[4,3,192]{2,0,1:T(4,128)S(1)} %pad_maximum_fusion.8), kind=kOutput, calls=%fused_computation.3 | convolution fusion | flops 44826624 | bytes 4801536 | tf_op jit(solution)/shard_map/ckq,cqm->ckm/dot_general | solution.py:120
  81.3 0.8 reshape.671
  82.1 7.7 %all-to-all-start.3 = ((f32[24,1,768]{2,1,0:T(1,128)}), f32[24,1,768]{2,1,0:T(1,128)S(1)}, u32[]{:S(2)}, u32[]{:S(2)}) async-start(f32[24,1,768]{2,1,0:T(1,128)} %reshape.671), calls=%async_computation.3 | async-start | bytes 147456 | tf_op jit(solution)/shard_map/all_to_all | solution.py:142
  89.8 0.7 fusion.51
  90.5 9.2 %all-to-all-done.3 = f32[24,1,768]{2,1,0:T(1,128)S(1)} async-done(((f32[24,1,768]{2,1,0:T(1,128)}), f32[24,1,768]{2,1,0:T(1,128)S(1)}, u32[]{:S(2)}, u32[]{:S(2)}) %all-to-all-start.3) | async-done | bytes 73760 | tf_op jit(solution)/shard_map/all_to_all | solution.py:142
  100.2 0.8 reduce.31
  101.4 3.7 %fusion.1 = f32[4,3,1536]{2,1,0:T(4,128)S(1)} fusion(f32[4,192,512]{2,1,0:T(8,128)} %copy-done.6, f32[4,192,512]{2,1,0:T(8,128)S(1)} %get-tuple-element.17, f32[4,192,512]{2,1,0:T(8,128)S(1)} %copy-done.5, f32[4,3,192]{2,0,1:T(4,128)S(1)} %pad_maximum_fusion.9), kind=kOutput, calls=%fused_computation.2 | convolution fusion | flops 44826624 | bytes 4801536 | tf_op jit(solution)/shard_map/ckq,cqm->ckm/dot_general | solution.py:120
  105.6 0.8 reshape.673
  106.3 5.9 %all-to-all-start.4 = ((f32[24,1,768]{2,1,0:T(1,128)}), f32[24,1,768]{2,1,0:T(1,128)S(1)}, u32[]{:S(2)}, u32[]{:S(2)}) async-start(f32[24,1,768]{2,1,0:T(1,128)} %reshape.673), calls=%async_computation.4 | async-start | bytes 147456 | tf_op jit(solution)/shard_map/all_to_all | solution.py:142
  112.2 9.9 %all-to-all-done.4 = f32[24,1,768]{2,1,0:T(1,128)S(1)} async-done(((f32[24,1,768]{2,1,0:T(1,128)}), f32[24,1,768]{2,1,0:T(1,128)S(1)}, u32[]{:S(2)}, u32[]{:S(2)}) %all-to-all-start.4) | async-done | bytes 73760 | tf_op jit(solution)/shard_map/all_to_all | solution.py:142
  122.1 0.8 reduce.32
  123.4 3.7 %fusion = f32[4,3,1536]{2,1,0:T(4,128)S(1)} fusion(f32[4,192,512]{2,1,0:T(8,128)} %copy-done.6, f32[4,192,512]{2,1,0:T(8,128)S(1)} %get-tuple-element.17, f32[4,192,512]{2,1,0:T(8,128)S(1)} %copy-done.5, f32[4,3,192]{2,0,1:T(4,128)S(1)} %pad_maximum_fusion.10), kind=kOutput, calls=%fused_computation.1 | convolution fusion | flops 44826624 | bytes 4801536 | tf_op jit(solution)/shard_map/ckq,cqm->ckm/dot_general | solution.py:120
  127.5 0.7 reshape.675
  128.2 3.7 %all-to-all-start.5 = ((f32[8,1,768]{2,1,0:T(1,128)}), f32[8,1,768]{2,1,0:T(1,128)S(1)}, u32[]{:S(2)}, u32[]{:S(2)}) async-start(f32[8,1,768]{2,1,0:T(1,128)} %reshape.675), calls=%async_computation.5 | async-start | bytes 49152 | tf_op jit(solution)/shard_map/all_to_all | solution.py:127
  131.9 0.7 compare_bitcast_fusion
  132.6 4.0 %all-to-all-done.5 = f32[8,1,768]{2,1,0:T(1,128)S(1)} async-done(((f32[8,1,768]{2,1,0:T(1,128)}), f32[8,1,768]{2,1,0:T(1,128)S(1)}, u32[]{:S(2)}, u32[]{:S(2)}) %all-to-all-start.5) | async-done | bytes 24608 | tf_op jit(solution)/shard_map/all_to_all | solution.py:127
  136.6 0.7 reduce.33
  (119 shorter events, 8.0 us)
Async XLA Ops:
  1.6 27.2 %all-to-all-start = ((bf16[32,2,128]{2,1,0:T(2,128)(2,1)}), bf16[32,2,128]{2,1,0:T(2,128)(2,1)S(1)}, u32[]{:S(2)}, u32[]{:S(2)}) async-start(bf16[32,2,128]{2,1,0:T(2,128)(2,1)} %reshape.665), calls=%async_computation | async-start | bytes 32768 | tf_op jit(solution)/shard_map/all_to_all | solution.py:50
  19.2 9.5 %copy-start.2 = (bf16[4,192,64]{2,1,0:T(8,128)(2,1)}, bf16[4,192,64]{2,1,0:T(8,128)(2,1)S(1)}, u32[]{:S(2)}) copy-start(bf16[4,192,64]{2,1,0:T(8,128)(2,1)S(1)} %get-tuple-element.24) | copy-start | bytes 294916
  27.4 1.5 %copy-start = (bf16[4,512,64]{1,2,0:T(8,128)(2,1)}, bf16[4,512,64]{1,2,0:T(8,128)(2,1)S(1)}, u32[]{:S(2)}) copy-start(bf16[4,512,64]{1,2,0:T(8,128)(2,1)S(1)} %get-tuple-element.22) | copy-start | bytes 786436
  30.9 10.5 %all-to-all-start.2 = ((bf16[8,2,4096]{2,1,0:T(2,128)(2,1)}), bf16[8,2,4096]{2,1,0:T(2,128)(2,1)S(1)}, u32[]{:S(2)}, u32[]{:S(2)}) async-start(bf16[8,2,4096]{2,1,0:T(2,128)(2,1)} %reshape.669), calls=%async_computation.2 | async-start | bytes 262144 | tf_op jit(solution)/shard_map/all_to_all | solution.py:36
  41.4 17.7 %all-to-all-start.1 = ((bf16[3,2,4864]{2,1,0:T(2,128)(2,1)}), bf16[3,2,4864]{2,1,0:T(2,128)(2,1)S(1)}, u32[]{:S(2)}, u32[]{:S(2)}) async-start(bf16[3,2,4864]{2,1,0:T(2,128)(2,1)} %reshape.667), calls=%async_computation.1 | async-start | bytes 116736 | tf_op jit(solution)/shard_map/all_to_all | solution.py:36
  74.7 2.5 %copy-start.9 = (bf16[4,192,1,16]{1,3,0,2:T(8,128)(2,1)S(1)}, bf16[4,192,1,16]{1,3,0,2:T(8,128)(2,1)}, u32[]{:S(2)}) copy-start(bf16[4,192,1,16]{1,3,0,2:T(8,128)(2,1)} %copy.280) | copy-start | bytes 73732
  74.7 2.5 %copy-start.10 = (bf16[4,192,16]{1,2,0:T(8,128)(2,1)S(1)}, bf16[4,192,16]{1,2,0:T(8,128)(2,1)}, u32[]{:S(2)}) copy-start(bf16[4,192,16]{1,2,0:T(8,128)(2,1)} %negate_bitcast_fusion) | copy-start | bytes 73732
  75.8 1.8 %copy-start.1 = (bf16[4,512,64]{1,2,0:T(8,128)(2,1)S(1)}, bf16[4,512,64]{1,2,0:T(8,128)(2,1)}, u32[]{:S(2)}) copy-start(bf16[4,512,64]{1,2,0:T(8,128)(2,1)} %copy-done) | copy-start | bytes 786436
  75.8 1.8 %copy-start.3 = (bf16[4,192,64]{2,1,0:T(8,128)(2,1)S(1)}, bf16[4,192,64]{2,1,0:T(8,128)(2,1)}, u32[]{:S(2)}) copy-start(bf16[4,192,64]{2,1,0:T(8,128)(2,1)} %copy-done.2) | copy-start | bytes 294916
  75.8 1.8 %copy-start.7 = (f32[192,512]{1,0:T(8,128)S(1)}, f32[192,512]{1,0:T(8,128)}, u32[]{:S(2)}) copy-start(f32[192,512]{1,0:T(8,128)} %compare_select_fusion) | copy-start | bytes 1179652
  75.8 1.8 %copy-start.8 = (bf16[4,192,64]{2,1,0:T(8,128)(2,1)S(1)}, bf16[4,192,64]{2,1,0:T(8,128)(2,1)}, u32[]{:S(2)}) copy-start(bf16[4,192,64]{2,1,0:T(8,128)(2,1)} %fusion.58) | copy-start | bytes 294916
  78.6 2.3 %copy-start.4 = (f32[4,192,512]{2,1,0:T(8,128)}, f32[4,192,512]{2,1,0:T(8,128)S(1)}, u32[]{:S(2)}) copy-start(f32[4,192,512]{2,1,0:T(8,128)S(1)} %get-tuple-element.16) | copy-start | bytes 4718596
  78.6 2.3 %copy-start.6 = (f32[4,192,512]{2,1,0:T(8,128)}, f32[4,192,512]{2,1,0:T(8,128)S(1)}, u32[]{:S(2)}) copy-start(f32[4,192,512]{2,1,0:T(8,128)S(1)} %get-tuple-element.18) | copy-start | bytes 4718596
  81.0 20.4 %copy-start.5 = (f32[4,192,512]{2,1,0:T(8,128)S(1)}, f32[4,192,512]{2,1,0:T(8,128)}, u32[]{:S(2)}) copy-start(f32[4,192,512]{2,1,0:T(8,128)} %copy-done.4) | copy-start | bytes 4718596
  82.1 17.5 %all-to-all-start.3 = ((f32[24,1,768]{2,1,0:T(1,128)}), f32[24,1,768]{2,1,0:T(1,128)S(1)}, u32[]{:S(2)}, u32[]{:S(2)}) async-start(f32[24,1,768]{2,1,0:T(1,128)} %reshape.671), calls=%async_computation.3 | async-start | bytes 147456 | tf_op jit(solution)/shard_map/all_to_all | solution.py:142
  106.3 15.8 %all-to-all-start.4 = ((f32[24,1,768]{2,1,0:T(1,128)}), f32[24,1,768]{2,1,0:T(1,128)S(1)}, u32[]{:S(2)}, u32[]{:S(2)}) async-start(f32[24,1,768]{2,1,0:T(1,128)} %reshape.673), calls=%async_computation.4 | async-start | bytes 147456 | tf_op jit(solution)/shard_map/all_to_all | solution.py:142
  128.2 8.4 %all-to-all-start.5 = ((f32[8,1,768]{2,1,0:T(1,128)}), f32[8,1,768]{2,1,0:T(1,128)S(1)}, u32[]{:S(2)}, u32[]{:S(2)}) async-start(f32[8,1,768]{2,1,0:T(1,128)} %reshape.675), calls=%async_computation.5 | async-start | bytes 49152 | tf_op jit(solution)/shard_map/all_to_all | solution.py:127

commit v6 on v5

--- a/solution.py
+++ b/solution.py
@@ -25,16 +25,10 @@
     return (jnp.cos(angle).astype(jnp.bfloat16), (-jnp.sin(angle)).astype(jnp.bfloat16))
 
 
-def antenna_major(block):
-    count, subant, halves, samples, chans = block.shape
-    return jnp.transpose(block, (4, 0, 1, 2, 3)).reshape(chans, count * subant, halves, samples)
-
-
 def gather_groups(block, axis):
     count = lax.axis_size(axis)
-    outgoing = jnp.broadcast_to(block[None], (count,) + block.shape)
-    gathered = lax.all_to_all(outgoing, axis, 0, 0, tiled=True)
-    return gathered.reshape((count * block.shape[0],) + block.shape[1:])
+    outgoing = jnp.broadcast_to(block[:, None, :], (block.shape[0], count, block.shape[1]))
+    return lax.all_to_all(outgoing, axis, 1, 1, tiled=True)
 
 
 def on_device(voltages, source_flux, initial_gains, antenna_positions, flagged, source_pixels):
@@ -47,24 +41,25 @@
     subant = antenna_positions.shape[2]
     per_chan = source_flux.shape[0]
     samples = voltages.shape[3]
-    own_volt = lax.all_to_all(voltages, "chan", split_axis=4, concat_axis=1, tiled=True)
-    volt_size = own_volt.size
-    gains_flat = initial_gains.reshape(-1)
+    count, own_ants, halves, _, all_chans = voltages.shape
+    width = halves * samples
+    local = jnp.transpose(voltages, (4, 0, 1, 2, 3)).reshape(all_chans, count * own_ants, width)
+    own_volt = lax.all_to_all(local, "chan", split_axis=0, concat_axis=1, tiled=True)
+    own_volt = own_volt.reshape(per_chan, subant * width)
+    volt_size = subant * width
+    gains_flat = initial_gains.reshape(per_chan, -1)
     gains_hi = lax.reduce_precision(gains_flat, exponent_bits=8, mantissa_bits=7)
     gains_rest = gains_flat - gains_hi
     gains_mid = lax.reduce_precision(gains_rest, exponent_bits=8, mantissa_bits=7)
     gains_lo = gains_rest - gains_mid
-    gains_parts = jnp.stack([gains_hi, gains_mid, gains_lo]).astype(jnp.bfloat16).reshape(-1)
-    row_both = gather_groups(jnp.concatenate([own_volt.reshape(-1), gains_parts])[None], "col")
-    row_volt = row_both[:, :volt_size].reshape((n_cols,) + own_volt.shape[1:])
-    col_volt = gather_groups(own_volt, "row")
-    row_antenna = antenna_major(row_volt)
-    col_antenna = antenna_major(col_volt)
-    row_count = row_antenna.shape[1]
-    col_count = col_antenna.shape[1]
-    row_left = row_antenna.reshape(per_chan, row_count, 2 * samples)
-    row_swap = jnp.concatenate([row_antenna[:, :, 1], -row_antenna[:, :, 0]], axis=2)
-    col_left = col_antenna.reshape(per_chan, col_count, 2 * samples)
+    gains_parts = jnp.stack([gains_hi, gains_mid, gains_lo], axis=1).astype(jnp.bfloat16)
+    gains_parts = gains_parts.reshape(per_chan, -1)
+    row_both = gather_groups(jnp.concatenate([own_volt, gains_parts], axis=1), "col")
+    row_count = n_cols * subant
+    col_count = n_rows * subant
+    row_left = row_both[:, :, :volt_size].reshape(per_chan, row_count, width)
+    col_left = gather_groups(own_volt, "row").reshape(per_chan, col_count, width)
+    row_swap = jnp.concatenate([row_left[:, :, samples:], -row_left[:, :, :samples]], axis=2)
     vis_re = (
         jnp.einsum("cqk,cpk->cqp", row_left, col_left, preferred_element_type=jnp.float32) / samples
     )
@@ -110,8 +105,8 @@
     power = keep * (model_re * model_re + model_im * model_im)
     highest = lax.Precision.HIGHEST
     row_flags = row_flag.reshape(1, 1, n_cols, subant)
-    parts = row_both[:, volt_size:].astype(jnp.float32).reshape(n_cols, 3, per_chan, 2, subant)
-    row_gains = jnp.transpose((parts[:, 0] + parts[:, 1]) + parts[:, 2], (1, 2, 0, 3))
+    parts = row_both[:, :, volt_size:].astype(jnp.float32).reshape(per_chan, n_cols, 3, 2, subant)
+    row_gains = jnp.transpose((parts[:, :, 0] + parts[:, :, 1]) + parts[:, :, 2], (0, 2, 1, 3))
     stacked_data = jnp.concatenate([data_re, data_im, power], axis=2)
     for iteration in range(ITERS):
         gain_re = row_gains[:, 0].reshape(per_chan, row_count)

time: 139 us -> 124 us (0.89)
  local copies, waits for them, and re-layouts: 28.6 us -> 14.9 us
  other arithmetic: 17.8 us -> 14.1 us
  waiting for transfers between devices: 31.2 us -> 34.1 us
    unnamed x41 -> x24, local copies, waits for them, and re-layouts: 12.6 us -> 7.21 us
    reshape x4 -> x6, local copies, waits for them, and re-layouts: 6.01 us -> 1.65 us  [the longest x1 0.83 us: on_device(): jnp.transpose(voltages, (4, 0, 1, 2, 3))]
    all_to_all x3, waiting for transfers between devices: 8.22 us -> 11.1 us  [the longest x2 11.1 us: gather_groups(): return lax.all_to_all(outgoing, axis, 1, 1, tiled=True)]
    another operation x2 -> x0, local copies, waits for them, and re-layouts: 2.29 us -> none  [the longest x1 2.08 us: on_device(): row_left = row_antenna.reshape(per_chan, row_count, 2 * samples)]
  transfers between devices with their start and end apart: 6 -> 6, of which waited for: 5 -> 5; matrix products, arithmetic and copies ran while one was open for 14% -> 12% of each run, Pallas kernels for 0% -> 0%
where the time goes in v6:
time: 124 us; the launch traced here: 123 us
  starting transfers between devices  47 us (38%)
  waiting for transfers between devices  34.1 us (28%)
  local copies, waits for them, and re-layouts  14.9 us (12%)
  other arithmetic  14.1 us (11%)
  matrix products  12.4 us (10%)
    all_to_all x2, waiting for transfers between devices, on_device(): incoming = lax.all_to_all(outgoing, ('row', 'col'), 0, 0, tiled=True)  19 us
    all_to_all x2, starting transfers between devices, gather_groups(): return lax.all_to_all(outgoing, axis, 1, 1, tiled=True)  16.2 us
    all_to_all x2, starting transfers between devices, on_device(): incoming = lax.all_to_all(outgoing, ('row', 'col'), 0, 0, tiled=True)  13.6 us
    all_to_all x1, starting transfers between devices, on_device(): lax.all_to_all(local, 'chan', split_axis=0, concat_axis=1, tiled=True)  13.5 us
    all_to_all x2, waiting for transfers between devices, gather_groups(): return lax.all_to_all(outgoing, axis, 1, 1, tiled=True)  11.1 us
    dot_general x3, matrix products, on_device(): jnp.einsum('ckq,cqm->ckm', weights, stacked_data, precision=highest)  10.3 us
    unnamed x24, local copies, waits for them, and re-layouts  7.21 us
    all_to_all x1, waiting for transfers between devices, on_device(): incoming = lax.all_to_all(partial, 'row', 0, 0, tiled=True)  4.01 us
  transfers between devices with their start and end apart: 6, of which 5 were waited for; matrix products, arithmetic and copies ran while one was open for 12% of the time, Pallas kernels for 0%

profile of v6, /device:TPU:1, one launch (start us, length us, event | category | flops | bytes accessed | tf_op | source)
XLA Modules:
  0.0 123.0 jit_solution(7707644777568564339)
XLA Ops:
  0.0 0.8 copy.230
  0.8 0.7 reshape.656
  1.5 13.5 %all-to-all-start = ((bf16[32,2,128]{2,1,0:T(2,128)(2,1)}), bf16[32,2,128]{2,1,0:T(2,128)(2,1)S(1)}, u32[]{:S(2)}, u32[]{:S(2)}) async-start(bf16[32,2,128]{2,1,0:T(2,128)(2,1)} %reshape.656), calls=%async_computation | async-start | bytes 32768 | tf_op jit(solution)/shard_map/all_to_all | solution.py:47
  15.1 0.7 convert_element_type.55
  15.8 0.8 copy.238
  16.5 0.7 constant_dynamic-slice_fusion
  17.5 2.0 %fusion.58 = bf16[4,192,64]{2,1,0:T(8,128)(2,1)} fusion(f32[192,64]{1,0:T(8,128)S(1)} %multiply_add_fusion.1, f32[4]{0:T(128)S(1)} %add_multiply_fusion.2), kind=kLoop, calls=%fused_computation.127 | loop fusion | flops 245760 | bytes 147472 | tf_op jit(solution)/shard_map/neg | solution.py:92
  19.6 1.6 %fusion.6 = (bf16[4,192,64]{2,1,0:T(8,128)(2,1)S(1)}, bf16[4,192,64]{2,1,0:T(8,128)(2,1)S(1)}) fusion(f32[192,64]{1,0:T(8,128)S(1)} %multiply_add_fusion.1, f32[4]{0:T(128)S(1)} %add_multiply_fusion.2), kind=kLoop, calls=%fused_computation.19 | loop fusion | flops 196608 | bytes 245776 | tf_op jit(solution)/shard_map/convert_element_type | solution.py:25
  21.2 0.7 subtract_convert_fusion
  22.0 0.5 broadcast.315
  22.5 1.4 %reduce.29 = f32[4,2,64]{2,1,0:T(2,128)S(1)} reduce(f32[4,2,1,64]{3,2,1,0:T(1,128)} %param.8, f32[]{:T(128)} %broadcast.315), dimensions={2}, to_apply=%param.8.reduce_sub_computation.3 | reduce | bytes 4100 | tf_op args[2]
  24.3 3.0 %multiply_convert_fusion.1 = (bf16[4,512,64]{1,2,0:T(8,128)(2,1)S(1)}, bf16[4,512,64]{1,2,0:T(8,128)(2,1)S(1)}) fusion(f32[512,64]{0,1:T(8,128)S(1)} %multiply_add_fusion, f32[4]{0:T(128)S(1)} %add_multiply_fusion.2, f32[4,64]{1,0:T(4,128)} %param.7), kind=kLoop, calls=%fused_computation.18 | loop fusion | flops 1310720 | bytes 656400 | tf_op jit(solution)/shard_map/convert_element_type | solution.py:89
  27.7 0.1 reshape.614
  27.8 0.7 broadcast_in_dim.24
  28.5 5.3 %all-to-all-start.2 = ((bf16[4,8,2048]{2,0,1:T(4,128)(2,1)}), bf16[4,8,2048]{2,0,1:T(4,128)(2,1)S(1)}, u32[]{:S(2)}, u32[]{:S(2)}) async-start(bf16[4,8,2048]{2,0,1:T(4,128)(2,1)} %broadcast_in_dim.24), calls=%async_computation.2 | async-start | bytes 262144 | tf_op jit(solution)/shard_map/all_to_all | solution.py:31
  33.7 5.2 %all-to-all-done.2 = bf16[4,8,2048]{2,0,1:T(4,128)(2,1)S(1)} async-done(((bf16[4,8,2048]{2,0,1:T(4,128)(2,1)}), bf16[4,8,2048]{2,0,1:T(4,128)(2,1)S(1)}, u32[]{:S(2)}, u32[]{:S(2)}) %all-to-all-start.2) | async-done | bytes 131104 | tf_op jit(solution)/shard_map/all_to_all | solution.py:31
  39.0 0.6 broadcast_in_dim.23
  39.6 10.9 %all-to-all-start.1 = ((bf16[4,3,2432]{2,0,1:T(4,128)(2,1)}), bf16[4,3,2432]{2,0,1:T(4,128)(2,1)S(1)}, u32[]{:S(2)}, u32[]{:S(2)}) async-start(bf16[4,3,2432]{2,0,1:T(4,128)(2,1)} %broadcast_in_dim.23), calls=%async_computation.1 | async-start | bytes 116736 | tf_op jit(solution)/shard_map/all_to_all | solution.py:31
  50.5 0.4 fusion.10
  51.0 0.4 reshape.620
  51.4 5.9 %all-to-all-done.1 = bf16[4,3,2432]{2,0,1:T(4,128)(2,1)S(1)} async-done(((bf16[4,3,2432]{2,0,1:T(4,128)(2,1)}), bf16[4,3,2432]{2,0,1:T(4,128)(2,1)S(1)}, u32[]{:S(2)}, u32[]{:S(2)}) %all-to-all-start.1) | async-done | bytes 58400 | tf_op jit(solution)/shard_map/all_to_all | solution.py:31
  57.7 0.1 reshape.619
  57.9 0.8 fusion.59
  58.7 1.0 copy.279
  59.7 1.0 copy.280
  60.8 0.4 convolution_multiply_fusion.1
  61.2 0.4 convolution_multiply_fusion
  61.6 0.5 copy-done.5
  62.1 0.9 add_multiply_fusion.1
  63.0 2.3 %fusion.2 = f32[4,3,1536]{2,1,0:T(4,128)S(1)} fusion(f32[4,192,512]{2,1,0:T(8,128)S(1)} %get-tuple-element.18, f32[4,192,512]{2,1,0:T(8,128)S(1)} %get-tuple-element.17, f32[4,192,512]{2,1,0:T(8,128)S(1)} %get-tuple-element.16, f32[4,3,192]{2,0,1:T(4,128)S(1)} %pad_maximum_fusion.8), kind=kOutput, calls=%fused_computation.3 | convolution fusion | flops 44826624 | bytes 4801536 | tf_op jit(solution)/shard_map/ckq,cqm->ckm/dot_general | solution.py:115
  65.7 0.8 reshape.658
  66.5 7.7 %all-to-all-start.3 = ((f32[24,1,768]{2,1,0:T(1,128)}), f32[24,1,768]{2,1,0:T(1,128)S(1)}, u32[]{:S(2)}, u32[]{:S(2)}) async-start(f32[24,1,768]{2,1,0:T(1,128)} %reshape.658), calls=%async_computation.3 | async-start | bytes 147456 | tf_op jit(solution)/shard_map/all_to_all | solution.py:137
  74.2 0.7 fusion.51
  74.9 9.2 %all-to-all-done.3 = f32[24,1,768]{2,1,0:T(1,128)S(1)} async-done(((f32[24,1,768]{2,1,0:T(1,128)}), f32[24,1,768]{2,1,0:T(1,128)S(1)}, u32[]{:S(2)}, u32[]{:S(2)}) %all-to-all-start.3) | async-done | bytes 73760 | tf_op jit(solution)/shard_map/all_to_all | solution.py:137
  84.1 0.5 broadcast.318
  84.6 0.8 reduce.30
  85.9 4.2 %fusion.1 = f32[4,3,1536]{2,1,0:T(4,128)S(1)} fusion(f32[4,192,512]{2,1,0:T(8,128)} %copy-done.4, f32[4,192,512]{2,1,0:T(8,128)} %copy-done.2, f32[4,192,512]{2,1,0:T(8,128)S(1)} %copy-done.1, f32[4,3,192]{2,0,1:T(4,128)S(1)} %pad_maximum_fusion.9), kind=kOutput, calls=%fused_computation.2 | convolution fusion | flops 44826624 | bytes 4801536 | tf_op jit(solution)/shard_map/ckq,cqm->ckm/dot_general | solution.py:115
  90.4 0.8 reshape.660
  91.2 5.9 %all-to-all-start.4 = ((f32[24,1,768]{2,1,0:T(1,128)}), f32[24,1,768]{2,1,0:T(1,128)S(1)}, u32[]{:S(2)}, u32[]{:S(2)}) async-start(f32[24,1,768]{2,1,0:T(1,128)} %reshape.660), calls=%async_computation.4 | async-start | bytes 147456 | tf_op jit(solution)/shard_map/all_to_all | solution.py:137
  97.2 9.9 %all-to-all-done.4 = f32[24,1,768]{2,1,0:T(1,128)S(1)} async-done(((f32[24,1,768]{2,1,0:T(1,128)}), f32[24,1,768]{2,1,0:T(1,128)S(1)}, u32[]{:S(2)}, u32[]{:S(2)}) %all-to-all-start.4) | async-done | bytes 73760 | tf_op jit(solution)/shard_map/all_to_all | solution.py:137
  107.0 0.8 reduce.31
  108.3 3.7 %fusion = f32[4,3,1536]{2,1,0:T(4,128)S(1)} fusion(f32[4,192,512]{2,1,0:T(8,128)} %copy-done.4, f32[4,192,512]{2,1,0:T(8,128)S(1)} %copy-done.3, f32[4,192,512]{2,1,0:T(8,128)S(1)} %copy-done.1, f32[4,3,192]{2,0,1:T(4,128)S(1)} %pad_maximum_fusion.10), kind=kOutput, calls=%fused_computation.1 | convolution fusion | flops 44826624 | bytes 4801536 | tf_op jit(solution)/shard_map/ckq,cqm->ckm/dot_general | solution.py:115
  112.4 0.7 reshape.662
  113.1 3.7 %all-to-all-start.5 = ((f32[8,1,768]{2,1,0:T(1,128)}), f32[8,1,768]{2,1,0:T(1,128)S(1)}, u32[]{:S(2)}, u32[]{:S(2)}) async-start(f32[8,1,768]{2,1,0:T(1,128)} %reshape.662), calls=%async_computation.5 | async-start | bytes 49152 | tf_op jit(solution)/shard_map/all_to_all | solution.py:122
  116.8 0.7 compare_bitcast_fusion
  117.5 4.0 %all-to-all-done.5 = f32[8,1,768]{2,1,0:T(1,128)S(1)} async-done(((f32[8,1,768]{2,1,0:T(1,128)}), f32[8,1,768]{2,1,0:T(1,128)S(1)}, u32[]{:S(2)}, u32[]{:S(2)}) %all-to-all-start.5) | async-done | bytes 24608 | tf_op jit(solution)/shard_map/all_to_all | solution.py:122
  121.5 0.7 reduce.32
  122.4 0.6 copy.268
  (98 shorter events, 3.7 us)
Async XLA Ops:
  1.5 25.9 %all-to-all-start = ((bf16[32,2,128]{2,1,0:T(2,128)(2,1)}), bf16[32,2,128]{2,1,0:T(2,128)(2,1)S(1)}, u32[]{:S(2)}, u32[]{:S(2)}) async-start(bf16[32,2,128]{2,1,0:T(2,128)(2,1)} %reshape.656), calls=%async_computation | async-start | bytes 32768 | tf_op jit(solution)/shard_map/all_to_all | solution.py:47
  28.5 10.5 %all-to-all-start.2 = ((bf16[4,8,2048]{2,0,1:T(4,128)(2,1)}), bf16[4,8,2048]{2,0,1:T(4,128)(2,1)S(1)}, u32[]{:S(2)}, u32[]{:S(2)}) async-start(bf16[4,8,2048]{2,0,1:T(4,128)(2,1)} %broadcast_in_dim.24), calls=%async_computation.2 | async-start | bytes 262144 | tf_op jit(solution)/shard_map/all_to_all | solution.py:31
  39.6 17.7 %all-to-all-start.1 = ((bf16[4,3,2432]{2,0,1:T(4,128)(2,1)}), bf16[4,3,2432]{2,0,1:T(4,128)(2,1)S(1)}, u32[]{:S(2)}, u32[]{:S(2)}) async-start(bf16[4,3,2432]{2,0,1:T(4,128)(2,1)} %broadcast_in_dim.23), calls=%async_computation.1 | async-start | bytes 116736 | tf_op jit(solution)/shard_map/all_to_all | solution.py:31
  61.1 0.9 copy-start.5
  63.0 2.4 %copy-start = (f32[4,192,512]{2,1,0:T(8,128)}, f32[4,192,512]{2,1,0:T(8,128)S(1)}, u32[]{:S(2)}) copy-start(f32[4,192,512]{2,1,0:T(8,128)S(1)} %get-tuple-element.16) | copy-start | bytes 4718596
  63.0 2.4 %copy-start.2 = (f32[4,192,512]{2,1,0:T(8,128)}, f32[4,192,512]{2,1,0:T(8,128)S(1)}, u32[]{:S(2)}) copy-start(f32[4,192,512]{2,1,0:T(8,128)S(1)} %get-tuple-element.17) | copy-start | bytes 4718596
  63.0 2.3 %copy-start.4 = (f32[4,192,512]{2,1,0:T(8,128)}, f32[4,192,512]{2,1,0:T(8,128)S(1)}, u32[]{:S(2)}) copy-start(f32[4,192,512]{2,1,0:T(8,128)S(1)} %get-tuple-element.18) | copy-start | bytes 4718596
  65.4 20.4 %copy-start.1 = (f32[4,192,512]{2,1,0:T(8,128)S(1)}, f32[4,192,512]{2,1,0:T(8,128)}, u32[]{:S(2)}) copy-start(f32[4,192,512]{2,1,0:T(8,128)} %copy-done) | copy-start | bytes 4718596
  66.5 17.6 %all-to-all-start.3 = ((f32[24,1,768]{2,1,0:T(1,128)}), f32[24,1,768]{2,1,0:T(1,128)S(1)}, u32[]{:S(2)}, u32[]{:S(2)}) async-start(f32[24,1,768]{2,1,0:T(1,128)} %reshape.658), calls=%async_computation.3 | async-start | bytes 147456 | tf_op jit(solution)/shard_map/all_to_all | solution.py:137
  90.1 18.2 %copy-start.3 = (f32[4,192,512]{2,1,0:T(8,128)S(1)}, f32[4,192,512]{2,1,0:T(8,128)}, u32[]{:S(2)}) copy-start(f32[4,192,512]{2,1,0:T(8,128)} %copy-done.2) | copy-start | bytes 4718596
  91.2 15.8 %all-to-all-start.4 = ((f32[24,1,768]{2,1,0:T(1,128)}), f32[24,1,768]{2,1,0:T(1,128)S(1)}, u32[]{:S(2)}, u32[]{:S(2)}) async-start(f32[24,1,768]{2,1,0:T(1,128)} %reshape.660), calls=%async_computation.4 | async-start | bytes 147456 | tf_op jit(solution)/shard_map/all_to_all | solution.py:137
  113.1 8.4 %all-to-all-start.5 = ((f32[8,1,768]{2,1,0:T(1,128)}), f32[8,1,768]{2,1,0:T(1,128)S(1)}, u32[]{:S(2)}, u32[]{:S(2)}) async-start(f32[8,1,768]{2,1,0:T(1,128)} %reshape.662), calls=%async_computation.5 | async-start | bytes 49152 | tf_op jit(solution)/shard_map/all_to_all | solution.py:122

commit v7 on v6

--- a/solution.py
+++ b/solution.py
@@ -103,19 +103,17 @@
     data_re = keep * (model_re * vis_re + model_im * vis_im)
     data_im = keep * (model_re * vis_im - model_im * vis_re)
     power = keep * (model_re * model_re + model_im * model_im)
-    highest = lax.Precision.HIGHEST
     row_flags = row_flag.reshape(1, 1, n_cols, subant)
     parts = row_both[:, :, volt_size:].astype(jnp.float32).reshape(per_chan, n_cols, 3, 2, subant)
     row_gains = jnp.transpose((parts[:, :, 0] + parts[:, :, 1]) + parts[:, :, 2], (0, 2, 1, 3))
-    stacked_data = jnp.concatenate([data_re, data_im, power], axis=2)
     for iteration in range(ITERS):
         gain_re = row_gains[:, 0].reshape(per_chan, row_count)
         gain_im = row_gains[:, 1].reshape(per_chan, row_count)
-        weights = jnp.stack([gain_re, gain_im, gain_re * gain_re + gain_im * gain_im], axis=1)
-        products = jnp.einsum("ckq,cqm->ckm", weights, stacked_data, precision=highest)
-        num_re = products[:, 0, :col_count] + products[:, 1, col_count : 2 * col_count]
-        num_im = products[:, 0, col_count : 2 * col_count] - products[:, 1, :col_count]
-        denominator = products[:, 2, 2 * col_count :]
+        weight_re = gain_re[:, :, None]
+        weight_im = gain_im[:, :, None]
+        num_re = jnp.sum(weight_re * data_re + weight_im * data_im, axis=1)
+        num_im = jnp.sum(weight_re * data_im - weight_im * data_re, axis=1)
+        denominator = jnp.sum((weight_re * weight_re + weight_im * weight_im) * power, axis=1)
         partial = jnp.stack([num_re, num_im, denominator], axis=0).reshape(3, per_chan, n_rows, subant)
         partial = jnp.transpose(partial, (2, 0, 1, 3))
         if iteration == ITERS - 1:

time: 124 us -> 118 us (0.952)
  matrix products: 12.4 us -> 4.89 us
  other arithmetic: 14.1 us -> 18.8 us
  local copies, waits for them, and re-layouts: 14.9 us -> 12.9 us
    dot_general x3 -> x0, matrix products: 10.3 us -> none  [on_device(): jnp.einsum('ckq,cqm->ckm', weights, stacked_data, precision=highest)]
    reduce_sum x0 -> x3, other arithmetic: none -> 4.27 us  [the longest x2 2.67 us: on_device(): num_re = jnp.sum(weight_re * data_re + weight_im * data_im, axis=1)]
    dot_general x1, matrix products: 0.9 us -> 2.53 us  [on_device(): jnp.einsum('cqk,cpk->cqp', steer_swap, weight_both, preferred_element_typ...]
    unnamed x24 -> x26, local copies, waits for them, and re-layouts: 7.21 us -> 5.92 us
  transfers between devices with their start and end apart: 6 -> 6, of which waited for: 5 -> 5; matrix products, arithmetic and copies ran while one was open for 12% -> 14% of each run, Pallas kernels for 0% -> 0%
where the time goes in v7:
time: 118 us; the launch traced here: 117 us
  starting transfers between devices  47 us (40%)
  waiting for transfers between devices  33 us (28%)
  other arithmetic  18.8 us (16%)
  local copies, waits for them, and re-layouts  12.9 us (11%)
  matrix products  4.89 us (4%)
    all_to_all x2, waiting for transfers between devices, on_device(): incoming = lax.all_to_all(outgoing, ('row', 'col'), 0, 0, tiled=True)  19 us
    all_to_all x2, starting transfers between devices, gather_groups(): return lax.all_to_all(outgoing, axis, 1, 1, tiled=True)  16.2 us
    all_to_all x2, starting transfers between devices, on_device(): incoming = lax.all_to_all(outgoing, ('row', 'col'), 0, 0, tiled=True)  13.6 us
    all_to_all x1, starting transfers between devices, on_device(): lax.all_to_all(local, 'chan', split_axis=0, concat_axis=1, tiled=True)  13.5 us
    all_to_all x2, waiting for transfers between devices, gather_groups(): return lax.all_to_all(outgoing, axis, 1, 1, tiled=True)  9.93 us
    unnamed x26, local copies, waits for them, and re-layouts  5.92 us
    all_to_all x1, waiting for transfers between devices, on_device(): incoming = lax.all_to_all(partial, 'row', 0, 0, tiled=True)  4.01 us
    all_to_all x1, starting transfers between devices, on_device(): incoming = lax.all_to_all(partial, 'row', 0, 0, tiled=True)  3.68 us
  transfers between devices with their start and end apart: 6, of which 5 were waited for; matrix products, arithmetic and copies ran while one was open for 14% of the time, Pallas kernels for 0%

profile of v7, /device:TPU:1, one launch (start us, length us, event | category | flops | bytes accessed | tf_op | source)
XLA Modules:
  0.0 117.1 jit_solution(7161932631963733977)
XLA Ops:
  0.0 0.8 copy.196
  0.8 0.7 reshape.518
  1.5 13.5 %all-to-all-start = ((bf16[32,2,128]{2,1,0:T(2,128)(2,1)}), bf16[32,2,128]{2,1,0:T(2,128)(2,1)S(1)}, u32[]{:S(2)}, u32[]{:S(2)}) async-start(bf16[32,2,128]{2,1,0:T(2,128)(2,1)} %reshape.518), calls=%async_computation | async-start | bytes 32768 | tf_op jit(solution)/shard_map/all_to_all | solution.py:47
  15.1 0.7 convert_element_type.55
  15.7 0.8 copy.203
  16.5 0.7 constant_dynamic-slice_fusion
  17.5 2.0 %fusion.43 = bf16[4,192,64]{2,1,0:T(8,128)(2,1)} fusion(f32[192,64]{1,0:T(8,128)S(1)} %multiply_add_fusion.1, f32[4]{0:T(128)S(1)} %add_multiply_fusion.2), kind=kLoop, calls=%fused_computation.108 | loop fusion | flops 245760 | bytes 147472 | tf_op jit(solution)/shard_map/neg | solution.py:92
  19.6 1.6 %fusion.3 = (bf16[4,192,64]{2,1,0:T(8,128)(2,1)S(1)}, bf16[4,192,64]{2,1,0:T(8,128)(2,1)S(1)}) fusion(f32[192,64]{1,0:T(8,128)S(1)} %multiply_add_fusion.1, f32[4]{0:T(128)S(1)} %add_multiply_fusion.2), kind=kLoop, calls=%fused_computation.24 | loop fusion | flops 196608 | bytes 245776 | tf_op jit(solution)/shard_map/convert_element_type | solution.py:25
  21.2 0.7 subtract_convert_fusion
  22.0 0.5 broadcast.306
  22.5 1.4 %reduce.11 = f32[4,2,64]{2,1,0:T(2,128)S(1)} reduce(f32[4,2,1,64]{3,2,1,0:T(1,128)} %param.8, f32[]{:T(128)} %broadcast.306), dimensions={2}, to_apply=%param.8.reduce_sub_computation.3 | reduce | bytes 4100 | tf_op args[2]
  24.4 3.0 %multiply_convert_fusion.1 = (bf16[4,512,64]{1,2,0:T(8,128)(2,1)S(1)}, bf16[4,512,64]{1,2,0:T(8,128)(2,1)S(1)}) fusion(f32[512,64]{0,1:T(8,128)S(1)} %multiply_add_fusion, f32[4]{0:T(128)S(1)} %add_multiply_fusion.2, f32[4,64]{1,0:T(4,128)} %param.7), kind=kLoop, calls=%fused_computation.23 | loop fusion | flops 1310720 | bytes 656400 | tf_op jit(solution)/shard_map/convert_element_type | solution.py:89
  27.4 0.9 compare_select_fusion
  28.5 0.1 reshape.485
  28.6 0.7 broadcast_in_dim.24
  29.3 5.3 %all-to-all-start.2 = ((bf16[4,8,2048]{2,0,1:T(4,128)(2,1)}), bf16[4,8,2048]{2,0,1:T(4,128)(2,1)S(1)}, u32[]{:S(2)}, u32[]{:S(2)}) async-start(bf16[4,8,2048]{2,0,1:T(4,128)(2,1)} %broadcast_in_dim.24), calls=%async_computation.2 | async-start | bytes 262144 | tf_op jit(solution)/shard_map/all_to_all | solution.py:31
  34.5 5.2 %all-to-all-done.2 = bf16[4,8,2048]{2,0,1:T(4,128)(2,1)S(1)} async-done(((bf16[4,8,2048]{2,0,1:T(4,128)(2,1)}), bf16[4,8,2048]{2,0,1:T(4,128)(2,1)S(1)}, u32[]{:S(2)}, u32[]{:S(2)}) %all-to-all-start.2) | async-done | bytes 131104 | tf_op jit(solution)/shard_map/all_to_all | solution.py:31
  39.8 0.6 broadcast_in_dim.23
  40.4 10.9 %all-to-all-start.1 = ((bf16[4,3,2432]{2,0,1:T(4,128)(2,1)}), bf16[4,3,2432]{2,0,1:T(4,128)(2,1)S(1)}, u32[]{:S(2)}, u32[]{:S(2)}) async-start(bf16[4,3,2432]{2,0,1:T(4,128)(2,1)} %broadcast_in_dim.23), calls=%async_computation.1 | async-start | bytes 116736 | tf_op jit(solution)/shard_map/all_to_all | solution.py:31
  51.3 1.6 %fusion.7 = f32[4,192,512]{2,1,0:T(8,128)} fusion(bf16[4,512,64]{1,2,0:T(8,128)(2,1)S(1)} %get-tuple-element.22, bf16[4,512,64]{1,2,0:T(8,128)(2,1)S(1)} %get-tuple-element.21, bf16[4,192,64]{2,1,0:T(8,128)(2,1)S(1)} %get-tuple-element.24, bf16[4,192,64]{2,1,0:T(8,128)(2,1)S(1)} %get-tuple-element.23), kind=kOutput, calls=%fused_computation.29 | convolution fusion | flops 102105088 | bytes 2293760 | tf_op jit(solution)/shard_map/cqk,cpk->cqp/dot_general | solution.py:94
  53.0 0.4 reshape.491
  53.4 4.7 %all-to-all-done.1 = bf16[4,3,2432]{2,0,1:T(4,128)(2,1)S(1)} async-done(((bf16[4,3,2432]{2,0,1:T(4,128)(2,1)}), bf16[4,3,2432]{2,0,1:T(4,128)(2,1)S(1)}, u32[]{:S(2)}, u32[]{:S(2)}) %all-to-all-start.1) | async-done | bytes 58400 | tf_op jit(solution)/shard_map/all_to_all | solution.py:31
  58.5 0.1 reshape.490
  58.6 0.1 fusion.44
  59.0 0.4 convolution_multiply_fusion.1
  59.5 0.4 convolution_multiply_fusion
  59.9 0.1 copy-done.5
  60.1 0.8 copy-done
  60.9 2.5 %add_reduce_fusion.2 = (f32[4,512]{1,0:T(4,128)S(1)}, f32[4,512]{1,0:T(4,128)S(1)}, f32[4,192,512]{2,1,0:T(8,128)S(1)}, f32[4,192,512]{2,1,0:T(8,128)S(1)}, f32[4,512]{1,0:T(4,128)S(1)}, /*index=5*/f32[4,192,512]{2,1,0:T(8,128)}) fusion(f32[4,192]{1,0:T(4,128)S(1)} %mul.423, f32[4,192]{1,0:T(4,128)S(1)} %mul.384, ...), kind=kOutput, calls=%fused_computation.9 | convolution fusion | flops 110749696 | bytes 10585088 | tf_op jit(solution)/shard_map/cqk,cpk->cqp/dot_general | solution.py:97
  63.8 0.8 reshape.520
  64.5 7.7 %all-to-all-start.3 = ((f32[24,1,768]{2,1,0:T(1,128)}), f32[24,1,768]{2,1,0:T(1,128)S(1)}, u32[]{:S(2)}, u32[]{:S(2)}) async-start(f32[24,1,768]{2,1,0:T(1,128)} %reshape.520), calls=%async_computation.3 | async-start | bytes 147456 | tf_op jit(solution)/shard_map/all_to_all | solution.py:135
  72.2 0.7 fusion.39
  72.9 9.2 %all-to-all-done.3 = f32[24,1,768]{2,1,0:T(1,128)S(1)} async-done(((f32[24,1,768]{2,1,0:T(1,128)}), f32[24,1,768]{2,1,0:T(1,128)S(1)}, u32[]{:S(2)}, u32[]{:S(2)}) %all-to-all-start.3) | async-done | bytes 73760 | tf_op jit(solution)/shard_map/all_to_all | solution.py:135
  82.1 0.5 broadcast.309
  82.6 0.8 reduce.12
  83.8 1.6 %multiply_reduce_fusion.1 = f32[4,512]{1,0:T(4,128)S(1)} fusion(f32[4,192,512]{2,1,0:T(8,128)} %get-tuple-element.18, f32[4,192]{1,0:T(4,128)S(1)} %multiply_add_fusion.3), kind=kLoop, calls=%fused_computation.3 | loop fusion | flops 784384 | bytes 1584128 | tf_op jit(solution)/shard_map/reduce_sum | solution.py:116
  85.5 0.5 add_reduce_fusion.1
  86.3 0.8 reshape.522
  87.0 6.0 %all-to-all-start.4 = ((f32[24,1,768]{2,1,0:T(1,128)}), f32[24,1,768]{2,1,0:T(1,128)S(1)}, u32[]{:S(2)}, u32[]{:S(2)}) async-start(f32[24,1,768]{2,1,0:T(1,128)} %reshape.522), calls=%async_computation.4 | async-start | bytes 147456 | tf_op jit(solution)/shard_map/all_to_all | solution.py:135
  93.0 9.9 %all-to-all-done.4 = f32[24,1,768]{2,1,0:T(1,128)S(1)} async-done(((f32[24,1,768]{2,1,0:T(1,128)}), f32[24,1,768]{2,1,0:T(1,128)S(1)}, u32[]{:S(2)}, u32[]{:S(2)}) %all-to-all-start.4) | async-done | bytes 73760 | tf_op jit(solution)/shard_map/all_to_all | solution.py:135
  102.9 0.8 reduce.13
  104.1 2.1 %add_reduce_fusion = (f32[4,512]{1,0:T(4,128)S(1)}, f32[4,512]{1,0:T(4,128)S(1)}, f32[4,512]{1,0:T(4,128)S(1)}) fusion(f32[4,192,512]{2,1,0:T(8,128)S(1)} %get-tuple-element.14, f32[4,192,512]{2,1,0:T(8,128)S(1)} %get-tuple-element.13, f32[4,192]{1,0:T(4,128)S(1)} %mul.455, f32[4,192]{1,0:T(4,128)S(1)} %mul.452, f32[4,192,512]{2,1,0:T(8,128)} %get-tuple-element.18, ...), kind=kLoop, calls=%fused_computation.2 | loop fusion | flops 3926016 | bytes 4752384 | tf_op jit(solution)/shard_map/reduce_sum | solution.py:114
  106.6 0.7 reshape.524
  107.3 3.7 %all-to-all-start.5 = ((f32[8,1,768]{2,1,0:T(1,128)}), f32[8,1,768]{2,1,0:T(1,128)S(1)}, u32[]{:S(2)}, u32[]{:S(2)}) async-start(f32[8,1,768]{2,1,0:T(1,128)} %reshape.524), calls=%async_computation.5 | async-start | bytes 49152 | tf_op jit(solution)/shard_map/all_to_all | solution.py:120
  110.9 0.7 compare_bitcast_fusion
  111.6 4.0 %all-to-all-done.5 = f32[8,1,768]{2,1,0:T(1,128)S(1)} async-done(((f32[8,1,768]{2,1,0:T(1,128)}), f32[8,1,768]{2,1,0:T(1,128)S(1)}, u32[]{:S(2)}, u32[]{:S(2)}) %all-to-all-start.5) | async-done | bytes 24608 | tf_op jit(solution)/shard_map/all_to_all | solution.py:120
  115.6 0.7 reduce.14
  116.5 0.6 copy.229
  (92 shorter events, 3.6 us)
Async XLA Ops:
  1.5 26.7 %all-to-all-start = ((bf16[32,2,128]{2,1,0:T(2,128)(2,1)}), bf16[32,2,128]{2,1,0:T(2,128)(2,1)S(1)}, u32[]{:S(2)}, u32[]{:S(2)}) async-start(bf16[32,2,128]{2,1,0:T(2,128)(2,1)} %reshape.518), calls=%async_computation | async-start | bytes 32768 | tf_op jit(solution)/shard_map/all_to_all | solution.py:47
  21.1 31.8 %copy-start.3 = (bf16[4,192,64]{2,1,0:T(8,128)(2,1)}, bf16[4,192,64]{2,1,0:T(8,128)(2,1)S(1)}, u32[]{:S(2)}) copy-start(bf16[4,192,64]{2,1,0:T(8,128)(2,1)S(1)} %get-tuple-element.24) | copy-start | bytes 294916
  27.4 25.5 %copy-start.1 = (bf16[4,512,64]{1,2,0:T(8,128)(2,1)}, bf16[4,512,64]{1,2,0:T(8,128)(2,1)S(1)}, u32[]{:S(2)}) copy-start(bf16[4,512,64]{1,2,0:T(8,128)(2,1)S(1)} %get-tuple-element.22) | copy-start | bytes 786436
  29.3 10.5 %all-to-all-start.2 = ((bf16[4,8,2048]{2,0,1:T(4,128)(2,1)}), bf16[4,8,2048]{2,0,1:T(4,128)(2,1)S(1)}, u32[]{:S(2)}, u32[]{:S(2)}) async-start(bf16[4,8,2048]{2,0,1:T(4,128)(2,1)} %broadcast_in_dim.24), calls=%async_computation.2 | async-start | bytes 262144 | tf_op jit(solution)/shard_map/all_to_all | solution.py:31
  40.4 17.7 %all-to-all-start.1 = ((bf16[4,3,2432]{2,0,1:T(4,128)(2,1)}), bf16[4,3,2432]{2,0,1:T(4,128)(2,1)S(1)}, u32[]{:S(2)}, u32[]{:S(2)}) async-start(bf16[4,3,2432]{2,0,1:T(4,128)(2,1)} %broadcast_in_dim.23), calls=%async_computation.1 | async-start | bytes 116736 | tf_op jit(solution)/shard_map/all_to_all | solution.py:31
  59.0 1.0 copy-start.5
  59.0 1.0 copy-start.6
  59.4 1.5 %copy-start = (f32[4,192,512]{2,1,0:T(8,128)S(1)}, f32[4,192,512]{2,1,0:T(8,128)}, u32[]{:S(2)}) copy-start(f32[4,192,512]{2,1,0:T(8,128)} %fusion.7) | copy-start | bytes 4718596
  59.4 1.5 %copy-start.2 = (bf16[4,512,64]{1,2,0:T(8,128)(2,1)S(1)}, bf16[4,512,64]{1,2,0:T(8,128)(2,1)}, u32[]{:S(2)}) copy-start(bf16[4,512,64]{1,2,0:T(8,128)(2,1)} %copy-done.1) | copy-start | bytes 786436
  59.4 1.5 %copy-start.4 = (bf16[4,192,64]{2,1,0:T(8,128)(2,1)S(1)}, bf16[4,192,64]{2,1,0:T(8,128)(2,1)}, u32[]{:S(2)}) copy-start(bf16[4,192,64]{2,1,0:T(8,128)(2,1)} %copy-done.3) | copy-start | bytes 294916
  64.5 17.5 %all-to-all-start.3 = ((f32[24,1,768]{2,1,0:T(1,128)}), f32[24,1,768]{2,1,0:T(1,128)S(1)}, u32[]{:S(2)}, u32[]{:S(2)}) async-start(f32[24,1,768]{2,1,0:T(1,128)} %reshape.520), calls=%async_computation.3 | async-start | bytes 147456 | tf_op jit(solution)/shard_map/all_to_all | solution.py:135
  87.0 15.9 %all-to-all-start.4 = ((f32[24,1,768]{2,1,0:T(1,128)}), f32[24,1,768]{2,1,0:T(1,128)S(1)}, u32[]{:S(2)}, u32[]{:S(2)}) async-start(f32[24,1,768]{2,1,0:T(1,128)} %reshape.522), calls=%async_computation.4 | async-start | bytes 147456 | tf_op jit(solution)/shard_map/all_to_all | solution.py:135
  107.3 8.4 %all-to-all-start.5 = ((f32[8,1,768]{2,1,0:T(1,128)}), f32[8,1,768]{2,1,0:T(1,128)S(1)}, u32[]{:S(2)}, u32[]{:S(2)}) async-start(f32[8,1,768]{2,1,0:T(1,128)} %reshape.524), calls=%async_computation.5 | async-start | bytes 49152 | tf_op jit(solution)/shard_map/all_to_all | solution.py:120

commit v8 on v7

--- a/solution.py
+++ b/solution.py
@@ -54,11 +54,15 @@
     gains_lo = gains_rest - gains_mid
     gains_parts = jnp.stack([gains_hi, gains_mid, gains_lo], axis=1).astype(jnp.bfloat16)
     gains_parts = gains_parts.reshape(per_chan, -1)
-    row_both = gather_groups(jnp.concatenate([own_volt, gains_parts], axis=1), "col")
+    every = gather_groups(jnp.concatenate([own_volt, gains_parts], axis=1), ("row", "col"))
+    row_both = lax.dynamic_slice_in_dim(every, row_index * n_cols, n_cols, 1)
     row_count = n_cols * subant
     col_count = n_rows * subant
     row_left = row_both[:, :, :volt_size].reshape(per_chan, row_count, width)
-    col_left = gather_groups(own_volt, "row").reshape(per_chan, col_count, width)
+    col_both = lax.dynamic_index_in_dim(
+        every.reshape(per_chan, n_rows, n_cols, every.shape[2]), col_index, 2, keepdims=False
+    )
+    col_left = col_both[:, :, :volt_size].reshape(per_chan, col_count, width)
     row_swap = jnp.concatenate([row_left[:, :, samples:], -row_left[:, :, :samples]], axis=2)
     vis_re = (
         jnp.einsum("cqk,cpk->cqp", row_left, col_left, preferred_element_type=jnp.float32) / samples

time: 118 us -> 121 us (1.025)
  waiting for transfers between devices: 33 us -> 40.2 us
  starting transfers between devices: 47 us -> 43.8 us
    all_to_all x1, waiting for transfers between devices: 0.01 us -> 4.5 us  [on_device(): lax.all_to_all(local, 'chan', split_axis=0, concat_axis=1, tiled=True)]
    all_to_all x2, starting transfers between devices: 13.6 us -> 10.5 us  [on_device(): incoming = lax.all_to_all(outgoing, ('row', 'col'), 0, 0, tiled=True)]
    all_to_all x2 -> x1, waiting for transfers between devices: 9.93 us -> 12.4 us  [gather_groups(): return lax.all_to_all(outgoing, axis, 1, 1, tiled=True)]
    all_to_all x2 -> x1, starting transfers between devices: 16.2 us -> 15.9 us  [gather_groups(): return lax.all_to_all(outgoing, axis, 1, 1, tiled=True)]
    unnamed x26 -> x30, local copies, waits for them, and re-layouts: 5.92 us -> 5.87 us
  transfers between devices with their start and end apart: 6 -> 5, of which waited for: 5 -> 5; matrix products, arithmetic and copies ran while one was open for 14% -> 12% of each run, Pallas kernels for 0% -> 0%
where the time goes in v8:
time: 121 us; the launch traced here: 120 us
  starting transfers between devices  43.8 us (36%)
  waiting for transfers between devices  40.2 us (33%)
  other arithmetic  18.1 us (15%)
  local copies, waits for them, and re-layouts  12.5 us (10%)
  matrix products  4.88 us (4%)
    all_to_all x2, waiting for transfers between devices, on_device(): incoming = lax.all_to_all(outgoing, ('row', 'col'), 0, 0, tiled=True)  19.2 us
    all_to_all x1, starting transfers between devices, gather_groups(): return lax.all_to_all(outgoing, axis, 1, 1, tiled=True)  15.9 us
    all_to_all x1, starting transfers between devices, on_device(): lax.all_to_all(local, 'chan', split_axis=0, concat_axis=1, tiled=True)  13.5 us
    all_to_all x1, waiting for transfers between devices, gather_groups(): return lax.all_to_all(outgoing, axis, 1, 1, tiled=True)  12.4 us
    all_to_all x2, starting transfers between devices, on_device(): incoming = lax.all_to_all(outgoing, ('row', 'col'), 0, 0, tiled=True)  10.5 us
    unnamed x30, local copies, waits for them, and re-layouts  5.87 us
    all_to_all x1, waiting for transfers between devices, on_device(): lax.all_to_all(local, 'chan', split_axis=0, concat_axis=1, tiled=True)  4.5 us
    all_to_all x1, starting transfers between devices, on_device(): incoming = lax.all_to_all(partial, 'row', 0, 0, tiled=True)  4.01 us
  transfers between devices with their start and end apart: 5, of which 5 were waited for; matrix products, arithmetic and copies ran while one was open for 12% of the time, Pallas kernels for 0%

profile of v8, /device:TPU:1, one launch (start us, length us, event | category | flops | bytes accessed | tf_op | source)
XLA Modules:
  0.0 120.0 jit_solution(11626006409848797993)
XLA Ops:
  0.0 0.8 copy.198
  0.9 0.7 reshape.520
  1.6 13.5 %all-to-all-start = ((bf16[32,2,128]{2,1,0:T(2,128)(2,1)}), bf16[32,2,128]{2,1,0:T(2,128)(2,1)S(1)}, u32[]{:S(2)}, u32[]{:S(2)}) async-start(bf16[32,2,128]{2,1,0:T(2,128)(2,1)} %reshape.520), calls=%async_computation | async-start | bytes 32768 | tf_op jit(solution)/shard_map/all_to_all | solution.py:47
  15.0 0.7 convert_element_type.55
  15.7 0.5 broadcast.306
  16.2 1.4 %reduce.11 = f32[4,2,64]{2,1,0:T(2,128)S(1)} reduce(f32[4,2,1,64]{3,2,1,0:T(1,128)} %param.8, f32[]{:T(128)} %broadcast.306), dimensions={2}, to_apply=%param.8.reduce_sub_computation.3 | reduce | bytes 4100 | tf_op args[2]
  17.8 0.7 subtract_convert_fusion
  18.5 0.7 constant_dynamic-slice_fusion
  19.5 4.5 %all-to-all-done = bf16[32,2,128]{2,1,0:T(2,128)(2,1)S(1)} async-done(((bf16[32,2,128]{2,1,0:T(2,128)(2,1)}), bf16[32,2,128]{2,1,0:T(2,128)(2,1)S(1)}, u32[]{:S(2)}, u32[]{:S(2)}) %all-to-all-start) | async-done | bytes 16416 | tf_op jit(solution)/shard_map/all_to_all | solution.py:47
  24.2 0.1 reshape.486
  24.3 0.9 broadcast_in_dim.21
  25.2 15.9 %all-to-all-start.1 = ((bf16[4,24,2432]{2,0,1:T(4,128)(2,1)}), bf16[4,24,2432]{2,0,1:T(4,128)(2,1)S(1)}, u32[]{:S(2)}, u32[]{:S(2)}) async-start(bf16[4,24,2432]{2,0,1:T(4,128)(2,1)} %broadcast_in_dim.21), calls=%async_computation.1 | async-start | bytes 933888 | tf_op jit(solution)/shard_map/all_to_all | solution.py:31
  41.6 1.6 %fusion.3 = (bf16[4,192,64]{2,1,0:T(8,128)(2,1)S(1)}, bf16[4,192,64]{2,1,0:T(8,128)(2,1)S(1)}) fusion(f32[192,64]{1,0:T(8,128)S(1)} %multiply_add_fusion.1, f32[4]{0:T(128)S(1)} %add_multiply_fusion.2), kind=kLoop, calls=%fused_computation.24 | loop fusion | flops 196608 | bytes 245776 | tf_op jit(solution)/shard_map/convert_element_type | solution.py:25
  43.2 2.2 %multiply_convert_fusion.1 = (bf16[4,512,64]{1,2,0:T(8,128)(2,1)S(1)}, bf16[4,512,64]{1,2,0:T(8,128)(2,1)S(1)}) fusion(f32[512,64]{0,1:T(8,128)S(1)} %multiply_add_fusion, f32[4]{0:T(128)S(1)} %add_multiply_fusion.2, f32[4,64]{1,0:T(4,128)S(1)} %copy-done.8), kind=kLoop, calls=%fused_computation.23 | loop fusion | flops 1310720 | bytes 656400 | tf_op jit(solution)/shard_map/convert_element_type | solution.py:93
  45.5 0.7 copy-done.1
  46.2 1.6 %fusion.7 = f32[4,192,512]{2,1,0:T(8,128)} fusion(bf16[4,512,64]{1,2,0:T(8,128)(2,1)S(1)} %get-tuple-element.22, bf16[4,512,64]{1,2,0:T(8,128)(2,1)S(1)} %get-tuple-element.21, bf16[4,192,64]{2,1,0:T(8,128)(2,1)S(1)} %get-tuple-element.24, bf16[4,192,64]{2,1,0:T(8,128)(2,1)S(1)} %get-tuple-element.23), kind=kOutput, calls=%fused_computation.29 | convolution fusion | flops 102105088 | bytes 2293760 | tf_op jit(solution)/shard_map/cqk,cpk->cqp/dot_general | solution.py:98
  47.8 2.0 %fusion.43 = bf16[4,192,64]{2,1,0:T(8,128)(2,1)} fusion(f32[192,64]{1,0:T(8,128)S(1)} %multiply_add_fusion.1, f32[4]{0:T(128)S(1)} %add_multiply_fusion.2), kind=kLoop, calls=%fused_computation.111 | loop fusion | flops 245760 | bytes 147472 | tf_op jit(solution)/shard_map/neg | solution.py:96
  49.8 0.9 compare_select_fusion
  50.7 12.4 %all-to-all-done.1 = bf16[4,24,2432]{2,0,1:T(4,128)(2,1)S(1)} async-done(((bf16[4,24,2432]{2,0,1:T(4,128)(2,1)}), bf16[4,24,2432]{2,0,1:T(4,128)(2,1)S(1)}, u32[]{:S(2)}, u32[]{:S(2)}) %all-to-all-start.1) | async-done | bytes 466976 | tf_op jit(solution)/shard_map/all_to_all | solution.py:31
  63.6 0.1 reshape.491
  63.8 0.4 reshape.493
  64.2 0.1 fusion.44
  64.4 0.1 copy.243
  64.6 0.4 convolution_multiply_fusion.1
  65.0 0.4 convolution_multiply_fusion
  65.4 0.1 copy-done.5
  65.6 0.8 copy-done
  66.5 2.5 %add_reduce_fusion.2 = (f32[4,512]{1,0:T(4,128)S(1)}, f32[4,512]{1,0:T(4,128)S(1)}, f32[4,192,512]{2,1,0:T(8,128)S(1)}, f32[4,192,512]{2,1,0:T(8,128)S(1)}, f32[4,512]{1,0:T(4,128)S(1)}, /*index=5*/f32[4,192,512]{2,1,0:T(8,128)}) fusion(f32[4,192]{1,0:T(4,128)S(1)} %mul.424, f32[4,192]{1,0:T(4,128)S(1)} %mul.385, ...), kind=kOutput, calls=%fused_computation.9 | convolution fusion | flops 110749696 | bytes 10585088 | tf_op jit(solution)/shard_map/cqk,cpk->cqp/dot_general | solution.py:101
  69.3 0.8 reshape.522
  70.1 5.2 %all-to-all-start.2 = ((f32[24,1,768]{2,1,0:T(1,128)}), f32[24,1,768]{2,1,0:T(1,128)S(1)}, u32[]{:S(2)}, u32[]{:S(2)}) async-start(f32[24,1,768]{2,1,0:T(1,128)} %reshape.522), calls=%async_computation.2 | async-start | bytes 147456 | tf_op jit(solution)/shard_map/all_to_all | solution.py:139
  75.3 0.7 fusion.39
  76.0 9.2 %all-to-all-done.2 = f32[24,1,768]{2,1,0:T(1,128)S(1)} async-done(((f32[24,1,768]{2,1,0:T(1,128)}), f32[24,1,768]{2,1,0:T(1,128)S(1)}, u32[]{:S(2)}, u32[]{:S(2)}) %all-to-all-start.2) | async-done | bytes 73760 | tf_op jit(solution)/shard_map/all_to_all | solution.py:139
  85.2 0.5 broadcast.309
  85.7 0.8 reduce.12
  86.5 0.1 reshape.523
  87.0 1.6 %multiply_reduce_fusion.1 = f32[4,512]{1,0:T(4,128)S(1)} fusion(f32[4,192,512]{2,1,0:T(8,128)} %get-tuple-element.18, f32[4,192]{1,0:T(4,128)S(1)} %multiply_add_fusion.3), kind=kLoop, calls=%fused_computation.3 | loop fusion | flops 784384 | bytes 1584128 | tf_op jit(solution)/shard_map/reduce_sum | solution.py:120
  88.6 0.5 add_reduce_fusion.1
  89.4 0.8 reshape.524
  90.2 5.3 %all-to-all-start.3 = ((f32[24,1,768]{2,1,0:T(1,128)}), f32[24,1,768]{2,1,0:T(1,128)S(1)}, u32[]{:S(2)}, u32[]{:S(2)}) async-start(f32[24,1,768]{2,1,0:T(1,128)} %reshape.524), calls=%async_computation.3 | async-start | bytes 147456 | tf_op jit(solution)/shard_map/all_to_all | solution.py:139
  95.4 10.0 %all-to-all-done.3 = f32[24,1,768]{2,1,0:T(1,128)S(1)} async-done(((f32[24,1,768]{2,1,0:T(1,128)}), f32[24,1,768]{2,1,0:T(1,128)S(1)}, u32[]{:S(2)}, u32[]{:S(2)}) %all-to-all-start.3) | async-done | bytes 73760 | tf_op jit(solution)/shard_map/all_to_all | solution.py:139
  105.5 0.8 reduce.13
  106.7 2.1 %add_reduce_fusion = (f32[4,512]{1,0:T(4,128)S(1)}, f32[4,512]{1,0:T(4,128)S(1)}, f32[4,512]{1,0:T(4,128)S(1)}) fusion(f32[4,192,512]{2,1,0:T(8,128)S(1)} %get-tuple-element.14, f32[4,192,512]{2,1,0:T(8,128)S(1)} %get-tuple-element.13, f32[4,192]{1,0:T(4,128)S(1)} %mul.456, f32[4,192]{1,0:T(4,128)S(1)} %mul.453, f32[4,192,512]{2,1,0:T(8,128)} %get-tuple-element.18, ...), kind=kLoop, calls=%fused_computation.2 | loop fusion | flops 3926016 | bytes 4752384 | tf_op jit(solution)/shard_map/reduce_sum | solution.py:118
  109.2 0.7 reshape.526
  109.8 4.0 %all-to-all-start.4 = ((f32[8,1,768]{2,1,0:T(1,128)}), f32[8,1,768]{2,1,0:T(1,128)S(1)}, u32[]{:S(2)}, u32[]{:S(2)}) async-start(f32[8,1,768]{2,1,0:T(1,128)} %reshape.526), calls=%async_computation.4 | async-start | bytes 49152 | tf_op jit(solution)/shard_map/all_to_all | solution.py:124
  113.9 0.7 compare_bitcast_fusion
  114.6 4.0 %all-to-all-done.4 = f32[8,1,768]{2,1,0:T(1,128)S(1)} async-done(((f32[8,1,768]{2,1,0:T(1,128)}), f32[8,1,768]{2,1,0:T(1,128)S(1)}, u32[]{:S(2)}, u32[]{:S(2)}) %all-to-all-start.4) | async-done | bytes 24608 | tf_op jit(solution)/shard_map/all_to_all | solution.py:124
  118.6 0.7 reduce.14
  119.4 0.6 copy.231
  (95 shorter events, 3.4 us)
Async XLA Ops:
  0.0 41.1 %copy-start.7 = (f32[2,24,64]{2,1,0:T(8,128)S(1)}, f32[2,24,64]{2,1,0:T(8,128)}, u32[]{:S(2)}) copy-start(f32[2,24,64]{2,1,0:T(8,128)} %param.9) | copy-start | bytes 36868
  0.0 43.2 %copy-start.8 = (f32[4,64]{1,0:T(4,128)S(1)}, f32[4,64]{1,0:T(4,128)}, u32[]{:S(2)}) copy-start(f32[4,64]{1,0:T(4,128)} %param.7) | copy-start | bytes 3076
  1.6 22.5 %all-to-all-start = ((bf16[32,2,128]{2,1,0:T(2,128)(2,1)}), bf16[32,2,128]{2,1,0:T(2,128)(2,1)S(1)}, u32[]{:S(2)}, u32[]{:S(2)}) async-start(bf16[32,2,128]{2,1,0:T(2,128)(2,1)} %reshape.520), calls=%async_computation | async-start | bytes 32768 | tf_op jit(solution)/shard_map/all_to_all | solution.py:47
  25.2 37.9 %all-to-all-start.1 = ((bf16[4,24,2432]{2,0,1:T(4,128)(2,1)}), bf16[4,24,2432]{2,0,1:T(4,128)(2,1)S(1)}, u32[]{:S(2)}, u32[]{:S(2)}) async-start(bf16[4,24,2432]{2,0,1:T(4,128)(2,1)} %broadcast_in_dim.21), calls=%async_computation.1 | async-start | bytes 933888 | tf_op jit(solution)/shard_map/all_to_all | solution.py:31
  43.2 4.5 %copy-start.3 = (bf16[4,192,64]{2,1,0:T(8,128)(2,1)}, bf16[4,192,64]{2,1,0:T(8,128)(2,1)S(1)}, u32[]{:S(2)}) copy-start(bf16[4,192,64]{2,1,0:T(8,128)(2,1)S(1)} %get-tuple-element.24) | copy-start | bytes 294916
  45.5 0.7 copy-start.1
  64.6 1.0 copy-start.5
  64.6 1.0 copy-start.6
  65.0 1.5 %copy-start = (f32[4,192,512]{2,1,0:T(8,128)S(1)}, f32[4,192,512]{2,1,0:T(8,128)}, u32[]{:S(2)}) copy-start(f32[4,192,512]{2,1,0:T(8,128)} %fusion.7) | copy-start | bytes 4718596
  65.0 1.5 %copy-start.2 = (bf16[4,512,64]{1,2,0:T(8,128)(2,1)S(1)}, bf16[4,512,64]{1,2,0:T(8,128)(2,1)}, u32[]{:S(2)}) copy-start(bf16[4,512,64]{1,2,0:T(8,128)(2,1)} %copy-done.1) | copy-start | bytes 786436
  65.0 1.5 %copy-start.4 = (bf16[4,192,64]{2,1,0:T(8,128)(2,1)S(1)}, bf16[4,192,64]{2,1,0:T(8,128)(2,1)}, u32[]{:S(2)}) copy-start(bf16[4,192,64]{2,1,0:T(8,128)(2,1)} %copy-done.3) | copy-start | bytes 294916
  70.1 15.1 %all-to-all-start.2 = ((f32[24,1,768]{2,1,0:T(1,128)}), f32[24,1,768]{2,1,0:T(1,128)S(1)}, u32[]{:S(2)}, u32[]{:S(2)}) async-start(f32[24,1,768]{2,1,0:T(1,128)} %reshape.522), calls=%async_computation.2 | async-start | bytes 147456 | tf_op jit(solution)/shard_map/all_to_all | solution.py:139
  90.2 15.3 %all-to-all-start.3 = ((f32[24,1,768]{2,1,0:T(1,128)}), f32[24,1,768]{2,1,0:T(1,128)S(1)}, u32[]{:S(2)}, u32[]{:S(2)}) async-start(f32[24,1,768]{2,1,0:T(1,128)} %reshape.524), calls=%async_computation.3 | async-start | bytes 147456 | tf_op jit(solution)/shard_map/all_to_all | solution.py:139
  109.8 8.7 %all-to-all-start.4 = ((f32[8,1,768]{2,1,0:T(1,128)}), f32[8,1,768]{2,1,0:T(1,128)S(1)}, u32[]{:S(2)}, u32[]{:S(2)}) async-start(f32[8,1,768]{2,1,0:T(1,128)} %reshape.526), calls=%async_computation.4 | async-start | bytes 49152 | tf_op jit(solution)/shard_map/all_to_all | solution.py:124

commit v9 on v7

--- a/solution.py
+++ b/solution.py
@@ -58,7 +58,8 @@
     row_count = n_cols * subant
     col_count = n_rows * subant
     row_left = row_both[:, :, :volt_size].reshape(per_chan, row_count, width)
-    col_left = gather_groups(own_volt, "row").reshape(per_chan, col_count, width)
+    own_after = lax.optimization_barrier((row_both, own_volt))[1]
+    col_left = gather_groups(own_after, "row").reshape(per_chan, col_count, width)
     row_swap = jnp.concatenate([row_left[:, :, samples:], -row_left[:, :, :samples]], axis=2)
     vis_re = (
         jnp.einsum("cqk,cpk->cqp", row_left, col_left, preferred_element_type=jnp.float32) / samples

time: 118 us -> 118 us (level)
    all_to_all x2, starting transfers between devices: 13.6 us -> 12.2 us  [on_device(): incoming = lax.all_to_all(outgoing, ('row', 'col'), 0, 0, tiled=True)]
    all_to_all x2, starting transfers between devices: 16.2 us -> 17.6 us  [gather_groups(): return lax.all_to_all(outgoing, axis, 1, 1, tiled=True)]
where the time goes in v9:
time: 118 us; the launch traced here: 117 us
  starting transfers between devices  46.9 us (40%)
  waiting for transfers between devices  32.9 us (28%)
  other arithmetic  18.8 us (16%)
  local copies, waits for them, and re-layouts  12.9 us (11%)
  matrix products  4.88 us (4%)
    all_to_all x2, waiting for transfers between devices, on_device(): incoming = lax.all_to_all(outgoing, ('row', 'col'), 0, 0, tiled=True)  19 us
    all_to_all x2, starting transfers between devices, gather_groups(): return lax.all_to_all(outgoing, axis, 1, 1, tiled=True)  17.6 us
    all_to_all x1, starting transfers between devices, on_device(): lax.all_to_all(local, 'chan', split_axis=0, concat_axis=1, tiled=True)  13.5 us
    all_to_all x2, starting transfers between devices, on_device(): incoming = lax.all_to_all(outgoing, ('row', 'col'), 0, 0, tiled=True)  12.2 us
    all_to_all x2, waiting for transfers between devices, gather_groups(): return lax.all_to_all(outgoing, axis, 1, 1, tiled=True)  9.9 us
    unnamed x26, local copies, waits for them, and re-layouts  5.93 us
    all_to_all x1, waiting for transfers between devices, on_device(): incoming = lax.all_to_all(partial, 'row', 0, 0, tiled=True)  4.01 us
    all_to_all x1, starting transfers between devices, on_device(): incoming = lax.all_to_all(partial, 'row', 0, 0, tiled=True)  3.68 us
  transfers between devices with their start and end apart: 6, of which 5 were waited for; matrix products, arithmetic and copies ran while one was open for 14% of the time, Pallas kernels for 0%

profile of v9, /device:TPU:1, one launch (start us, length us, event | category | flops | bytes accessed | tf_op | source)
XLA Modules:
  0.0 117.0 jit_solution(9828248791042757759)
XLA Ops:
  0.0 0.8 copy.196
  0.8 0.7 reshape.517
  1.5 13.5 %all-to-all-start = ((bf16[32,2,128]{2,1,0:T(2,128)(2,1)}), bf16[32,2,128]{2,1,0:T(2,128)(2,1)S(1)}, u32[]{:S(2)}, u32[]{:S(2)}) async-start(bf16[32,2,128]{2,1,0:T(2,128)(2,1)} %reshape.517), calls=%async_computation | async-start | bytes 32768 | tf_op jit(solution)/shard_map/all_to_all | solution.py:47
  15.1 0.7 convert_element_type.55
  15.7 0.8 copy.203
  16.5 0.7 constant_dynamic-slice_fusion
  17.5 2.0 %fusion.43 = bf16[4,192,64]{2,1,0:T(8,128)(2,1)} fusion(f32[192,64]{1,0:T(8,128)S(1)} %multiply_add_fusion.1, f32[4]{0:T(128)S(1)} %add_multiply_fusion.2), kind=kLoop, calls=%fused_computation.108 | loop fusion | flops 245760 | bytes 147472 | tf_op jit(solution)/shard_map/neg | solution.py:93
  19.6 1.6 %fusion.3 = (bf16[4,192,64]{2,1,0:T(8,128)(2,1)S(1)}, bf16[4,192,64]{2,1,0:T(8,128)(2,1)S(1)}) fusion(f32[192,64]{1,0:T(8,128)S(1)} %multiply_add_fusion.1, f32[4]{0:T(128)S(1)} %add_multiply_fusion.2), kind=kLoop, calls=%fused_computation.24 | loop fusion | flops 196608 | bytes 245776 | tf_op jit(solution)/shard_map/convert_element_type | solution.py:25
  21.2 0.7 subtract_convert_fusion
  22.0 0.5 broadcast.307
  22.5 1.4 %reduce.11 = f32[4,2,64]{2,1,0:T(2,128)S(1)} reduce(f32[4,2,1,64]{3,2,1,0:T(1,128)} %param.8, f32[]{:T(128)} %broadcast.307), dimensions={2}, to_apply=%param.8.reduce_sub_computation.3 | reduce | bytes 4100 | tf_op args[2]
  24.4 3.0 %multiply_convert_fusion.1 = (bf16[4,512,64]{1,2,0:T(8,128)(2,1)S(1)}, bf16[4,512,64]{1,2,0:T(8,128)(2,1)S(1)}) fusion(f32[512,64]{0,1:T(8,128)S(1)} %multiply_add_fusion, f32[4]{0:T(128)S(1)} %add_multiply_fusion.2, f32[4,64]{1,0:T(4,128)} %param.7), kind=kLoop, calls=%fused_computation.23 | loop fusion | flops 1310720 | bytes 656400 | tf_op jit(solution)/shard_map/convert_element_type | solution.py:90
  27.4 0.9 compare_select_fusion
  28.5 0.1 reshape.484
  28.6 0.6 broadcast_in_dim.23
  29.2 10.9 %all-to-all-start.1 = ((bf16[4,3,2432]{2,0,1:T(4,128)(2,1)}), bf16[4,3,2432]{2,0,1:T(4,128)(2,1)S(1)}, u32[]{:S(2)}, u32[]{:S(2)}) async-start(bf16[4,3,2432]{2,0,1:T(4,128)(2,1)} %broadcast_in_dim.23), calls=%async_computation.1 | async-start | bytes 116736 | tf_op jit(solution)/shard_map/all_to_all | solution.py:31
  40.2 1.6 %fusion.7 = f32[4,192,512]{2,1,0:T(8,128)} fusion(bf16[4,512,64]{1,2,0:T(8,128)(2,1)S(1)} %get-tuple-element.24, bf16[4,512,64]{1,2,0:T(8,128)(2,1)S(1)} %get-tuple-element.23, bf16[4,192,64]{2,1,0:T(8,128)(2,1)S(1)} %get-tuple-element.26, bf16[4,192,64]{2,1,0:T(8,128)(2,1)S(1)} %get-tuple-element.25), kind=kOutput, calls=%fused_computation.29 | convolution fusion | flops 102105088 | bytes 2293760 | tf_op jit(solution)/shard_map/cqk,cpk->cqp/dot_general | solution.py:95
  41.8 5.2 %all-to-all-done.1 = bf16[4,3,2432]{2,0,1:T(4,128)(2,1)S(1)} async-done(((bf16[4,3,2432]{2,0,1:T(4,128)(2,1)}), bf16[4,3,2432]{2,0,1:T(4,128)(2,1)S(1)}, u32[]{:S(2)}, u32[]{:S(2)}) %all-to-all-start.1) | async-done | bytes 58400 | tf_op jit(solution)/shard_map/all_to_all | solution.py:31
  47.4 0.7 broadcast_in_dim.24
  48.0 6.7 %all-to-all-start.2 = ((bf16[4,8,2048]{2,0,1:T(4,128)(2,1)}), bf16[4,8,2048]{2,0,1:T(4,128)(2,1)S(1)}, u32[]{:S(2)}, u32[]{:S(2)}) async-start(bf16[4,8,2048]{2,0,1:T(4,128)(2,1)} %broadcast_in_dim.24), calls=%async_computation.2 | async-start | bytes 262144 | tf_op jit(solution)/shard_map/all_to_all | solution.py:31
  54.7 0.1 reshape.489
  55.1 0.1 copy.241
  55.2 4.7 %all-to-all-done.2 = bf16[4,8,2048]{2,0,1:T(4,128)(2,1)S(1)} async-done(((bf16[4,8,2048]{2,0,1:T(4,128)(2,1)}), bf16[4,8,2048]{2,0,1:T(4,128)(2,1)S(1)}, u32[]{:S(2)}, u32[]{:S(2)}) %all-to-all-start.2) | async-done | bytes 131104 | tf_op jit(solution)/shard_map/all_to_all | solution.py:31
  60.0 0.4 reshape.490
  60.4 0.4 convolution_multiply_fusion.1
  60.8 0.4 convolution_multiply_fusion
  61.2 0.1 copy-done.5
  61.4 0.8 copy-done
  62.3 2.5 %add_reduce_fusion.2 = (f32[4,512]{1,0:T(4,128)S(1)}, f32[4,512]{1,0:T(4,128)S(1)}, f32[4,192,512]{2,1,0:T(8,128)S(1)}, f32[4,192,512]{2,1,0:T(8,128)S(1)}, f32[4,512]{1,0:T(4,128)S(1)}, /*index=5*/f32[4,192,512]{2,1,0:T(8,128)}) fusion(f32[4,192]{1,0:T(4,128)S(1)} %mul.423, f32[4,192]{1,0:T(4,128)S(1)} %mul.384, ...), kind=kOutput, calls=%fused_computation.9 | convolution fusion | flops 110749696 | bytes 10585088 | tf_op jit(solution)/shard_map/cqk,cpk->cqp/dot_general | solution.py:98
  65.2 0.8 reshape.519
  65.9 6.2 %all-to-all-start.3 = ((f32[24,1,768]{2,1,0:T(1,128)}), f32[24,1,768]{2,1,0:T(1,128)S(1)}, u32[]{:S(2)}, u32[]{:S(2)}) async-start(f32[24,1,768]{2,1,0:T(1,128)} %reshape.519), calls=%async_computation.3 | async-start | bytes 147456 | tf_op jit(solution)/shard_map/all_to_all | solution.py:136
  72.1 0.7 fusion.39
  72.9 9.2 %all-to-all-done.3 = f32[24,1,768]{2,1,0:T(1,128)S(1)} async-done(((f32[24,1,768]{2,1,0:T(1,128)}), f32[24,1,768]{2,1,0:T(1,128)S(1)}, u32[]{:S(2)}, u32[]{:S(2)}) %all-to-all-start.3) | async-done | bytes 73760 | tf_op jit(solution)/shard_map/all_to_all | solution.py:136
  82.0 0.5 broadcast.310
  82.5 0.8 reduce.12
  83.8 1.6 %multiply_reduce_fusion.1 = f32[4,512]{1,0:T(4,128)S(1)} fusion(f32[4,192,512]{2,1,0:T(8,128)} %get-tuple-element.20, f32[4,192]{1,0:T(4,128)S(1)} %multiply_add_fusion.3), kind=kLoop, calls=%fused_computation.3 | loop fusion | flops 784384 | bytes 1584128 | tf_op jit(solution)/shard_map/reduce_sum | solution.py:117
  85.5 0.5 add_reduce_fusion.1
  86.2 0.8 reshape.521
  87.0 6.0 %all-to-all-start.4 = ((f32[24,1,768]{2,1,0:T(1,128)}), f32[24,1,768]{2,1,0:T(1,128)S(1)}, u32[]{:S(2)}, u32[]{:S(2)}) async-start(f32[24,1,768]{2,1,0:T(1,128)} %reshape.521), calls=%async_computation.4 | async-start | bytes 147456 | tf_op jit(solution)/shard_map/all_to_all | solution.py:136
  93.0 9.9 %all-to-all-done.4 = f32[24,1,768]{2,1,0:T(1,128)S(1)} async-done(((f32[24,1,768]{2,1,0:T(1,128)}), f32[24,1,768]{2,1,0:T(1,128)S(1)}, u32[]{:S(2)}, u32[]{:S(2)}) %all-to-all-start.4) | async-done | bytes 73760 | tf_op jit(solution)/shard_map/all_to_all | solution.py:136
  102.8 0.8 reduce.13
  104.1 2.1 %add_reduce_fusion = (f32[4,512]{1,0:T(4,128)S(1)}, f32[4,512]{1,0:T(4,128)S(1)}, f32[4,512]{1,0:T(4,128)S(1)}) fusion(f32[4,192,512]{2,1,0:T(8,128)S(1)} %get-tuple-element.16, f32[4,192,512]{2,1,0:T(8,128)S(1)} %get-tuple-element.15, f32[4,192]{1,0:T(4,128)S(1)} %mul.455, f32[4,192]{1,0:T(4,128)S(1)} %mul.452, f32[4,192,512]{2,1,0:T(8,128)} %get-tuple-element.20, ...), kind=kLoop, calls=%fused_computation.2 | loop fusion | flops 3926016 | bytes 4752384 | tf_op jit(solution)/shard_map/reduce_sum | solution.py:115
  106.5 0.7 reshape.523
  107.2 3.7 %all-to-all-start.5 = ((f32[8,1,768]{2,1,0:T(1,128)}), f32[8,1,768]{2,1,0:T(1,128)S(1)}, u32[]{:S(2)}, u32[]{:S(2)}) async-start(f32[8,1,768]{2,1,0:T(1,128)} %reshape.523), calls=%async_computation.5 | async-start | bytes 49152 | tf_op jit(solution)/shard_map/all_to_all | solution.py:121
  110.9 0.7 compare_bitcast_fusion
  111.6 4.0 %all-to-all-done.5 = f32[8,1,768]{2,1,0:T(1,128)S(1)} async-done(((f32[8,1,768]{2,1,0:T(1,128)}), f32[8,1,768]{2,1,0:T(1,128)S(1)}, u32[]{:S(2)}, u32[]{:S(2)}) %all-to-all-start.5) | async-done | bytes 24608 | tf_op jit(solution)/shard_map/all_to_all | solution.py:121
  115.6 0.7 reduce.14
  116.4 0.6 copy.229
  (92 shorter events, 3.6 us)
Async XLA Ops:
  1.5 26.7 %all-to-all-start = ((bf16[32,2,128]{2,1,0:T(2,128)(2,1)}), bf16[32,2,128]{2,1,0:T(2,128)(2,1)S(1)}, u32[]{:S(2)}, u32[]{:S(2)}) async-start(bf16[32,2,128]{2,1,0:T(2,128)(2,1)} %reshape.517), calls=%async_computation | async-start | bytes 32768 | tf_op jit(solution)/shard_map/all_to_all | solution.py:47
  21.1 20.6 %copy-start.3 = (bf16[4,192,64]{2,1,0:T(8,128)(2,1)}, bf16[4,192,64]{2,1,0:T(8,128)(2,1)S(1)}, u32[]{:S(2)}) copy-start(bf16[4,192,64]{2,1,0:T(8,128)(2,1)S(1)} %get-tuple-element.26) | copy-start | bytes 294916
  27.4 14.4 %copy-start.1 = (bf16[4,512,64]{1,2,0:T(8,128)(2,1)}, bf16[4,512,64]{1,2,0:T(8,128)(2,1)S(1)}, u32[]{:S(2)}) copy-start(bf16[4,512,64]{1,2,0:T(8,128)(2,1)S(1)} %get-tuple-element.24) | copy-start | bytes 786436
  29.2 17.7 %all-to-all-start.1 = ((bf16[4,3,2432]{2,0,1:T(4,128)(2,1)}), bf16[4,3,2432]{2,0,1:T(4,128)(2,1)S(1)}, u32[]{:S(2)}, u32[]{:S(2)}) async-start(bf16[4,3,2432]{2,0,1:T(4,128)(2,1)} %broadcast_in_dim.23), calls=%async_computation.1 | async-start | bytes 116736 | tf_op jit(solution)/shard_map/all_to_all | solution.py:31
  48.0 11.9 %all-to-all-start.2 = ((bf16[4,8,2048]{2,0,1:T(4,128)(2,1)}), bf16[4,8,2048]{2,0,1:T(4,128)(2,1)S(1)}, u32[]{:S(2)}, u32[]{:S(2)}) async-start(bf16[4,8,2048]{2,0,1:T(4,128)(2,1)} %broadcast_in_dim.24), calls=%async_computation.2 | async-start | bytes 262144 | tf_op jit(solution)/shard_map/all_to_all | solution.py:31
  60.4 1.0 copy-start.5
  60.4 1.0 copy-start.6
  60.8 1.5 %copy-start = (f32[4,192,512]{2,1,0:T(8,128)S(1)}, f32[4,192,512]{2,1,0:T(8,128)}, u32[]{:S(2)}) copy-start(f32[4,192,512]{2,1,0:T(8,128)} %fusion.7) | copy-start | bytes 4718596
  60.8 1.5 %copy-start.2 = (bf16[4,512,64]{1,2,0:T(8,128)(2,1)S(1)}, bf16[4,512,64]{1,2,0:T(8,128)(2,1)}, u32[]{:S(2)}) copy-start(bf16[4,512,64]{1,2,0:T(8,128)(2,1)} %copy-done.1) | copy-start | bytes 786436
  60.8 1.5 %copy-start.4 = (bf16[4,192,64]{2,1,0:T(8,128)(2,1)S(1)}, bf16[4,192,64]{2,1,0:T(8,128)(2,1)}, u32[]{:S(2)}) copy-start(bf16[4,192,64]{2,1,0:T(8,128)(2,1)} %copy-done.3) | copy-start | bytes 294916
  65.9 16.1 %all-to-all-start.3 = ((f32[24,1,768]{2,1,0:T(1,128)}), f32[24,1,768]{2,1,0:T(1,128)S(1)}, u32[]{:S(2)}, u32[]{:S(2)}) async-start(f32[24,1,768]{2,1,0:T(1,128)} %reshape.519), calls=%async_computation.3 | async-start | bytes 147456 | tf_op jit(solution)/shard_map/all_to_all | solution.py:136
  87.0 15.9 %all-to-all-start.4 = ((f32[24,1,768]{2,1,0:T(1,128)}), f32[24,1,768]{2,1,0:T(1,128)S(1)}, u32[]{:S(2)}, u32[]{:S(2)}) async-start(f32[24,1,768]{2,1,0:T(1,128)} %reshape.521), calls=%async_computation.4 | async-start | bytes 147456 | tf_op jit(solution)/shard_map/all_to_all | solution.py:136
  107.2 8.4 %all-to-all-start.5 = ((f32[8,1,768]{2,1,0:T(1,128)}), f32[8,1,768]{2,1,0:T(1,128)S(1)}, u32[]{:S(2)}, u32[]{:S(2)}) async-start(f32[8,1,768]{2,1,0:T(1,128)} %reshape.523), calls=%async_computation.5 | async-start | bytes 49152 | tf_op jit(solution)/shard_map/all_to_all | solution.py:121
